TPU v7x, 256 devices: a whole 4x4x8 slice. The times are simulated.
256 devices in a mesh: row: 8 (over y, core), col: 16 (over x_lo, z), req: 2 (over x_hi).
Axes of the slice: x: 4 (x_hi: 2, x_lo: 2; x = x_hi * 2 + x_lo), y: 4, z: 8, core: 2. Of those that a mesh axis runs over, the one named last changes fastest.
Arguments:
- tokens: bfloat16 [3072, 4096], P(('req', 'row'), 'col'), may hold values from -6 to 6
- up_weight: bfloat16 [4096, 21504], P('col', 'row'), may hold values from -0.09375 to 0.09375
- down_weight: bfloat16 [21504, 4096], P('row', 'col'), may hold values from -0.0390625 to 0.0390625
- pool_states: float32 [192, 2, 128, 64, 128], P('row', 'req', 'col'), may hold values from -6 to 6
- pool_edges: float32 [192, 2, 128, 64, 3], P('row', 'req', 'col'), may hold values from -6 to 6
- finish_ids: int32 [32], replicated, may hold values from 0 to 191, as said below
- slot_perm: int32 [32], replicated, may hold values from 0 to 31, each once
Outputs:
- layer_out: bfloat16 [3072, 4096], P(('req', 'row'), 'col')
- decode_states: float32 [32, 2, 128, 64, 128], P('req', None, 'col', 'row')
- decode_edges: float32 [32, 2, 128, 64, 3], P('req', None, 'col', 'row')
Inputs may be any that keep to these rules, and one draw needn't show every extreme that they name: `finish_ids`: entries are distinct; of the 24 slots r * 24 to (r + 1) * 24 - 1 of one index r of row, at most 8 are named, and exactly 8 for some index. `slot_perm`: every decode slot is named once.
All inputs are finite; a program needn't handle non-finite values.
Results may differ from a plain program's by a relative error of at most 0.0044.
Values may be sent and summed in bfloat16 or wider, within the bound.
No kernel may reach another device: no remote copies, remote signals or barrier semaphores. Data moves between devices by JAX's collectives and lax.ppermute only.
A program may use at most 128 MiB of HBM per device.

v0:
```python
import jax
import jax.numpy as jnp
from jax import lax
from jax.sharding import PartitionSpec as P


def handover(pool_states, pool_edges, finish_ids, slot_perm):
    finished = slot_perm.shape[0]
    numbers = jnp.arange(finished, dtype=jnp.int32)
    matches = slot_perm[None, :] == numbers[:, None]
    inverse = jnp.sum(jnp.where(matches, numbers[None, :], 0), axis=1)
    arrived = (
        lax.all_to_all(pool_states, "row", split_axis=3, concat_axis=0, tiled=True),
        lax.all_to_all(pool_edges, "row", split_axis=3, concat_axis=0, tiled=True),
    )
    wanted_rows = finish_ids[inverse]
    states = arrived[0][wanted_rows]
    edge_rows = arrived[1][wanted_rows]
    return (
        lax.all_to_all(states, "req", split_axis=0, concat_axis=1, tiled=True),
        lax.all_to_all(edge_rows, "req", split_axis=0, concat_axis=1, tiled=True),
    )


def on_device(tokens, up_weight, down_weight, pool_states, pool_edges, finish_ids, slot_perm):
    gathered = lax.all_gather(tokens, "row", axis=0, tiled=True)
    preact = lax.psum_scatter(
        jnp.dot(gathered, up_weight, preferred_element_type=jnp.float32),
        "col",
        scatter_dimension=0,
        tiled=True,
    )
    active = jnp.maximum(preact, 0.0)
    hidden = (active * active).astype(jnp.bfloat16)
    products = jnp.dot(
        lax.all_gather(hidden, "col", axis=0, tiled=True),
        down_weight,
        preferred_element_type=jnp.float32,
    )
    summed = lax.psum_scatter(products, "row", scatter_dimension=0, tiled=True)
    layer_out = (tokens.astype(jnp.float32) + summed).astype(jnp.bfloat16)
    decode_states, decode_edges = handover(pool_states, pool_edges, finish_ids, slot_perm)
    return (layer_out, decode_states, decode_edges)


def solution(mesh):
    in_specs = (
        P(("req", "row"), "col"),
        P("col", "row"),
        P("row", "col"),
        P("row", "req", "col", None, None),
        P("row", "req", "col", None, None),
        P(),
        P(),
    )
    out_specs = (
        P(("req", "row"), "col"),
        P("req", None, "col", "row", None),
        P("req", None, "col", "row", None),
    )
    return jax.shard_map(
        on_device, mesh=mesh, in_specs=in_specs, out_specs=out_specs, check_vma=False
    )
```

profile of v0, /device:TPU:8, one launch (start us, length us, event | category | flops | bytes accessed | tf_op | source)
XLA Modules:
  0.0 376.9 jit_solution(2078895432324157047)
XLA Ops:
  7.2 0.0 copy-start
  7.2 0.0 reduce-scatter.3.cloned.1.call-start
  7.2 14.0 %all_gather.6 = bf16[1536,256]{1,0:T(8,128)(2,1)S(1)} all-gather(bf16[192,256]{1,0:T(8,128)(2,1)} %param.7), channel_id=1, replica_groups=mesh['row'=8,'col'=16,'req'=2] {'row'}, dimensions={0}, use_global_device_ids=true | all-gather | bytes 884736 | tf_op jit(solution)/shard_map/all_gather | solution.py:26
  21.2 0.0 copy-done
  21.2 8.1 %fusion.2 = f32[1536,2688]{1,0:T(8,128)} fusion(bf16[1536,256]{1,0:T(8,128)(2,1)S(1)} %all_gather.6, bf16[256,2688]{1,0:T(8,128)(2,1)S(1)} %copy-done), kind=kOutput, calls=%fused_computation.16 | convolution fusion | flops 2113929216 | bytes 18677760 | tf_op jit(solution)/shard_map/dot_general | solution.py:28
  29.3 0.0 reduce-scatter.3.cloned.1.call-update
  29.3 0.0 all-gather.2.cloned.1.call-start
  29.3 185.7 %reduce-scatter.3.cloned.1.call-done = f32[96,2688]{1,0:T(8,128)} async-done(((f32[1536,2688]{1,0:T(8,128)}), f32[96,2688]{1,0:T(8,128)}) %reduce-scatter.3.cloned.1.call-update) | async-done | bytes 1032208 | tf_op jit(solution)/shard_map/reduce_scatter | solution.py:27
  215.0 2.1 multiply_convert_fusion
  217.1 0.0 all-gather.2.cloned.1.call-update
  217.1 0.0 copy-done.4
  217.1 0.3 copy.50
  217.4 1.2 reshape.63
  218.7 4.8 %all-to-all-start.2 = ((f32[8,1,4608]{2,1,0:T(1,128)}), f32[8,1,4608]{2,1,0:T(1,128)S(1)}, u32[]{:S(2)}, u32[]{:S(2)}) async-start(f32[8,1,4608]{2,1,0:T(1,128)} %reshape.63), calls=%async_computation.4 | async-start | bytes 294912 | tf_op jit(solution)/shard_map/all_to_all | solution.py:14
  223.5 9.0 %copy.46 = f32[24,1,8,64,128]{4,2,0,1,3:T(8,128)} copy(f32[24,1,8,64,128]{4,3,2,1,0:T(8,128)} %param.10) | data formatting | bytes 12582912 | tf_op args[3]
  232.5 0.0 all-to-all-done.2
  232.5 4.9 %all-to-all-start = ((f32[24,1,8,64,128]{4,2,0,1,3:T(8,128)}), f32[24,1,8,64,128]{4,2,0,1,3:T(8,128)}, u32[]{:S(2)}, u32[]{:S(2)}) async-start(f32[24,1,8,64,128]{4,2,0,1,3:T(8,128)} %copy.46), calls=%async_computation.2 | async-start | bytes 12582912 | tf_op jit(solution)/shard_map/all_to_all | solution.py:13
  237.5 0.2 reduce-scatter.5.cloned.1.call-start
  237.7 77.0 %all-gather.2.cloned.1.call-done = bf16[1536,2688]{1,0:T(8,128)(2,1)} async-done(((bf16[96,2688]{1,0:T(8,128)(2,1)}), bf16[1536,2688]{1,0:T(8,128)(2,1)}) %all-gather.2.cloned.1.call-update) | async-done | bytes 8257552 | tf_op jit(solution)/shard_map/all_gather | solution.py:36
  314.7 0.0 copy-done.5
  314.7 6.9 %fusion.3 = f32[1536,256]{1,0:T(8,128)} fusion(bf16[1536,2688]{1,0:T(8,128)(2,1)} %all-gather.2.cloned.1.call-done, bf16[2688,256]{1,0:T(8,128)(2,1)S(1)} %copy-done.5), kind=kOutput, calls=%fused_computation.17 | convolution fusion | flops 2113929216 | bytes 11206656 | tf_op jit(solution)/shard_map/dot_general | solution.py:35
  321.7 0.0 reduce-scatter.5.cloned.1.call-update
  321.7 0.0 copy-done.6
  321.7 0.1 select_reduce_fusion
  321.8 0.0 copy-done.2
  321.9 0.7 gather_fusion
  322.6 0.5 broadcast.50
  323.1 1.0 reduce
  324.1 0.5 reshape.64
  324.6 0.2 copy.64
  324.8 2.1 copy.58
  326.9 2.2 gather_fusion.2
  329.2 0.8 reshape.65
  330.0 0.0 all-to-all-done
  330.0 4.0 %all-to-all-start.3 = ((f32[2,1,3072]{2,1,0:T(1,128)}), f32[2,1,3072]{2,1,0:T(1,128)S(1)}, u32[]{:S(2)}, u32[]{:S(2)}) async-start(f32[2,1,3072]{2,1,0:T(1,128)} %reshape.65), calls=%async_computation.5 | async-start | bytes 49152 | tf_op jit(solution)/shard_map/all_to_all | solution.py:21
  334.0 6.5 %copy.63 = f32[24,1,8,64,128]{4,3,2,0,1:T(8,128)S(1)} copy(f32[24,1,8,64,128]{4,2,0,1,3:T(8,128)} %all-to-all-done) | data formatting | bytes 12582912 | tf_op jit(solution)/shard_map/all_to_all | solution.py:13
  340.4 0.0 copy-start.1
  340.5 3.6 copy.48
  344.0 4.5 %gather_fusion.1 = f32[32,8,8,128]{3,2,1,0:T(8,128)} fusion(f32[192,8,8,128]{3,2,1,0:T(8,128)} %bitcast.46, s32[1024]{0:T(1024)S(1)} %pad_clamp_fusion), kind=kCustom, calls=%fused_computation.1 | custom fusion | bytes 2097280 | tf_op jit(solution)/shard_map/gather | solution.py:17
  348.5 0.0 all-to-all-done.3
  348.5 4.8 %all-to-all-start.1 = ((f32[32,1,8,8,128]{4,3,2,1,0:T(8,128)}), f32[32,1,8,8,128]{4,3,2,1,0:T(8,128)S(1)}, u32[]{:S(2)}, u32[]{:S(2)}) async-start(f32[32,1,8,8,128]{4,3,2,1,0:T(8,128)} %bitcast.8), calls=%async_computation.3 | async-start | bytes 2097152 | tf_op jit(solution)/shard_map/all_to_all | solution.py:20
  353.3 0.7 reduce.1
  354.0 0.2 reshape.66
  354.3 0.2 copy.59
  354.5 0.7 copy.57
  355.2 12.5 %all-to-all-done.1 = f32[32,1,8,8,128]{4,3,2,1,0:T(8,128)S(1)} async-done(((f32[32,1,8,8,128]{4,3,2,1,0:T(8,128)}), f32[32,1,8,8,128]{4,3,2,1,0:T(8,128)S(1)}, u32[]{:S(2)}, u32[]{:S(2)}) %all-to-all-start.1) | async-done | bytes 1048608 | tf_op jit(solution)/shard_map/all_to_all | solution.py:20
  367.7 1.0 copy.56
  368.8 1.6 add_convert_fusion
  (13 shorter events, 0.1 us)
Async XLA Ops:
  7.2 14.0 %copy-start = (bf16[256,2688]{1,0:T(8,128)(2,1)S(1)}, bf16[256,2688]{1,0:T(8,128)(2,1)}, u32[]{:S(2)}) copy-start(bf16[256,2688]{1,0:T(8,128)(2,1)} %param.8) | copy-start | bytes 4128772
  7.2 207.8 %reduce-scatter.3.cloned.1.call-start = ((), (), s32[]{:S(2)}) async-start(), calls=%async_computation.6 | async-start | bytes 17547264 | tf_op jit(solution)/shard_map/reduce_scatter | solution.py:27
  29.3 187.8 %copy-start.4 = (f32[24,1,8,64,3]{3,2,4,1,0:T(8,128)S(1)}, f32[24,1,8,64,3]{3,2,4,1,0:T(8,128)}, u32[]{:S(2)}) copy-start(f32[24,1,8,64,3]{3,2,4,1,0:T(8,128)} %param.11) | copy-start | bytes 442372
  29.3 285.4 %all-gather.2.cloned.1.call-start = ((), (), s32[]{:S(2)}) async-start(), calls=%async_computation.7 | async-start | bytes 8773632 | tf_op jit(solution)/shard_map/all_gather | solution.py:36
  218.7 13.8 %all-to-all-start.2 = ((f32[8,1,4608]{2,1,0:T(1,128)}), f32[8,1,4608]{2,1,0:T(1,128)S(1)}, u32[]{:S(2)}, u32[]{:S(2)}) async-start(f32[8,1,4608]{2,1,0:T(1,128)} %reshape.63), calls=%async_computation.4 | async-start | bytes 294912 | tf_op jit(solution)/shard_map/all_to_all | solution.py:14
  232.5 82.2 %copy-start.5 = (bf16[2688,256]{1,0:T(8,128)(2,1)S(1)}, bf16[2688,256]{1,0:T(8,128)(2,1)}, u32[]{:S(2)}) copy-start(bf16[2688,256]{1,0:T(8,128)(2,1)} %param.9) | copy-start | bytes 4128772
  232.5 97.5 %all-to-all-start = ((f32[24,1,8,64,128]{4,2,0,1,3:T(8,128)}), f32[24,1,8,64,128]{4,2,0,1,3:T(8,128)}, u32[]{:S(2)}, u32[]{:S(2)}) async-start(f32[24,1,8,64,128]{4,2,0,1,3:T(8,128)} %copy.46), calls=%async_computation.2 | async-start | bytes 12582912 | tf_op jit(solution)/shard_map/all_to_all | solution.py:13
  237.5 84.2 %copy-start.6 = (s32[32]{0:T(128)S(1)}, s32[32]{0:T(128)}, u32[]{:S(2)}) copy-start(s32[32]{0:T(128)} %param.13) | copy-start | bytes 388
  237.5 84.4 %copy-start.2 = (s32[32]{0:T(128)S(1)}, s32[32]{0:T(128)}, u32[]{:S(2)}) copy-start(s32[32]{0:T(128)} %param.12) | copy-start | bytes 388
  237.5 131.3 %reduce-scatter.5.cloned.1.call-start = ((), (), s32[]{:S(2)}) async-start(), calls=%async_computation.8 | async-start | bytes 1769472 | tf_op jit(solution)/shard_map/reduce_scatter | solution.py:40
  330.0 18.5 %all-to-all-start.3 = ((f32[2,1,3072]{2,1,0:T(1,128)}), f32[2,1,3072]{2,1,0:T(1,128)S(1)}, u32[]{:S(2)}, u32[]{:S(2)}) async-start(f32[2,1,3072]{2,1,0:T(1,128)} %reshape.65), calls=%async_computation.5 | async-start | bytes 49152 | tf_op jit(solution)/shard_map/all_to_all | solution.py:21
  340.4 29.9 %copy-start.1 = (bf16[256,2688]{1,0:T(8,128)(2,1)S(1)}, bf16[256,2688]{1,0:T(8,128)(2,1)}, u32[]{:S(2)}) copy-start(bf16[256,2688]{1,0:T(8,128)(2,1)} %param.8) | copy-start | bytes 4128772
  344.0 24.7 %copy-start.3 = (bf16[192,256]{1,0:T(8,128)(2,1)S(1)}, bf16[192,256]{1,0:T(8,128)(2,1)}, u32[]{:S(2)}) copy-start(bf16[192,256]{1,0:T(8,128)(2,1)} %param.7) | copy-start | bytes 294916
  348.5 19.2 %all-to-all-start.1 = ((f32[32,1,8,8,128]{4,3,2,1,0:T(8,128)}), f32[32,1,8,8,128]{4,3,2,1,0:T(8,128)S(1)}, u32[]{:S(2)}, u32[]{:S(2)}) async-start(f32[32,1,8,8,128]{4,3,2,1,0:T(8,128)} %bitcast.8), calls=%async_computation.3 | async-start | bytes 2097152 | tf_op jit(solution)/shard_map/all_to_all | solution.py:20
Sparse Core Ops, SparseCore 0:
  29.4 185.5 reduce-scatter.2
  217.4 97.3 all-gather.1
  321.8 30.1 reduce-scatter.4
where the time goes:
time: 378 us; the launch traced here: 377 us
  waiting for transfers between devices  275 us (73%)
  local copies, waits for them, and re-layouts  34.4 us (9%)
  starting transfers between devices  18.8 us (5%)
  matrix products  15 us (4%)
  blocking collectives  14 us (4%)
  between operations  13.9 us (4%)
  other arithmetic  5.52 us (1%)
    reduce_scatter x1, waiting for transfers between devices, on_device(): lax.psum_scatter(jnp.dot(gathered, up_weight, preferred_element_type=jnp....  186 us
    all_gather x1, waiting for transfers between devices, on_device(): lax.all_gather(hidden, 'col', axis=0, tiled=True)  77 us
    unnamed x23, local copies, waits for them, and re-layouts  14 us
    all_gather x1, blocking collectives, on_device(): gathered = lax.all_gather(tokens, 'row', axis=0, tiled=True)  14 us
    all_to_all x1, waiting for transfers between devices, handover(): lax.all_to_all(states, 'req', split_axis=0, concat_axis=1, tiled=True)  12.5 us
    all_to_all x2, local copies, waits for them, and re-layouts, handover(): lax.all_to_all(pool_states, 'row', split_axis=3, concat_axis=0, tiled=True)  10 us
    dot_general x1, matrix products, on_device(): jnp.dot(gathered, up_weight, preferred_element_type=jnp.float32)  8.06 us
  transfers between devices with their start and end apart: 7, of which 3 were waited for; matrix products, arithmetic and copies ran while one was open for 11% of the time, Pallas kernels for 0%

commit v1 on v0

v1 whole, which is shorter than its diff:
```python
import jax
import jax.numpy as jnp
import numpy as np
from jax import lax
from jax.sharding import Mesh
from jax.sharding import PartitionSpec as P

MOST = 8
SWAP = [(0, 1), (1, 0)]


def handover(pool_states, pool_edges, finish_ids, slot_perm):
    local = pool_states.shape[0]
    finished = slot_perm.shape[0]
    r = lax.axis_index("row")
    numbers = jnp.arange(finished, dtype=jnp.int32)
    matches = slot_perm[None, :] == numbers[:, None]
    inverse = jnp.sum(jnp.where(matches, numbers[None, :], 0), axis=1)
    row_of = finish_ids // local
    same = row_of[:, None] == row_of[None, :]
    earlier = numbers[None, :] < numbers[:, None]
    rank = jnp.sum(jnp.where(same & earlier, 1, 0), axis=1)
    slots = jnp.arange(MOST, dtype=jnp.int32)
    chosen = (row_of[None, :] == r) & (rank[None, :] == slots[:, None])
    local_slot = jnp.sum(jnp.where(chosen, finish_ids[None, :] - r * local, 0), axis=1)
    picked = jnp.concatenate([pool_states[local_slot], pool_edges[local_slot]], axis=-1)
    arrived = lax.all_to_all(picked, "row", split_axis=3, concat_axis=0, tiled=True)
    source = inverse
    wanted = row_of[source] * MOST + rank[source]
    rows = arrived[wanted]
    both = lax.all_to_all(rows, "req", split_axis=0, concat_axis=1, tiled=True)
    n = pool_states.shape[-1]
    return both[..., :n], both[..., n:]


def ffn(tokens, up_weight, down_weight):
    i = lax.axis_index("cx")
    block, width = tokens.shape
    half = block // 2
    halves = tokens.reshape(2, half, width)
    mine = lax.dynamic_index_in_dim(halves, i, 0, keepdims=False)
    theirs = lax.dynamic_index_in_dim(halves, 1 - i, 0, keepdims=False)
    recv = lax.ppermute(theirs, "cx", SWAP)
    xa = jnp.concatenate([mine, recv], axis=1)
    xg = lax.all_gather(xa, "row", axis=0, tiled=True)
    w1 = jnp.concatenate([up_weight, lax.ppermute(up_weight, "cx", SWAP)], axis=0)
    preact = lax.psum_scatter(
        jnp.dot(xg, w1, preferred_element_type=jnp.float32),
        "cz",
        scatter_dimension=0,
        tiled=True,
    )
    active = jnp.maximum(preact, 0.0)
    hidden = (active * active).astype(jnp.bfloat16)
    hg = lax.all_gather(hidden, "cz", axis=0, tiled=True)
    w2 = jnp.concatenate([down_weight, lax.ppermute(down_weight, "cx", SWAP)], axis=1)
    products = jnp.dot(hg, w2, preferred_element_type=jnp.float32)
    summed = lax.psum_scatter(products, "row", scatter_dimension=0, tiled=True)
    own = summed[:, :width]
    other = lax.ppermute(summed[:, width:], "cx", SWAP)
    full = jnp.where(i == 0, jnp.concatenate([own, other], 0), jnp.concatenate([other, own], 0))
    return (tokens.astype(jnp.float32) + full).astype(jnp.bfloat16)


def on_device(tokens, up_weight, down_weight, pool_states, pool_edges, finish_ids, slot_perm):
    layer_out = ffn(tokens, up_weight, down_weight)
    decode_states, decode_edges = handover(pool_states, pool_edges, finish_ids, slot_perm)
    return (layer_out, decode_states, decode_edges)


def solution(mesh):
    devices = np.asarray(mesh.devices)
    rows, cols, reqs = devices.shape
    split = Mesh(devices.reshape(rows, 2, cols // 2, reqs), ("row", "cx", "cz", "req"))
    col = ("cx", "cz")
    in_specs = (
        P(("req", "row"), col),
        P(col, "row"),
        P("row", col),
        P("row", "req", col, None, None),
        P("row", "req", col, None, None),
        P(),
        P(),
    )
    out_specs = (
        P(("req", "row"), col),
        P("req", None, col, "row", None),
        P("req", None, col, "row", None),
    )
    return jax.shard_map(
        on_device, mesh=split, in_specs=in_specs, out_specs=out_specs, check_vma=False
    )
```

time: 378 us -> 344 us (0.910)
  waiting for transfers between devices: 275 us -> 253 us
  local copies, waits for them, and re-layouts: 34.4 us -> 28.5 us
  starting transfers between devices: 18.8 us -> 14.2 us
    reduce_scatter x2, waiting for transfers between devices: 186 us -> 96.3 us  [the longest x1 96.3 us: ffn(): lax.psum_scatter(jnp.dot(xg, w1, preferred_element_type=jnp.float32), 'cz...]
    all_to_all x4 -> x2, waiting for transfers between devices: 12.5 us -> 75.2 us  [the longest x1 50.5 us: handover(): lax.all_to_all(picked, 'row', split_axis=3, concat_axis=0, tiled=True)]
    ppermute x0 -> x4, waiting for transfers between devices: none -> 60.7 us  [the longest x1 30.4 us: ffn(): lax.ppermute(down_weight, 'cx', SWAP)]
    all_gather x1, waiting for transfers between devices: 77 us -> 21 us  [ffn(): hg = lax.all_gather(hidden, 'cz', axis=0, tiled=True)]
    unnamed x23 -> x14, local copies, waits for them, and re-layouts: 14 us -> 2.67 us
    all_to_all x4 -> x2, starting transfers between devices: 18.5 us -> 9.35 us  [the longest x1 5.1 us: handover(): lax.all_to_all(picked, 'row', split_axis=3, concat_axis=0, tiled=True)]
    all_to_all x6 -> x2, local copies, waits for them, and re-layouts: 13 us -> 7.19 us  [handover(): lax.all_to_all(picked, 'row', split_axis=3, concat_axis=0, tiled=True)]
    ppermute x0 -> x4, starting transfers between devices: none -> 4.75 us  [the longest x1 1.58 us: ffn(): lax.ppermute(up_weight, 'cx', SWAP)]
  transfers between devices with their start and end apart: 7 -> 9, of which waited for: 3 -> 6; matrix products, arithmetic and copies ran while one was open for 11% -> 9% of each run, Pallas kernels for 0% -> 0%
where the time goes in v1:
time: 344 us; the launch traced here: 342 us
  waiting for transfers between devices  253 us (74%)
  local copies, waits for them, and re-layouts  28.5 us (8%)
  starting transfers between devices  14.2 us (4%)
  between operations  13.9 us (4%)
  blocking collectives  13.6 us (4%)
  matrix products  12.7 us (4%)
  other arithmetic  6.26 us (2%)
    reduce_scatter x1, waiting for transfers between devices, ffn(): lax.psum_scatter(jnp.dot(xg, w1, preferred_element_type=jnp.float32), 'cz...  96.3 us
    all_to_all x1, waiting for transfers between devices, handover(): lax.all_to_all(picked, 'row', split_axis=3, concat_axis=0, tiled=True)  50.5 us
    ppermute x1, waiting for transfers between devices, ffn(): lax.ppermute(down_weight, 'cx', SWAP)  30.4 us
    ppermute x1, waiting for transfers between devices, ffn(): recv = lax.ppermute(theirs, 'cx', SWAP)  30.3 us
    all_to_all x1, waiting for transfers between devices, handover(): both = lax.all_to_all(rows, 'req', split_axis=0, concat_axis=1, tiled=True)  24.7 us
    all_gather x1, waiting for transfers between devices, ffn(): hg = lax.all_gather(hidden, 'cz', axis=0, tiled=True)  21 us
    all_gather x1, blocking collectives, ffn(): xg = lax.all_gather(xa, 'row', axis=0, tiled=True)  13.6 us
    all_to_all x2, local copies, waits for them, and re-layouts, handover(): lax.all_to_all(picked, 'row', split_axis=3, concat_axis=0, tiled=True)  7.19 us
  transfers between devices with their start and end apart: 9, of which 6 were waited for; matrix products, arithmetic and copies ran while one was open for 9% of the time, Pallas kernels for 0%

profile of v1, /device:TPU:8, one launch (start us, length us, event | category | flops | bytes accessed | tf_op | source)
XLA Modules:
  0.0 342.4 jit_solution(12249648840841902804)
XLA Ops:
  7.2 0.0 copy-start
  7.2 0.0 reduce-scatter.3.cloned.1.call-start
  7.2 1.6 collective-permute-start.1
  8.8 0.8 dynamic-slice_bitcast_fusion.1
  9.6 0.6 collective-permute-start
  10.2 30.3 %collective-permute-done = bf16[96,256]{1,0:T(8,128)(2,1)S(1)} collective-permute-done((bf16[96,256]{1,0:T(8,128)(2,1)S(1)}, bf16[96,256]{1,0:T(8,128)(2,1)S(1)}, u32[]{:S(2)}, u32[]{:S(2)}) %collective-permute-start) | collective-permute-done | bytes 49184 | tf_op jit(solution)/shard_map/ppermute | solution.py:43
  40.5 13.6 %all_gather.6 = bf16[768,512]{1,0:T(8,128)(2,1)S(1)} all-gather(bf16[96,512]{1,0:T(8,128)(2,1)S(1)} %pad_maximum_fusion.1), channel_id=1, replica_groups=mesh['row'=8,'cx'=2,'cz'=8,'req'=2] {'row'}, dimensions={0}, use_global_device_ids=true | all-gather | bytes 884736 | tf_op jit(solution)/shard_map/all_gather | solution.py:45
  54.1 0.0 collective-permute-done.1
  54.1 6.9 %fusion = f32[768,2688]{1,0:T(8,128)} fusion(bf16[768,512]{1,0:T(8,128)(2,1)S(1)} %all_gather.6, bf16[256,2688]{1,0:T(8,128)(2,1)S(1)} %collective-permute-done.1, bf16[256,2688]{1,0:T(8,128)(2,1)} %param.8), kind=kOutput, calls=%fused_computation.7 | convolution fusion | flops 2119434240 | bytes 11796480 | tf_op jit(solution)/shard_map/dot_general | solution.py:48
  61.1 0.0 reduce-scatter.3.cloned.1.call-update
  61.1 0.0 all-gather.2.cloned.1.call-start
  61.1 96.3 %reduce-scatter.3.cloned.1.call-done = f32[96,2688]{1,0:T(8,128)} async-done(((f32[768,2688]{1,0:T(8,128)}), f32[96,2688]{1,0:T(8,128)}) %reduce-scatter.3.cloned.1.call-update) | async-done | bytes 1032208 | tf_op jit(solution)/shard_map/reduce_scatter | solution.py:47
  157.4 2.1 multiply_convert_fusion
  159.5 0.0 all-gather.2.cloned.1.call-update
  159.5 0.0 reduce-scatter.5.cloned.1.call-start
  159.6 0.0 copy-done.4
  159.6 1.5 collective-permute-start.2
  161.1 30.4 %collective-permute-done.2 = bf16[2688,256]{1,0:T(8,128)(2,1)S(1)} collective-permute-done((bf16[2688,256]{1,0:T(8,128)(2,1)S(1)}, bf16[2688,256]{1,0:T(8,128)(2,1)S(1)}, u32[]{:S(2)}, u32[]{:S(2)}) %collective-permute-start.2) | collective-permute-done | bytes 1376288 | tf_op jit(solution)/shard_map/ppermute | solution.py:56
  191.5 21.0 %all-gather.2.cloned.1.call-done = bf16[768,2688]{1,0:T(8,128)(2,1)} async-done(((bf16[96,2688]{1,0:T(8,128)(2,1)}), bf16[768,2688]{1,0:T(8,128)(2,1)}) %all-gather.2.cloned.1.call-update) | async-done | bytes 4128784 | tf_op jit(solution)/shard_map/all_gather | solution.py:55
  212.6 5.7 %fusion.4 = f32[768,512]{1,0:T(8,128)} fusion(bf16[768,2688]{1,0:T(8,128)(2,1)} %all-gather.2.cloned.1.call-done, bf16[2688,256]{1,0:T(8,128)(2,1)S(1)} %collective-permute-done.2, bf16[2688,256]{1,0:T(8,128)(2,1)S(1)} %copy-done.4), kind=kOutput, calls=%fused_computation.11 | convolution fusion | flops 2119434240 | bytes 8454144 | tf_op jit(solution)/shard_map/dot_general | solution.py:57
  218.3 0.0 reduce-scatter.5.cloned.1.call-update
  218.4 0.2 select_reduce_fusion.1
  218.6 0.1 select_reduce_fusion.2
  218.7 0.6 gather_fusion.1
  219.3 0.7 copy.35
  220.0 4.8 %gather_fusion = f32[8,8,64,128]{3,2,1,0:T(8,128)} fusion(f32[24,8,64,128]{3,2,1,0:T(8,128)} %bitcast.45, s32[1024]{0:T(1024)S(1)} %pad_clamp_fusion.2), kind=kCustom, calls=%fused_computation | custom fusion | bytes 4194336 | tf_op jit(solution)/shard_map/gather | solution.py:26
  224.8 2.0 pad_maximum_fusion
  226.9 4.4 %copy.36 = f32[8,1,8,64,131]{4,2,0,1,3:T(8,128)} copy(f32[8,1,8,64,131]{4,3,2,0,1:T(8,128)S(1)} %pad_maximum_fusion) | data formatting | bytes 4292608 | tf_op jit(solution)/shard_map/concatenate | solution.py:26
  231.3 5.1 %all-to-all-start = ((f32[8,1,8,64,131]{4,2,0,1,3:T(8,128)}), f32[8,1,8,64,131]{4,2,0,1,3:T(8,128)}, u32[]{:S(2)}, u32[]{:S(2)}) async-start(f32[8,1,8,64,131]{4,2,0,1,3:T(8,128)} %copy.36), calls=%async_computation.2 | async-start | bytes 8388608 | tf_op jit(solution)/shard_map/all_to_all | solution.py:27
  236.4 0.1 select_reduce_fusion
  236.5 0.7 gather_fusion.3
  237.2 0.7 gather_fusion.2
  237.9 50.5 %all-to-all-done = f32[8,1,8,64,131]{4,2,0,1,3:T(8,128)} async-done(((f32[8,1,8,64,131]{4,2,0,1,3:T(8,128)}), f32[8,1,8,64,131]{4,2,0,1,3:T(8,128)}, u32[]{:S(2)}, u32[]{:S(2)}) %all-to-all-start) | async-done | bytes 2146336 | tf_op jit(solution)/shard_map/all_to_all | solution.py:27
  288.4 4.6 %copy.43 = f32[8,1,8,64,131]{4,3,2,0,1:T(8,128)S(1)} copy(f32[8,1,8,64,131]{4,2,0,1,3:T(8,128)} %all-to-all-done) | data formatting | bytes 4292608 | tf_op jit(solution)/shard_map/all_to_all | solution.py:27
  293.0 2.6 copy.38
  295.6 4.2 %gather_fusion.4 = f32[32,8,8,131]{3,2,1,0:T(8,128)} fusion(f32[64,8,8,131]{3,2,1,0:T(8,128)} %bitcast.39, s32[1024]{0:T(1024)S(1)} %pad_clamp_fusion), kind=kCustom, calls=%fused_computation.4 | custom fusion | bytes 2146432 | tf_op jit(solution)/shard_map/gather | solution.py:30
  299.8 4.2 %all-to-all-start.1 = ((f32[32,1,8,8,131]{4,3,2,1,0:T(8,128)}), f32[32,1,8,8,131]{4,3,2,1,0:T(8,128)S(1)}, u32[]{:S(2)}, u32[]{:S(2)}) async-start(f32[32,1,8,8,131]{4,3,2,1,0:T(8,128)} %bitcast.42), calls=%async_computation.3 | async-start | bytes 4194304 | tf_op jit(solution)/shard_map/all_to_all | solution.py:31
  304.0 1.6 fusion.17
  305.6 1.0 collective-permute-start.3
  306.7 24.7 %all-to-all-done.1 = f32[32,1,8,8,131]{4,3,2,1,0:T(8,128)S(1)} async-done(((f32[32,1,8,8,131]{4,3,2,1,0:T(8,128)}), f32[32,1,8,8,131]{4,3,2,1,0:T(8,128)S(1)}, u32[]{:S(2)}, u32[]{:S(2)}) %all-to-all-start.1) | async-done | bytes 1073184 | tf_op jit(solution)/shard_map/all_to_all | solution.py:31
  331.4 0.1 slice.28
  331.5 0.0 copy-start.1
  331.5 0.1 slice.29
  331.6 0.0 copy-start.2
  331.6 1.1 copy.40
  332.7 1.5 copy.41
  334.2 0.0 collective-permute-done.3
  334.2 1.6 fusion.9
  (18 shorter events, 0.1 us)
Async XLA Ops:
  7.2 211.5 %copy-start = (f32[24,1,8,64,3]{3,2,4,1,0:T(8,128)S(1)}, f32[24,1,8,64,3]{3,2,4,1,0:T(8,128)}, u32[]{:S(2)}) copy-start(f32[24,1,8,64,3]{3,2,4,1,0:T(8,128)} %param.11) | copy-start | bytes 442372
  7.2 150.2 %reduce-scatter.3.cloned.1.call-start = ((), (), s32[]{:S(2)}) async-start(), calls=%async_computation.4 | async-start | bytes 9289728 | tf_op jit(solution)/shard_map/reduce_scatter | solution.py:47
  7.2 46.9 %collective-permute-start.1 = (bf16[256,2688]{1,0:T(8,128)(2,1)}, bf16[256,2688]{1,0:T(8,128)(2,1)S(1)}, u32[]{:S(2)}, u32[]{:S(2)}) collective-permute-start(bf16[256,2688]{1,0:T(8,128)(2,1)} %param.8), channel_id=1, source_target_pairs={{0,16},{16,0},{1,17},{17,1},{2,18},{18,2},{3,19},{19,3},{4,20},{20... | collective-permute-start | bytes 4128776 | tf_op jit(solution)/shard_map/ppermute | solution.py:46
  9.6 30.9 %collective-permute-start = (bf16[96,256]{1,0:T(8,128)(2,1)S(1)}, bf16[96,256]{1,0:T(8,128)(2,1)S(1)}, u32[]{:S(2)}, u32[]{:S(2)}) collective-permute-start(bf16[96,256]{1,0:T(8,128)(2,1)S(1)} %get-tuple-element.29), channel_id=1, source_target_pairs={{0,16},{16,0},{1,17},{17,1},{2,18},{18,2},{3,19},{19,3},{4,20},{20... | collective-permute-start | bytes 147464 | tf_op jit(solution)/shard_map/ppermute | solution.py:43
  61.1 98.5 %copy-start.4 = (bf16[2688,256]{1,0:T(8,128)(2,1)S(1)}, bf16[2688,256]{1,0:T(8,128)(2,1)}, u32[]{:S(2)}) copy-start(bf16[2688,256]{1,0:T(8,128)(2,1)} %param.9) | copy-start | bytes 4128772
  61.1 151.5 %all-gather.2.cloned.1.call-start = ((), (), s32[]{:S(2)}) async-start(), calls=%async_computation.5 | async-start | bytes 4644864 | tf_op jit(solution)/shard_map/all_gather | solution.py:55
  159.5 144.5 %reduce-scatter.5.cloned.1.call-start = ((), (), s32[]{:S(2)}) async-start(), calls=%async_computation.6 | async-start | bytes 1769472 | tf_op jit(solution)/shard_map/reduce_scatter | solution.py:58
  159.6 32.0 %collective-permute-start.2 = (bf16[2688,256]{1,0:T(8,128)(2,1)S(1)}, bf16[2688,256]{1,0:T(8,128)(2,1)S(1)}, u32[]{:S(2)}, u32[]{:S(2)}) collective-permute-start(bf16[2688,256]{1,0:T(8,128)(2,1)S(1)} %copy-done.4), channel_id=1, source_target_pairs={{0,16},{16,0},{1,17},{17,1},{2,18},{18,2},{3,19},{19,3},{4,20},{20... | collective-permute-start | bytes 4128776 | tf_op jit(solution)/shard_map/ppermute | solution.py:56
  161.1 57.2 %copy-start.3 = (s32[32]{0:T(128)S(1)}, s32[32]{0:T(128)}, u32[]{:S(2)}) copy-start(s32[32]{0:T(128)} %param.12) | copy-start | bytes 388
  231.3 5.1 %copy-start.5 = (s32[32]{0:T(128)S(1)}, s32[32]{0:T(128)}, u32[]{:S(2)}) copy-start(s32[32]{0:T(128)} %param.13) | copy-start | bytes 388
  231.3 57.1 %all-to-all-start = ((f32[8,1,8,64,131]{4,2,0,1,3:T(8,128)}), f32[8,1,8,64,131]{4,2,0,1,3:T(8,128)}, u32[]{:S(2)}, u32[]{:S(2)}) async-start(f32[8,1,8,64,131]{4,2,0,1,3:T(8,128)} %copy.36), calls=%async_computation.2 | async-start | bytes 8388608 | tf_op jit(solution)/shard_map/all_to_all | solution.py:27
  299.8 31.6 %all-to-all-start.1 = ((f32[32,1,8,8,131]{4,3,2,1,0:T(8,128)}), f32[32,1,8,8,131]{4,3,2,1,0:T(8,128)S(1)}, u32[]{:S(2)}, u32[]{:S(2)}) async-start(f32[32,1,8,8,131]{4,3,2,1,0:T(8,128)} %bitcast.42), calls=%async_computation.3 | async-start | bytes 4194304 | tf_op jit(solution)/shard_map/all_to_all | solution.py:31
  305.6 28.6 %collective-permute-start.3 = (f32[96,256]{1,0:T(8,128)}, f32[96,256]{1,0:T(8,128)}, u32[]{:S(2)}, u32[]{:S(2)}) collective-permute-start(f32[96,256]{1,0:T(8,128)} %get-tuple-element.27), channel_id=1, source_target_pairs={{0,16},{16,0},{1,17},{17,1},{2,18},{18,2},{3,19},{19,3},{4,20},{20... | collective-permute-start | bytes 294920 | tf_op jit(solution)/shard_map/ppermute | solution.py:60
  331.5 2.8 copy-start.1
  331.6 2.7 copy-start.2
Sparse Core Ops, SparseCore 0:
  61.2 96.1 reduce-scatter.2
  159.8 52.7 all-gather.1
  218.5 36.9 reduce-scatter.4

commit v2 on v1

--- a/solution.py
+++ b/solution.py
@@ -4,6 +4,7 @@
 from jax import lax
 from jax.sharding import Mesh
 from jax.sharding import PartitionSpec as P
+
 
 MOST = 8
 SWAP = [(0, 1), (1, 0)]
@@ -25,8 +26,7 @@
     local_slot = jnp.sum(jnp.where(chosen, finish_ids[None, :] - r * local, 0), axis=1)
     picked = jnp.concatenate([pool_states[local_slot], pool_edges[local_slot]], axis=-1)
     arrived = lax.all_to_all(picked, "row", split_axis=3, concat_axis=0, tiled=True)
-    source = inverse
-    wanted = row_of[source] * MOST + rank[source]
+    wanted = row_of[inverse] * MOST + rank[inverse]
     rows = arrived[wanted]
     both = lax.all_to_all(rows, "req", split_axis=0, concat_axis=1, tiled=True)
     n = pool_states.shape[-1]
@@ -43,17 +43,15 @@
     recv = lax.ppermute(theirs, "cx", SWAP)
     xa = jnp.concatenate([mine, recv], axis=1)
     xg = lax.all_gather(xa, "row", axis=0, tiled=True)
-    w1 = jnp.concatenate([up_weight, lax.ppermute(up_weight, "cx", SWAP)], axis=0)
-    preact = lax.psum_scatter(
-        jnp.dot(xg, w1, preferred_element_type=jnp.float32),
-        "cz",
-        scatter_dimension=0,
-        tiled=True,
-    )
+    w1p = lax.ppermute(up_weight, "cx", SWAP)
+    w1 = jnp.concatenate([up_weight, w1p], axis=0)
+    partial = jnp.dot(xg, w1, preferred_element_type=jnp.float32)
+    preact = lax.psum_scatter(partial, "cz", scatter_dimension=0, tiled=True)
     active = jnp.maximum(preact, 0.0)
     hidden = (active * active).astype(jnp.bfloat16)
     hg = lax.all_gather(hidden, "cz", axis=0, tiled=True)
-    w2 = jnp.concatenate([down_weight, lax.ppermute(down_weight, "cx", SWAP)], axis=1)
+    w2p = lax.ppermute(down_weight, "cx", SWAP)
+    w2 = jnp.concatenate([down_weight, w2p], axis=1)
     products = jnp.dot(hg, w2, preferred_element_type=jnp.float32)
     summed = lax.psum_scatter(products, "row", scatter_dimension=0, tiled=True)
     own = summed[:, :width]

time: 344 us -> 344 us (level)
  no operation moved by 1% of the time
where the time goes in v2:
time: 344 us; the launch traced here: 342 us
  waiting for transfers between devices  253 us (74%)
  local copies, waits for them, and re-layouts  28.5 us (8%)
  starting transfers between devices  14.2 us (4%)
  between operations  13.9 us (4%)
  blocking collectives  13.6 us (4%)
  matrix products  12.7 us (4%)
  other arithmetic  6.26 us (2%)
    reduce_scatter x1, waiting for transfers between devices, ffn(): preact = lax.psum_scatter(partial, 'cz', scatter_dimension=0, tiled=True)  96.3 us
    all_to_all x1, waiting for transfers between devices, handover(): lax.all_to_all(picked, 'row', split_axis=3, concat_axis=0, tiled=True)  50.5 us
    ppermute x1, waiting for transfers between devices, ffn(): w2p = lax.ppermute(down_weight, 'cx', SWAP)  30.4 us
    ppermute x1, waiting for transfers between devices, ffn(): recv = lax.ppermute(theirs, 'cx', SWAP)  30.3 us
    all_to_all x1, waiting for transfers between devices, handover(): both = lax.all_to_all(rows, 'req', split_axis=0, concat_axis=1, tiled=True)  24.7 us
    all_gather x1, waiting for transfers between devices, ffn(): hg = lax.all_gather(hidden, 'cz', axis=0, tiled=True)  21 us
    all_gather x1, blocking collectives, ffn(): xg = lax.all_gather(xa, 'row', axis=0, tiled=True)  13.6 us
    all_to_all x2, local copies, waits for them, and re-layouts, handover(): lax.all_to_all(picked, 'row', split_axis=3, concat_axis=0, tiled=True)  7.19 us
  transfers between devices with their start and end apart: 9, of which 6 were waited for; matrix products, arithmetic and copies ran while one was open for 9% of the time, Pallas kernels for 0%

profile of v2, /device:TPU:8, one launch (start us, length us, event | category | flops | bytes accessed | tf_op | source)
XLA Modules:
  0.0 342.4 jit_solution(12249648840841902804)
XLA Ops:
  7.2 0.0 copy-start
  7.2 0.0 reduce-scatter.3.cloned.1.call-start
  7.2 1.6 collective-permute-start.1
  8.8 0.8 dynamic-slice_bitcast_fusion.1
  9.6 0.6 collective-permute-start
  10.2 30.3 %collective-permute-done = bf16[96,256]{1,0:T(8,128)(2,1)S(1)} collective-permute-done((bf16[96,256]{1,0:T(8,128)(2,1)S(1)}, bf16[96,256]{1,0:T(8,128)(2,1)S(1)}, u32[]{:S(2)}, u32[]{:S(2)}) %collective-permute-start) | collective-permute-done | bytes 49184 | tf_op jit(solution)/shard_map/ppermute | solution.py:43
  40.5 13.6 %all_gather.6 = bf16[768,512]{1,0:T(8,128)(2,1)S(1)} all-gather(bf16[96,512]{1,0:T(8,128)(2,1)S(1)} %pad_maximum_fusion.1), channel_id=1, replica_groups=mesh['row'=8,'cx'=2,'cz'=8,'req'=2] {'row'}, dimensions={0}, use_global_device_ids=true | all-gather | bytes 884736 | tf_op jit(solution)/shard_map/all_gather | solution.py:45
  54.1 0.0 collective-permute-done.1
  54.1 6.9 %fusion = f32[768,2688]{1,0:T(8,128)} fusion(bf16[768,512]{1,0:T(8,128)(2,1)S(1)} %all_gather.6, bf16[256,2688]{1,0:T(8,128)(2,1)S(1)} %collective-permute-done.1, bf16[256,2688]{1,0:T(8,128)(2,1)} %param.8), kind=kOutput, calls=%fused_computation.7 | convolution fusion | flops 2119434240 | bytes 11796480 | tf_op jit(solution)/shard_map/dot_general | solution.py:48
  61.1 0.0 reduce-scatter.3.cloned.1.call-update
  61.1 0.0 all-gather.2.cloned.1.call-start
  61.1 96.3 %reduce-scatter.3.cloned.1.call-done = f32[96,2688]{1,0:T(8,128)} async-done(((f32[768,2688]{1,0:T(8,128)}), f32[96,2688]{1,0:T(8,128)}) %reduce-scatter.3.cloned.1.call-update) | async-done | bytes 1032208 | tf_op jit(solution)/shard_map/reduce_scatter | solution.py:49
  157.4 2.1 multiply_convert_fusion
  159.5 0.0 all-gather.2.cloned.1.call-update
  159.5 0.0 reduce-scatter.5.cloned.1.call-start
  159.6 0.0 copy-done.4
  159.6 1.5 collective-permute-start.2
  161.1 30.4 %collective-permute-done.2 = bf16[2688,256]{1,0:T(8,128)(2,1)S(1)} collective-permute-done((bf16[2688,256]{1,0:T(8,128)(2,1)S(1)}, bf16[2688,256]{1,0:T(8,128)(2,1)S(1)}, u32[]{:S(2)}, u32[]{:S(2)}) %collective-permute-start.2) | collective-permute-done | bytes 1376288 | tf_op jit(solution)/shard_map/ppermute | solution.py:53
  191.5 21.0 %all-gather.2.cloned.1.call-done = bf16[768,2688]{1,0:T(8,128)(2,1)} async-done(((bf16[96,2688]{1,0:T(8,128)(2,1)}), bf16[768,2688]{1,0:T(8,128)(2,1)}) %all-gather.2.cloned.1.call-update) | async-done | bytes 4128784 | tf_op jit(solution)/shard_map/all_gather | solution.py:52
  212.6 5.7 %fusion.4 = f32[768,512]{1,0:T(8,128)} fusion(bf16[768,2688]{1,0:T(8,128)(2,1)} %all-gather.2.cloned.1.call-done, bf16[2688,256]{1,0:T(8,128)(2,1)S(1)} %collective-permute-done.2, bf16[2688,256]{1,0:T(8,128)(2,1)S(1)} %copy-done.4), kind=kOutput, calls=%fused_computation.11 | convolution fusion | flops 2119434240 | bytes 8454144 | tf_op jit(solution)/shard_map/dot_general | solution.py:55
  218.3 0.0 reduce-scatter.5.cloned.1.call-update
  218.4 0.2 select_reduce_fusion.1
  218.6 0.1 select_reduce_fusion.2
  218.7 0.6 gather_fusion.1
  219.3 0.7 copy.35
  220.0 4.8 %gather_fusion = f32[8,8,64,128]{3,2,1,0:T(8,128)} fusion(f32[24,8,64,128]{3,2,1,0:T(8,128)} %bitcast.45, s32[1024]{0:T(1024)S(1)} %pad_clamp_fusion.2), kind=kCustom, calls=%fused_computation | custom fusion | bytes 4194336 | tf_op jit(solution)/shard_map/gather | solution.py:27
  224.8 2.0 pad_maximum_fusion
  226.9 4.4 %copy.36 = f32[8,1,8,64,131]{4,2,0,1,3:T(8,128)} copy(f32[8,1,8,64,131]{4,3,2,0,1:T(8,128)S(1)} %pad_maximum_fusion) | data formatting | bytes 4292608 | tf_op jit(solution)/shard_map/concatenate | solution.py:27
  231.3 5.1 %all-to-all-start = ((f32[8,1,8,64,131]{4,2,0,1,3:T(8,128)}), f32[8,1,8,64,131]{4,2,0,1,3:T(8,128)}, u32[]{:S(2)}, u32[]{:S(2)}) async-start(f32[8,1,8,64,131]{4,2,0,1,3:T(8,128)} %copy.36), calls=%async_computation.2 | async-start | bytes 8388608 | tf_op jit(solution)/shard_map/all_to_all | solution.py:28
  236.4 0.1 select_reduce_fusion
  236.5 0.7 gather_fusion.3
  237.2 0.7 gather_fusion.2
  237.9 50.5 %all-to-all-done = f32[8,1,8,64,131]{4,2,0,1,3:T(8,128)} async-done(((f32[8,1,8,64,131]{4,2,0,1,3:T(8,128)}), f32[8,1,8,64,131]{4,2,0,1,3:T(8,128)}, u32[]{:S(2)}, u32[]{:S(2)}) %all-to-all-start) | async-done | bytes 2146336 | tf_op jit(solution)/shard_map/all_to_all | solution.py:28
  288.4 4.6 %copy.43 = f32[8,1,8,64,131]{4,3,2,0,1:T(8,128)S(1)} copy(f32[8,1,8,64,131]{4,2,0,1,3:T(8,128)} %all-to-all-done) | data formatting | bytes 4292608 | tf_op jit(solution)/shard_map/all_to_all | solution.py:28
  293.0 2.6 copy.38
  295.6 4.2 %gather_fusion.4 = f32[32,8,8,131]{3,2,1,0:T(8,128)} fusion(f32[64,8,8,131]{3,2,1,0:T(8,128)} %bitcast.39, s32[1024]{0:T(1024)S(1)} %pad_clamp_fusion), kind=kCustom, calls=%fused_computation.4 | custom fusion | bytes 2146432 | tf_op jit(solution)/shard_map/gather | solution.py:30
  299.8 4.2 %all-to-all-start.1 = ((f32[32,1,8,8,131]{4,3,2,1,0:T(8,128)}), f32[32,1,8,8,131]{4,3,2,1,0:T(8,128)S(1)}, u32[]{:S(2)}, u32[]{:S(2)}) async-start(f32[32,1,8,8,131]{4,3,2,1,0:T(8,128)} %bitcast.42), calls=%async_computation.3 | async-start | bytes 4194304 | tf_op jit(solution)/shard_map/all_to_all | solution.py:31
  304.0 1.6 fusion.17
  305.6 1.0 collective-permute-start.3
  306.7 24.7 %all-to-all-done.1 = f32[32,1,8,8,131]{4,3,2,1,0:T(8,128)S(1)} async-done(((f32[32,1,8,8,131]{4,3,2,1,0:T(8,128)}), f32[32,1,8,8,131]{4,3,2,1,0:T(8,128)S(1)}, u32[]{:S(2)}, u32[]{:S(2)}) %all-to-all-start.1) | async-done | bytes 1073184 | tf_op jit(solution)/shard_map/all_to_all | solution.py:31
  331.4 0.1 slice.28
  331.5 0.0 copy-start.1
  331.5 0.1 slice.29
  331.6 0.0 copy-start.2
  331.6 1.1 copy.40
  332.7 1.5 copy.41
  334.2 0.0 collective-permute-done.3
  334.2 1.6 fusion.9
  (18 shorter events, 0.1 us)
Async XLA Ops:
  7.2 211.5 %copy-start = (f32[24,1,8,64,3]{3,2,4,1,0:T(8,128)S(1)}, f32[24,1,8,64,3]{3,2,4,1,0:T(8,128)}, u32[]{:S(2)}) copy-start(f32[24,1,8,64,3]{3,2,4,1,0:T(8,128)} %param.11) | copy-start | bytes 442372
  7.2 150.2 %reduce-scatter.3.cloned.1.call-start = ((), (), s32[]{:S(2)}) async-start(), calls=%async_computation.4 | async-start | bytes 9289728 | tf_op jit(solution)/shard_map/reduce_scatter | solution.py:49
  7.2 46.9 %collective-permute-start.1 = (bf16[256,2688]{1,0:T(8,128)(2,1)}, bf16[256,2688]{1,0:T(8,128)(2,1)S(1)}, u32[]{:S(2)}, u32[]{:S(2)}) collective-permute-start(bf16[256,2688]{1,0:T(8,128)(2,1)} %param.8), channel_id=1, source_target_pairs={{0,16},{16,0},{1,17},{17,1},{2,18},{18,2},{3,19},{19,3},{4,20},{20... | collective-permute-start | bytes 4128776 | tf_op jit(solution)/shard_map/ppermute | solution.py:46
  9.6 30.9 %collective-permute-start = (bf16[96,256]{1,0:T(8,128)(2,1)S(1)}, bf16[96,256]{1,0:T(8,128)(2,1)S(1)}, u32[]{:S(2)}, u32[]{:S(2)}) collective-permute-start(bf16[96,256]{1,0:T(8,128)(2,1)S(1)} %get-tuple-element.29), channel_id=1, source_target_pairs={{0,16},{16,0},{1,17},{17,1},{2,18},{18,2},{3,19},{19,3},{4,20},{20... | collective-permute-start | bytes 147464 | tf_op jit(solution)/shard_map/ppermute | solution.py:43
  61.1 98.5 %copy-start.4 = (bf16[2688,256]{1,0:T(8,128)(2,1)S(1)}, bf16[2688,256]{1,0:T(8,128)(2,1)}, u32[]{:S(2)}) copy-start(bf16[2688,256]{1,0:T(8,128)(2,1)} %param.9) | copy-start | bytes 4128772
  61.1 151.5 %all-gather.2.cloned.1.call-start = ((), (), s32[]{:S(2)}) async-start(), calls=%async_computation.5 | async-start | bytes 4644864 | tf_op jit(solution)/shard_map/all_gather | solution.py:52
  159.5 144.5 %reduce-scatter.5.cloned.1.call-start = ((), (), s32[]{:S(2)}) async-start(), calls=%async_computation.6 | async-start | bytes 1769472 | tf_op jit(solution)/shard_map/reduce_scatter | solution.py:56
  159.6 32.0 %collective-permute-start.2 = (bf16[2688,256]{1,0:T(8,128)(2,1)S(1)}, bf16[2688,256]{1,0:T(8,128)(2,1)S(1)}, u32[]{:S(2)}, u32[]{:S(2)}) collective-permute-start(bf16[2688,256]{1,0:T(8,128)(2,1)S(1)} %copy-done.4), channel_id=1, source_target_pairs={{0,16},{16,0},{1,17},{17,1},{2,18},{18,2},{3,19},{19,3},{4,20},{20... | collective-permute-start | bytes 4128776 | tf_op jit(solution)/shard_map/ppermute | solution.py:53
  161.1 57.2 %copy-start.3 = (s32[32]{0:T(128)S(1)}, s32[32]{0:T(128)}, u32[]{:S(2)}) copy-start(s32[32]{0:T(128)} %param.12) | copy-start | bytes 388
  231.3 5.1 %copy-start.5 = (s32[32]{0:T(128)S(1)}, s32[32]{0:T(128)}, u32[]{:S(2)}) copy-start(s32[32]{0:T(128)} %param.13) | copy-start | bytes 388
  231.3 57.1 %all-to-all-start = ((f32[8,1,8,64,131]{4,2,0,1,3:T(8,128)}), f32[8,1,8,64,131]{4,2,0,1,3:T(8,128)}, u32[]{:S(2)}, u32[]{:S(2)}) async-start(f32[8,1,8,64,131]{4,2,0,1,3:T(8,128)} %copy.36), calls=%async_computation.2 | async-start | bytes 8388608 | tf_op jit(solution)/shard_map/all_to_all | solution.py:28
  299.8 31.6 %all-to-all-start.1 = ((f32[32,1,8,8,131]{4,3,2,1,0:T(8,128)}), f32[32,1,8,8,131]{4,3,2,1,0:T(8,128)S(1)}, u32[]{:S(2)}, u32[]{:S(2)}) async-start(f32[32,1,8,8,131]{4,3,2,1,0:T(8,128)} %bitcast.42), calls=%async_computation.3 | async-start | bytes 4194304 | tf_op jit(solution)/shard_map/all_to_all | solution.py:31
  305.6 28.6 %collective-permute-start.3 = (f32[96,256]{1,0:T(8,128)}, f32[96,256]{1,0:T(8,128)}, u32[]{:S(2)}, u32[]{:S(2)}) collective-permute-start(f32[96,256]{1,0:T(8,128)} %get-tuple-element.27), channel_id=1, source_target_pairs={{0,16},{16,0},{1,17},{17,1},{2,18},{18,2},{3,19},{19,3},{4,20},{20... | collective-permute-start | bytes 294920 | tf_op jit(solution)/shard_map/ppermute | solution.py:58
  331.5 2.8 copy-start.1
  331.6 2.7 copy-start.2
Sparse Core Ops, SparseCore 0:
  61.2 96.1 reduce-scatter.2
  159.8 52.7 all-gather.1
  218.5 36.9 reduce-scatter.4

commit v3 on v2

--- a/solution.py
+++ b/solution.py
@@ -43,10 +43,13 @@
     recv = lax.ppermute(theirs, "cx", SWAP)
     xa = jnp.concatenate([mine, recv], axis=1)
     xg = lax.all_gather(xa, "row", axis=0, tiled=True)
-    w1p = lax.ppermute(up_weight, "cx", SWAP)
-    w1 = jnp.concatenate([up_weight, w1p], axis=0)
-    partial = jnp.dot(xg, w1, preferred_element_type=jnp.float32)
-    preact = lax.psum_scatter(partial, "cz", scatter_dimension=0, tiled=True)
+    cut = up_weight.shape[1] // 2
+    pieces = []
+    for w in (up_weight[:, :cut], up_weight[:, cut:]):
+        wp = lax.ppermute(w, "cx", SWAP)
+        partial = jnp.dot(xg, jnp.concatenate([w, wp], axis=0), preferred_element_type=jnp.float32)
+        pieces.append(lax.psum_scatter(partial, "cz", scatter_dimension=0, tiled=True))
+    preact = jnp.concatenate(pieces, axis=1)
     active = jnp.maximum(preact, 0.0)
     hidden = (active * active).astype(jnp.bfloat16)
     hg = lax.all_gather(hidden, "cz", axis=0, tiled=True)

time: 344 us -> 348 us (1.012)
    ppermute x1 -> x2, waiting for transfers between devices: 0.01 us -> 16.2 us  [ffn(): wp = lax.ppermute(w, 'cx', SWAP)]
    ppermute x1, waiting for transfers between devices: 30.3 us -> 16.1 us  [ffn(): recv = lax.ppermute(theirs, 'cx', SWAP)]
    reduce_scatter x1 -> x2, waiting for transfers between devices: 96.3 us -> 95.3 us  [ffn(): lax.psum_scatter(partial, 'cz', scatter_dimension=0, tiled=True)]
  transfers between devices with their start and end apart: 9 -> 11, of which waited for: 6 -> 8; matrix products, arithmetic and copies ran while one was open for 9% -> 10% of each run, Pallas kernels for 0% -> 0%
where the time goes in v3:
time: 348 us; the launch traced here: 347 us
  waiting for transfers between devices  254 us (73%)
  local copies, waits for them, and re-layouts  29.9 us (9%)
  starting transfers between devices  15.9 us (5%)
  between operations  13.9 us (4%)
  blocking collectives  13.6 us (4%)
  matrix products  12.6 us (4%)
  other arithmetic  6.37 us (2%)
    reduce_scatter x2, waiting for transfers between devices, ffn(): lax.psum_scatter(partial, 'cz', scatter_dimension=0, tiled=True)  95.3 us
    all_to_all x1, waiting for transfers between devices, handover(): lax.all_to_all(picked, 'row', split_axis=3, concat_axis=0, tiled=True)  50.5 us
    ppermute x1, waiting for transfers between devices, ffn(): w2p = lax.ppermute(down_weight, 'cx', SWAP)  30.4 us
    all_to_all x1, waiting for transfers between devices, handover(): both = lax.all_to_all(rows, 'req', split_axis=0, concat_axis=1, tiled=True)  24.7 us
    all_gather x1, waiting for transfers between devices, ffn(): hg = lax.all_gather(hidden, 'cz', axis=0, tiled=True)  20.9 us
    ppermute x2, waiting for transfers between devices, ffn(): wp = lax.ppermute(w, 'cx', SWAP)  16.2 us
    ppermute x1, waiting for transfers between devices, ffn(): recv = lax.ppermute(theirs, 'cx', SWAP)  16.1 us
    all_gather x1, blocking collectives, ffn(): xg = lax.all_gather(xa, 'row', axis=0, tiled=True)  13.6 us
  transfers between devices with their start and end apart: 11, of which 8 were waited for; matrix products, arithmetic and copies ran while one was open for 10% of the time, Pallas kernels for 0%

profile of v3, /device:TPU:8, one launch (start us, length us, event | category | flops | bytes accessed | tf_op | source)
XLA Modules:
  0.0 346.5 jit_solution(8920849175743316506)
XLA Ops:
  7.2 0.0 reduce-scatter.4.cloned.1.call-start
  7.2 1.7 fusion.24
  8.9 0.3 copy.48
  9.2 1.6 collective-permute-start.1
  10.8 0.6 collective-permute-start
  11.4 16.1 %collective-permute-done = bf16[96,256]{1,0:T(8,128)(2,1)S(1)} collective-permute-done((bf16[96,256]{1,0:T(8,128)(2,1)S(1)}, bf16[96,256]{1,0:T(8,128)(2,1)S(1)}, u32[]{:S(2)}, u32[]{:S(2)}) %collective-permute-start) | collective-permute-done | bytes 49184 | tf_op jit(solution)/shard_map/ppermute | solution.py:43
  27.5 13.6 %all_gather.6 = bf16[768,512]{1,0:T(8,128)(2,1)S(1)} all-gather(bf16[96,512]{1,0:T(8,128)(2,1)S(1)} %pad_maximum_fusion.1), channel_id=1, replica_groups=mesh['row'=8,'cx'=2,'cz'=8,'req'=2] {'row'}, dimensions={0}, use_global_device_ids=true | all-gather | bytes 884736 | tf_op jit(solution)/shard_map/all_gather | solution.py:45
  41.1 3.4 fusion.4
  44.5 0.0 reduce-scatter.4.cloned.1.call-update
  44.5 0.0 reduce-scatter.6.cloned.1.call-start
  44.6 0.3 copy.49
  44.9 1.6 collective-permute-start.2
  46.4 16.2 %collective-permute-done.2 = bf16[256,1344]{0,1:T(8,128)(2,1)S(1)} collective-permute-done((bf16[256,1344]{0,1:T(8,128)(2,1)S(1)}, bf16[256,1344]{0,1:T(8,128)(2,1)S(1)}, u32[]{:S(2)}, u32[]{:S(2)}) %collective-permute-start.2) | collective-permute-done | bytes 688160 | tf_op jit(solution)/shard_map/ppermute | solution.py:49
  62.6 3.5 %fusion.8 = f32[768,1344]{1,0:T(8,128)} fusion(bf16[768,512]{1,0:T(8,128)(2,1)S(1)} %all_gather.6, bf16[256,1344]{0,1:T(8,128)(2,1)S(1)} %collective-permute-done.2, bf16[256,1344]{0,1:T(8,128)(2,1)S(1)} %copy.49), kind=kOutput, calls=%fused_computation.15 | convolution fusion | flops 1059717120 | bytes 6291456 | tf_op jit(solution)/shard_map/dot_general | solution.py:50
  66.1 0.0 reduce-scatter.6.cloned.1.call-update
  66.2 0.0 all-gather.2.cloned.1.call-start
  66.2 37.5 %reduce-scatter.4.cloned.1.call-done = f32[96,1344]{1,0:T(8,128)} async-done(((f32[768,1344]{1,0:T(8,128)}), f32[96,1344]{1,0:T(8,128)}) %reduce-scatter.4.cloned.1.call-update) | async-done | bytes 516112 | tf_op jit(solution)/shard_map/reduce_scatter | solution.py:51
  103.7 57.8 %reduce-scatter.6.cloned.1.call-done = f32[96,1344]{1,0:T(8,128)} async-done(((f32[768,1344]{1,0:T(8,128)}), f32[96,1344]{1,0:T(8,128)}) %reduce-scatter.6.cloned.1.call-update) | async-done | bytes 516112 | tf_op jit(solution)/shard_map/reduce_scatter | solution.py:51
  161.5 2.2 fusion.13
  163.8 0.0 reduce-scatter.8.cloned.1.call-start
  163.8 1.5 collective-permute-start.3
  165.4 30.4 %collective-permute-done.3 = bf16[2688,256]{1,0:T(8,128)(2,1)S(1)} collective-permute-done((bf16[2688,256]{1,0:T(8,128)(2,1)S(1)}, bf16[2688,256]{1,0:T(8,128)(2,1)S(1)}, u32[]{:S(2)}, u32[]{:S(2)}) %collective-permute-start.3) | collective-permute-done | bytes 1376288 | tf_op jit(solution)/shard_map/ppermute | solution.py:56
  195.8 20.9 %all-gather.2.cloned.1.call-done = bf16[768,2688]{1,0:T(8,128)(2,1)} async-done(((bf16[96,2688]{1,0:T(8,128)(2,1)}), bf16[768,2688]{1,0:T(8,128)(2,1)}) %all-gather.2.cloned.1.call-update) | async-done | bytes 4128784 | tf_op jit(solution)/shard_map/all_gather | solution.py:55
  216.7 5.8 %fusion = f32[768,512]{1,0:T(8,128)} fusion(bf16[768,2688]{1,0:T(8,128)(2,1)} %all-gather.2.cloned.1.call-done, bf16[2688,256]{1,0:T(8,128)(2,1)S(1)} %collective-permute-done.3, bf16[2688,256]{1,0:T(8,128)(2,1)S(1)} %copy-done.4), kind=kOutput, calls=%fused_computation.7 | convolution fusion | flops 2119434240 | bytes 8454144 | tf_op jit(solution)/shard_map/dot_general | solution.py:58
  222.5 0.2 select_reduce_fusion.1
  222.7 0.1 select_reduce_fusion.2
  222.9 0.6 gather_fusion.1
  223.4 0.7 copy.41
  224.1 4.8 %gather_fusion = f32[8,8,64,128]{3,2,1,0:T(8,128)} fusion(f32[24,8,64,128]{3,2,1,0:T(8,128)} %bitcast.46, s32[1024]{0:T(1024)S(1)} %pad_clamp_fusion.2), kind=kCustom, calls=%fused_computation | custom fusion | bytes 4194336 | tf_op jit(solution)/shard_map/gather | solution.py:27
  228.9 2.0 pad_maximum_fusion
  231.0 4.4 %copy.42 = f32[8,1,8,64,131]{4,2,0,1,3:T(8,128)} copy(f32[8,1,8,64,131]{4,3,2,0,1:T(8,128)S(1)} %pad_maximum_fusion) | data formatting | bytes 4292608 | tf_op jit(solution)/shard_map/concatenate | solution.py:27
  235.4 5.1 %all-to-all-start = ((f32[8,1,8,64,131]{4,2,0,1,3:T(8,128)}), f32[8,1,8,64,131]{4,2,0,1,3:T(8,128)}, u32[]{:S(2)}, u32[]{:S(2)}) async-start(f32[8,1,8,64,131]{4,2,0,1,3:T(8,128)} %copy.42), calls=%async_computation.3 | async-start | bytes 8388608 | tf_op jit(solution)/shard_map/all_to_all | solution.py:28
  240.5 0.1 select_reduce_fusion
  240.7 0.7 gather_fusion.3
  241.3 0.7 gather_fusion.2
  242.1 50.5 %all-to-all-done = f32[8,1,8,64,131]{4,2,0,1,3:T(8,128)} async-done(((f32[8,1,8,64,131]{4,2,0,1,3:T(8,128)}), f32[8,1,8,64,131]{4,2,0,1,3:T(8,128)}, u32[]{:S(2)}, u32[]{:S(2)}) %all-to-all-start) | async-done | bytes 2146336 | tf_op jit(solution)/shard_map/all_to_all | solution.py:28
  292.5 4.6 %copy.51 = f32[8,1,8,64,131]{4,3,2,0,1:T(8,128)S(1)} copy(f32[8,1,8,64,131]{4,2,0,1,3:T(8,128)} %all-to-all-done) | data formatting | bytes 4292608 | tf_op jit(solution)/shard_map/all_to_all | solution.py:28
  297.2 2.6 copy.44
  299.7 4.2 %gather_fusion.4 = f32[32,8,8,131]{3,2,1,0:T(8,128)} fusion(f32[64,8,8,131]{3,2,1,0:T(8,128)} %bitcast.40, s32[1024]{0:T(1024)S(1)} %pad_clamp_fusion), kind=kCustom, calls=%fused_computation.4 | custom fusion | bytes 2146432 | tf_op jit(solution)/shard_map/gather | solution.py:30
  303.9 4.2 %all-to-all-start.1 = ((f32[32,1,8,8,131]{4,3,2,1,0:T(8,128)}), f32[32,1,8,8,131]{4,3,2,1,0:T(8,128)S(1)}, u32[]{:S(2)}, u32[]{:S(2)}) async-start(f32[32,1,8,8,131]{4,3,2,1,0:T(8,128)} %bitcast.43), calls=%async_computation.4 | async-start | bytes 4194304 | tf_op jit(solution)/shard_map/all_to_all | solution.py:31
  308.2 1.6 fusion.25
  309.8 1.0 collective-permute-start.4
  310.8 24.7 %all-to-all-done.1 = f32[32,1,8,8,131]{4,3,2,1,0:T(8,128)S(1)} async-done(((f32[32,1,8,8,131]{4,3,2,1,0:T(8,128)}), f32[32,1,8,8,131]{4,3,2,1,0:T(8,128)S(1)}, u32[]{:S(2)}, u32[]{:S(2)}) %all-to-all-start.1) | async-done | bytes 1073184 | tf_op jit(solution)/shard_map/all_to_all | solution.py:31
  335.5 0.1 slice.36
  335.6 0.1 slice.37
  335.7 1.1 copy.46
  336.8 1.5 copy.47
  338.4 1.6 fusion.15
  (27 shorter events, 0.2 us)
Async XLA Ops:
  7.2 215.7 %copy-start = (f32[24,1,8,64,3]{3,2,4,1,0:T(8,128)S(1)}, f32[24,1,8,64,3]{3,2,4,1,0:T(8,128)}, u32[]{:S(2)}) copy-start(f32[24,1,8,64,3]{3,2,4,1,0:T(8,128)} %param.11) | copy-start | bytes 442372
  7.2 3.6 %copy-start.1 = (bf16[192,256]{1,0:T(8,128)(2,1)S(1)}, bf16[192,256]{1,0:T(8,128)(2,1)}, u32[]{:S(2)}) copy-start(bf16[192,256]{1,0:T(8,128)(2,1)} %param.7) | copy-start | bytes 294916
  7.2 96.6 %reduce-scatter.4.cloned.1.call-start = ((), (), s32[]{:S(2)}) async-start(), calls=%async_computation.5 | async-start | bytes 4866048 | tf_op jit(solution)/shard_map/reduce_scatter | solution.py:51
  9.2 32.0 %collective-permute-start.1 = (bf16[256,1344]{0,1:T(8,128)(2,1)S(1)}, bf16[256,1344]{0,1:T(8,128)(2,1)S(1)}, u32[]{:S(2)}, u32[]{:S(2)}) collective-permute-start(bf16[256,1344]{0,1:T(8,128)(2,1)S(1)} %copy.48), channel_id=1, source_target_pairs={{0,16},{16,0},{1,17},{17,1},{2,18},{18,2},{3,19},{19,3},{4,20},{20... | collective-permute-start | bytes 2064392 | tf_op jit(solution)/shard_map/ppermute | solution.py:49
  10.8 16.7 %collective-permute-start = (bf16[96,256]{1,0:T(8,128)(2,1)S(1)}, bf16[96,256]{1,0:T(8,128)(2,1)S(1)}, u32[]{:S(2)}, u32[]{:S(2)}) collective-permute-start(bf16[96,256]{1,0:T(8,128)(2,1)S(1)} %get-tuple-element.31), channel_id=1, source_target_pairs={{0,16},{16,0},{1,17},{17,1},{2,18},{18,2},{3,19},{19,3},{4,20},{20... | collective-permute-start | bytes 147464 | tf_op jit(solution)/shard_map/ppermute | solution.py:43
  44.5 117.0 %reduce-scatter.6.cloned.1.call-start = ((), (), s32[]{:S(2)}) async-start(), calls=%async_computation.6 | async-start | bytes 4866048 | tf_op jit(solution)/shard_map/reduce_scatter | solution.py:51
  44.9 17.8 %collective-permute-start.2 = (bf16[256,1344]{0,1:T(8,128)(2,1)S(1)}, bf16[256,1344]{0,1:T(8,128)(2,1)S(1)}, u32[]{:S(2)}, u32[]{:S(2)}) collective-permute-start(bf16[256,1344]{0,1:T(8,128)(2,1)S(1)} %copy.49), channel_id=1, source_target_pairs={{0,16},{16,0},{1,17},{17,1},{2,18},{18,2},{3,19},{19,3},{4,20},{20... | collective-permute-start | bytes 2064392 | tf_op jit(solution)/shard_map/ppermute | solution.py:49
  66.1 97.7 %copy-start.4 = (bf16[2688,256]{1,0:T(8,128)(2,1)S(1)}, bf16[2688,256]{1,0:T(8,128)(2,1)}, u32[]{:S(2)}) copy-start(bf16[2688,256]{1,0:T(8,128)(2,1)} %param.9) | copy-start | bytes 4128772
  66.2 150.6 %all-gather.2.cloned.1.call-start = ((), (), s32[]{:S(2)}) async-start(), calls=%async_computation.7 | async-start | bytes 4644864 | tf_op jit(solution)/shard_map/all_gather | solution.py:55
  163.8 144.4 %reduce-scatter.8.cloned.1.call-start = ((), (), s32[]{:S(2)}) async-start(), calls=%async_computation.8 | async-start | bytes 1769472 | tf_op jit(solution)/shard_map/reduce_scatter | solution.py:59
  163.8 32.0 %collective-permute-start.3 = (bf16[2688,256]{1,0:T(8,128)(2,1)S(1)}, bf16[2688,256]{1,0:T(8,128)(2,1)S(1)}, u32[]{:S(2)}, u32[]{:S(2)}) collective-permute-start(bf16[2688,256]{1,0:T(8,128)(2,1)S(1)} %copy-done.4), channel_id=1, source_target_pairs={{0,16},{16,0},{1,17},{17,1},{2,18},{18,2},{3,19},{19,3},{4,20},{20... | collective-permute-start | bytes 4128776 | tf_op jit(solution)/shard_map/ppermute | solution.py:56
  165.4 57.1 %copy-start.3 = (s32[32]{0:T(128)S(1)}, s32[32]{0:T(128)}, u32[]{:S(2)}) copy-start(s32[32]{0:T(128)} %param.12) | copy-start | bytes 388
  235.4 5.1 %copy-start.5 = (s32[32]{0:T(128)S(1)}, s32[32]{0:T(128)}, u32[]{:S(2)}) copy-start(s32[32]{0:T(128)} %param.13) | copy-start | bytes 388
  235.4 57.1 %all-to-all-start = ((f32[8,1,8,64,131]{4,2,0,1,3:T(8,128)}), f32[8,1,8,64,131]{4,2,0,1,3:T(8,128)}, u32[]{:S(2)}, u32[]{:S(2)}) async-start(f32[8,1,8,64,131]{4,2,0,1,3:T(8,128)} %copy.42), calls=%async_computation.3 | async-start | bytes 8388608 | tf_op jit(solution)/shard_map/all_to_all | solution.py:28
  303.9 31.6 %all-to-all-start.1 = ((f32[32,1,8,8,131]{4,3,2,1,0:T(8,128)}), f32[32,1,8,8,131]{4,3,2,1,0:T(8,128)S(1)}, u32[]{:S(2)}, u32[]{:S(2)}) async-start(f32[32,1,8,8,131]{4,3,2,1,0:T(8,128)} %bitcast.43), calls=%async_computation.4 | async-start | bytes 4194304 | tf_op jit(solution)/shard_map/all_to_all | solution.py:31
  309.8 28.6 %collective-permute-start.4 = (f32[96,256]{1,0:T(8,128)}, f32[96,256]{1,0:T(8,128)}, u32[]{:S(2)}, u32[]{:S(2)}) collective-permute-start(f32[96,256]{1,0:T(8,128)} %get-tuple-element.29), channel_id=1, source_target_pairs={{0,16},{16,0},{1,17},{17,1},{2,18},{18,2},{3,19},{19,3},{4,20},{20... | collective-permute-start | bytes 294920 | tf_op jit(solution)/shard_map/ppermute | solution.py:61
  335.7 2.7 copy-start.2
Sparse Core Ops, SparseCore 0:
  44.7 59.0 reduce-scatter.3
  106.3 55.1 reduce-scatter.5
  163.9 52.7 all-gather.1
  222.6 36.9 reduce-scatter.7

commit v4 on v2

--- a/solution.py
+++ b/solution.py
@@ -8,6 +8,15 @@
 
 MOST = 8
 SWAP = [(0, 1), (1, 0)]
+CROSS = [(0, 3), (3, 0), (1, 2), (2, 1)]
+
+
+def fetch_partner(w, axis):
+    cut = w.shape[axis] // 2
+    near, far = jnp.split(w, [cut], axis=axis)
+    return jnp.concatenate(
+        [lax.ppermute(near, "cx", SWAP), lax.ppermute(far, ("cx", "req"), CROSS)], axis=axis
+    )
 
 
 def handover(pool_states, pool_edges, finish_ids, slot_perm):
@@ -43,14 +52,14 @@
     recv = lax.ppermute(theirs, "cx", SWAP)
     xa = jnp.concatenate([mine, recv], axis=1)
     xg = lax.all_gather(xa, "row", axis=0, tiled=True)
-    w1p = lax.ppermute(up_weight, "cx", SWAP)
+    w1p = fetch_partner(up_weight, 1)
     w1 = jnp.concatenate([up_weight, w1p], axis=0)
     partial = jnp.dot(xg, w1, preferred_element_type=jnp.float32)
     preact = lax.psum_scatter(partial, "cz", scatter_dimension=0, tiled=True)
     active = jnp.maximum(preact, 0.0)
     hidden = (active * active).astype(jnp.bfloat16)
     hg = lax.all_gather(hidden, "cz", axis=0, tiled=True)
-    w2p = lax.ppermute(down_weight, "cx", SWAP)
+    w2p = fetch_partner(down_weight, 0)
     w2 = jnp.concatenate([down_weight, w2p], axis=1)
     products = jnp.dot(hg, w2, preferred_element_type=jnp.float32)
     summed = lax.psum_scatter(products, "row", scatter_dimension=0, tiled=True)

time: 344 us -> 331 us (0.962)
  waiting for transfers between devices: 253 us -> 235 us
  starting transfers between devices: 14.2 us -> 18.5 us
    ppermute x1, waiting for transfers between devices: 30.3 us -> 13.9 us  [ffn(): recv = lax.ppermute(theirs, 'cx', SWAP)]
    ppermute x2 -> x4, waiting for transfers between devices: 30.4 us -> 16.1 us  [the longest x2 13.7 us: fetch_partner(): lax.ppermute(near, 'cx', SWAP)]
    all_gather x1, waiting for transfers between devices: 21 us -> 33.2 us  [ffn(): hg = lax.all_gather(hidden, 'cz', axis=0, tiled=True)]
    ppermute x2 -> x4, starting transfers between devices: 3.13 us -> 7.32 us  [the longest x2 4.16 us: fetch_partner(): lax.ppermute(far, ('cx', 'req'), CROSS)]
  transfers between devices with their start and end apart: 9 -> 11, of which waited for: 6 -> 7; matrix products, arithmetic and copies ran while one was open for 9% -> 9% of each run, Pallas kernels for 0% -> 0%
where the time goes in v4:
time: 331 us; the launch traced here: 330 us
  waiting for transfers between devices  235 us (71%)
  local copies, waits for them, and re-layouts  29.7 us (9%)
  starting transfers between devices  18.5 us (6%)
  between operations  13.9 us (4%)
  blocking collectives  13.6 us (4%)
  matrix products  13.1 us (4%)
  other arithmetic  6.25 us (2%)
    reduce_scatter x1, waiting for transfers between devices, ffn(): preact = lax.psum_scatter(partial, 'cz', scatter_dimension=0, tiled=True)  96.3 us
    all_to_all x1, waiting for transfers between devices, handover(): lax.all_to_all(picked, 'row', split_axis=3, concat_axis=0, tiled=True)  50.5 us
    all_gather x1, waiting for transfers between devices, ffn(): hg = lax.all_gather(hidden, 'cz', axis=0, tiled=True)  33.2 us
    all_to_all x1, waiting for transfers between devices, handover(): both = lax.all_to_all(rows, 'req', split_axis=0, concat_axis=1, tiled=True)  24.7 us
    ppermute x1, waiting for transfers between devices, ffn(): recv = lax.ppermute(theirs, 'cx', SWAP)  13.9 us
    ppermute x2, waiting for transfers between devices, fetch_partner(): lax.ppermute(near, 'cx', SWAP)  13.7 us
    all_gather x1, blocking collectives, ffn(): xg = lax.all_gather(xa, 'row', axis=0, tiled=True)  13.6 us
    all_to_all x2, local copies, waits for them, and re-layouts, handover(): lax.all_to_all(picked, 'row', split_axis=3, concat_axis=0, tiled=True)  7.19 us
  transfers between devices with their start and end apart: 11, of which 7 were waited for; matrix products, arithmetic and copies ran while one was open for 9% of the time, Pallas kernels for 0%

profile of v4, /device:TPU:8, one launch (start us, length us, event | category | flops | bytes accessed | tf_op | source)
XLA Modules:
  0.0 329.8 jit_solution(4497897773677386160)
XLA Ops:
  7.2 0.0 copy-start
  7.2 0.0 reduce-scatter.3.cloned.1.call-start
  7.2 1.8 copy.43
  9.1 0.1 fusion.22
  9.2 1.6 collective-permute-start.1
  10.8 2.1 collective-permute-start.2
  12.9 0.7 collective-permute-start
  13.5 13.9 %collective-permute-done = bf16[96,256]{1,0:T(8,128)(2,1)S(1)} collective-permute-done((bf16[96,256]{1,0:T(8,128)(2,1)S(1)}, bf16[96,256]{1,0:T(8,128)(2,1)S(1)}, u32[]{:S(2)}, u32[]{:S(2)}) %collective-permute-start) | collective-permute-done | bytes 49184 | tf_op jit(solution)/shard_map/ppermute | solution.py:52
  27.5 13.6 %all_gather.6 = bf16[768,512]{1,0:T(8,128)(2,1)S(1)} all-gather(bf16[96,512]{1,0:T(8,128)(2,1)S(1)} %pad_maximum_fusion.1), channel_id=1, replica_groups=mesh['row'=8,'cx'=2,'cz'=8,'req'=2] {'row'}, dimensions={0}, use_global_device_ids=true | all-gather | bytes 884736 | tf_op jit(solution)/shard_map/all_gather | solution.py:54
  41.1 7.0 %fusion = f32[768,2688]{1,0:T(8,128)} fusion(bf16[768,512]{1,0:T(8,128)(2,1)S(1)} %all_gather.6, bf16[256,1344]{0,1:T(8,128)(2,1)} %collective-permute-done.2, bf16[256,1344]{0,1:T(8,128)(2,1)} %collective-permute-done.1, bf16[256,2688]{0,1:T(8,128)(2,1)S(1)} %copy.43), kind=kOutput, calls=%fused_computation.7 | convolution fusion | flops 2122186752 | bytes 11796480 | tf_op jit(solution)/shard_map/dot_general | solution.py:57
  48.1 0.0 reduce-scatter.3.cloned.1.call-update
  48.1 0.0 all-gather.2.cloned.1.call-start
  48.2 96.3 %reduce-scatter.3.cloned.1.call-done = f32[96,2688]{1,0:T(8,128)} async-done(((f32[768,2688]{1,0:T(8,128)}), f32[96,2688]{1,0:T(8,128)}) %reduce-scatter.3.cloned.1.call-update) | async-done | bytes 1032208 | tf_op jit(solution)/shard_map/reduce_scatter | solution.py:58
  144.4 2.1 multiply_convert_fusion
  146.5 0.0 all-gather.2.cloned.1.call-update
  146.5 0.0 reduce-scatter.5.cloned.1.call-start
  146.6 0.1 fusion.21
  146.7 1.6 collective-permute-start.3
  148.3 2.1 collective-permute-start.4
  150.3 13.7 %collective-permute-done.3 = bf16[1344,256]{1,0:T(8,128)(2,1)} collective-permute-done((bf16[1344,256]{1,0:T(8,128)(2,1)S(1)}, bf16[1344,256]{1,0:T(8,128)(2,1)}, u32[]{:S(2)}, u32[]{:S(2)}) %collective-permute-start.3) | collective-permute-done | bytes 688160 | tf_op jit(solution)/shard_map/ppermute | solution.py:18
  164.0 2.4 collective-permute-done.4
  166.4 33.2 %all-gather.2.cloned.1.call-done = bf16[768,2688]{1,0:T(8,128)(2,1)} async-done(((bf16[96,2688]{1,0:T(8,128)(2,1)}), bf16[768,2688]{1,0:T(8,128)(2,1)}) %all-gather.2.cloned.1.call-update) | async-done | bytes 4128784 | tf_op jit(solution)/shard_map/all_gather | solution.py:61
  199.6 6.1 %fusion.6 = f32[768,512]{1,0:T(8,128)} fusion(bf16[768,2688]{1,0:T(8,128)(2,1)} %all-gather.2.cloned.1.call-done, bf16[1344,256]{1,0:T(8,128)(2,1)} %collective-permute-done.4, bf16[1344,256]{1,0:T(8,128)(2,1)} %collective-permute-done.3, bf16[2688,256]{1,0:T(8,128)(2,1)S(1)} %copy-done.1), kind=kOutput, calls=%fused_computation.13 | convolution fusion | flops 2122186752 | bytes 8454144 | tf_op jit(solution)/shard_map/dot_general | solution.py:64
  205.7 0.0 reduce-scatter.5.cloned.1.call-update
  205.8 0.2 select_reduce_fusion.1
  206.0 0.1 select_reduce_fusion.2
  206.1 0.6 gather_fusion.1
  206.7 0.7 copy.44
  207.4 4.8 %gather_fusion = f32[8,8,64,128]{3,2,1,0:T(8,128)} fusion(f32[24,8,64,128]{3,2,1,0:T(8,128)} %bitcast.45, s32[1024]{0:T(1024)S(1)} %pad_clamp_fusion.2), kind=kCustom, calls=%fused_computation | custom fusion | bytes 4194336 | tf_op jit(solution)/shard_map/gather | solution.py:36
  212.2 2.0 pad_maximum_fusion
  214.3 4.4 %copy.45 = f32[8,1,8,64,131]{4,2,0,1,3:T(8,128)} copy(f32[8,1,8,64,131]{4,3,2,0,1:T(8,128)S(1)} %pad_maximum_fusion) | data formatting | bytes 4292608 | tf_op jit(solution)/shard_map/concatenate | solution.py:36
  218.7 5.1 %all-to-all-start = ((f32[8,1,8,64,131]{4,2,0,1,3:T(8,128)}), f32[8,1,8,64,131]{4,2,0,1,3:T(8,128)}, u32[]{:S(2)}, u32[]{:S(2)}) async-start(f32[8,1,8,64,131]{4,2,0,1,3:T(8,128)} %copy.45), calls=%async_computation.2 | async-start | bytes 8388608 | tf_op jit(solution)/shard_map/all_to_all | solution.py:37
  223.8 0.1 select_reduce_fusion
  223.9 0.7 gather_fusion.3
  224.6 0.7 gather_fusion.2
  225.3 50.5 %all-to-all-done = f32[8,1,8,64,131]{4,2,0,1,3:T(8,128)} async-done(((f32[8,1,8,64,131]{4,2,0,1,3:T(8,128)}), f32[8,1,8,64,131]{4,2,0,1,3:T(8,128)}, u32[]{:S(2)}, u32[]{:S(2)}) %all-to-all-start) | async-done | bytes 2146336 | tf_op jit(solution)/shard_map/all_to_all | solution.py:37
  275.8 4.6 %copy.52 = f32[8,1,8,64,131]{4,3,2,0,1:T(8,128)S(1)} copy(f32[8,1,8,64,131]{4,2,0,1,3:T(8,128)} %all-to-all-done) | data formatting | bytes 4292608 | tf_op jit(solution)/shard_map/all_to_all | solution.py:37
  280.4 2.6 copy.47
  283.0 4.2 %gather_fusion.4 = f32[32,8,8,131]{3,2,1,0:T(8,128)} fusion(f32[64,8,8,131]{3,2,1,0:T(8,128)} %bitcast.39, s32[1024]{0:T(1024)S(1)} %pad_clamp_fusion), kind=kCustom, calls=%fused_computation.4 | custom fusion | bytes 2146432 | tf_op jit(solution)/shard_map/gather | solution.py:39
  287.2 4.2 %all-to-all-start.1 = ((f32[32,1,8,8,131]{4,3,2,1,0:T(8,128)}), f32[32,1,8,8,131]{4,3,2,1,0:T(8,128)S(1)}, u32[]{:S(2)}, u32[]{:S(2)}) async-start(f32[32,1,8,8,131]{4,3,2,1,0:T(8,128)} %bitcast.42), calls=%async_computation.3 | async-start | bytes 4194304 | tf_op jit(solution)/shard_map/all_to_all | solution.py:40
  291.4 1.6 fusion.23
  293.1 1.0 collective-permute-start.5
  294.1 24.7 %all-to-all-done.1 = f32[32,1,8,8,131]{4,3,2,1,0:T(8,128)S(1)} async-done(((f32[32,1,8,8,131]{4,3,2,1,0:T(8,128)}), f32[32,1,8,8,131]{4,3,2,1,0:T(8,128)S(1)}, u32[]{:S(2)}, u32[]{:S(2)}) %all-to-all-start.1) | async-done | bytes 1073184 | tf_op jit(solution)/shard_map/all_to_all | solution.py:40
  318.8 0.1 slice.28
  318.9 0.1 slice.29
  319.0 1.1 copy.49
  320.1 1.5 copy.50
  321.6 1.6 fusion.13
  (25 shorter events, 0.1 us)
Async XLA Ops:
  7.2 199.0 %copy-start = (f32[24,1,8,64,3]{3,2,4,1,0:T(8,128)S(1)}, f32[24,1,8,64,3]{3,2,4,1,0:T(8,128)}, u32[]{:S(2)}) copy-start(f32[24,1,8,64,3]{3,2,4,1,0:T(8,128)} %param.11) | copy-start | bytes 442372
  7.2 5.7 %copy-start.2 = (bf16[192,256]{1,0:T(8,128)(2,1)S(1)}, bf16[192,256]{1,0:T(8,128)(2,1)}, u32[]{:S(2)}) copy-start(bf16[192,256]{1,0:T(8,128)(2,1)} %param.7) | copy-start | bytes 294916
  7.2 137.2 %reduce-scatter.3.cloned.1.call-start = ((), (), s32[]{:S(2)}) async-start(), calls=%async_computation.4 | async-start | bytes 9289728 | tf_op jit(solution)/shard_map/reduce_scatter | solution.py:58
  9.2 32.0 %collective-permute-start.1 = (bf16[256,1344]{0,1:T(8,128)(2,1)S(1)}, bf16[256,1344]{0,1:T(8,128)(2,1)}, u32[]{:S(2)}, u32[]{:S(2)}) collective-permute-start(bf16[256,1344]{0,1:T(8,128)(2,1)S(1)} %get-tuple-element.28), channel_id=1, source_target_pairs={{0,16},{16,0},{1,17},{17,1},{2,18},{18,2},{3,19},{19,3},{4,20},{20... | collective-permute-start | bytes 2064392 | tf_op jit(solution)/shard_map/ppermute | solution.py:18
  10.8 30.4 %collective-permute-start.2 = (bf16[256,1344]{0,1:T(8,128)(2,1)S(1)}, bf16[256,1344]{0,1:T(8,128)(2,1)}, u32[]{:S(2)}, u32[]{:S(2)}) collective-permute-start(bf16[256,1344]{0,1:T(8,128)(2,1)S(1)} %get-tuple-element.29), channel_id=1, source_target_pairs={{0,17},{17,0},{1,16},{16,1},{2,19},{19,2},{3,18},{18,3},{4,21},{21... | collective-permute-start | bytes 2064392 | tf_op jit(solution)/shard_map/ppermute | solution.py:18
  12.9 14.6 %collective-permute-start = (bf16[96,256]{1,0:T(8,128)(2,1)S(1)}, bf16[96,256]{1,0:T(8,128)(2,1)S(1)}, u32[]{:S(2)}, u32[]{:S(2)}) collective-permute-start(bf16[96,256]{1,0:T(8,128)(2,1)S(1)} %get-tuple-element.33), channel_id=1, source_target_pairs={{0,16},{16,0},{1,17},{17,1},{2,18},{18,2},{3,19},{19,3},{4,20},{20... | collective-permute-start | bytes 147464 | tf_op jit(solution)/shard_map/ppermute | solution.py:52
  48.1 98.5 %copy-start.1 = (bf16[2688,256]{1,0:T(8,128)(2,1)S(1)}, bf16[2688,256]{1,0:T(8,128)(2,1)}, u32[]{:S(2)}) copy-start(bf16[2688,256]{1,0:T(8,128)(2,1)} %param.9) | copy-start | bytes 4128772
  48.1 151.5 %all-gather.2.cloned.1.call-start = ((), (), s32[]{:S(2)}) async-start(), calls=%async_computation.5 | async-start | bytes 4644864 | tf_op jit(solution)/shard_map/all_gather | solution.py:61
  146.5 144.9 %reduce-scatter.5.cloned.1.call-start = ((), (), s32[]{:S(2)}) async-start(), calls=%async_computation.6 | async-start | bytes 1769472 | tf_op jit(solution)/shard_map/reduce_scatter | solution.py:65
  146.7 17.3 %collective-permute-start.3 = (bf16[1344,256]{1,0:T(8,128)(2,1)S(1)}, bf16[1344,256]{1,0:T(8,128)(2,1)}, u32[]{:S(2)}, u32[]{:S(2)}) collective-permute-start(bf16[1344,256]{1,0:T(8,128)(2,1)S(1)} %get-tuple-element.26), channel_id=1, source_target_pairs={{0,16},{16,0},{1,17},{17,1},{2,18},{18,2},{3,19},{19,3},{4,20},{20... | collective-permute-start | bytes 2064392 | tf_op jit(solution)/shard_map/ppermute | solution.py:18
  148.3 18.1 %collective-permute-start.4 = (bf16[1344,256]{1,0:T(8,128)(2,1)S(1)}, bf16[1344,256]{1,0:T(8,128)(2,1)}, u32[]{:S(2)}, u32[]{:S(2)}) collective-permute-start(bf16[1344,256]{1,0:T(8,128)(2,1)S(1)} %get-tuple-element.27), channel_id=1, source_target_pairs={{0,17},{17,0},{1,16},{16,1},{2,19},{19,2},{3,18},{18,3},{4,21},{21... | collective-permute-start | bytes 2064392 | tf_op jit(solution)/shard_map/ppermute | solution.py:18
  150.3 55.4 %copy-start.4 = (s32[32]{0:T(128)S(1)}, s32[32]{0:T(128)}, u32[]{:S(2)}) copy-start(s32[32]{0:T(128)} %param.12) | copy-start | bytes 388
  218.7 5.1 %copy-start.5 = (s32[32]{0:T(128)S(1)}, s32[32]{0:T(128)}, u32[]{:S(2)}) copy-start(s32[32]{0:T(128)} %param.13) | copy-start | bytes 388
  218.7 57.1 %all-to-all-start = ((f32[8,1,8,64,131]{4,2,0,1,3:T(8,128)}), f32[8,1,8,64,131]{4,2,0,1,3:T(8,128)}, u32[]{:S(2)}, u32[]{:S(2)}) async-start(f32[8,1,8,64,131]{4,2,0,1,3:T(8,128)} %copy.45), calls=%async_computation.2 | async-start | bytes 8388608 | tf_op jit(solution)/shard_map/all_to_all | solution.py:37
  287.2 31.6 %all-to-all-start.1 = ((f32[32,1,8,8,131]{4,3,2,1,0:T(8,128)}), f32[32,1,8,8,131]{4,3,2,1,0:T(8,128)S(1)}, u32[]{:S(2)}, u32[]{:S(2)}) async-start(f32[32,1,8,8,131]{4,3,2,1,0:T(8,128)} %bitcast.42), calls=%async_computation.3 | async-start | bytes 4194304 | tf_op jit(solution)/shard_map/all_to_all | solution.py:40
  293.1 28.6 %collective-permute-start.5 = (f32[96,256]{1,0:T(8,128)}, f32[96,256]{1,0:T(8,128)}, u32[]{:S(2)}, u32[]{:S(2)}) collective-permute-start(f32[96,256]{1,0:T(8,128)} %get-tuple-element.31), channel_id=1, source_target_pairs={{0,16},{16,0},{1,17},{17,1},{2,18},{18,2},{3,19},{19,3},{4,20},{20... | collective-permute-start | bytes 294920 | tf_op jit(solution)/shard_map/ppermute | solution.py:67
  319.0 2.7 copy-start.3
Sparse Core Ops, SparseCore 0:
  48.2 96.1 reduce-scatter.2
  146.8 52.7 all-gather.1
  205.9 36.9 reduce-scatter.4

commit v5 on v4

--- a/solution.py
+++ b/solution.py
@@ -42,6 +42,27 @@
     return both[..., :n], both[..., n:]
 
 
+def gather_row(x):
+    n = lax.axis_size("row")
+    r = lax.axis_index("row")
+    got = [x] + [
+        lax.ppermute(x, "row", [(j, (j + s) % n) for j in range(n)]) for s in range(1, n)
+    ]
+    ahead = jnp.stack([got[(-t) % n] for t in range(n)])
+    return jnp.roll(ahead, r, axis=0).reshape(n * x.shape[0], *x.shape[1:])
+
+
+def scatter_row(x):
+    n = lax.axis_size("row")
+    r = lax.axis_index("row")
+    blocks = x.reshape(n, x.shape[0] // n, *x.shape[1:])
+    total = lax.dynamic_index_in_dim(blocks, r, 0, keepdims=False)
+    for s in range(1, n):
+        part = lax.dynamic_index_in_dim(blocks, (r + s) % n, 0, keepdims=False)
+        total = total + lax.ppermute(part, "row", [(j, (j + s) % n) for j in range(n)])
+    return total
+
+
 def ffn(tokens, up_weight, down_weight):
     i = lax.axis_index("cx")
     block, width = tokens.shape
@@ -51,7 +72,7 @@
     theirs = lax.dynamic_index_in_dim(halves, 1 - i, 0, keepdims=False)
     recv = lax.ppermute(theirs, "cx", SWAP)
     xa = jnp.concatenate([mine, recv], axis=1)
-    xg = lax.all_gather(xa, "row", axis=0, tiled=True)
+    xg = gather_row(xa)
     w1p = fetch_partner(up_weight, 1)
     w1 = jnp.concatenate([up_weight, w1p], axis=0)
     partial = jnp.dot(xg, w1, preferred_element_type=jnp.float32)
@@ -62,7 +83,7 @@
     w2p = fetch_partner(down_weight, 0)
     w2 = jnp.concatenate([down_weight, w2p], axis=1)
     products = jnp.dot(hg, w2, preferred_element_type=jnp.float32)
-    summed = lax.psum_scatter(products, "row", scatter_dimension=0, tiled=True)
+    summed = scatter_row(products)
     own = summed[:, :width]
     other = lax.ppermute(summed[:, width:], "cx", SWAP)
     full = jnp.where(i == 0, jnp.concatenate([own, other], 0), jnp.concatenate([other, own], 0))

time: 331 us -> 269 us (0.81)
  waiting for transfers between devices: 235 us -> 160 us
  starting transfers between devices: 18.5 us -> 39.9 us
  blocking collectives: 13.6 us -> 0 us
    all_to_all x1, waiting for transfers between devices: 50.5 us -> 0.01 us  [handover(): lax.all_to_all(picked, 'row', split_axis=3, concat_axis=0, tiled=True)]
    ppermute x0 -> x14, starting transfers between devices: none -> 20.7 us  [the longest x7 13.5 us: scatter_row(): lax.ppermute(part, 'row', [(j, (j + s) % n) for j in range(n)])]
    all_gather x1, waiting for transfers between devices: 33.2 us -> 13.3 us  [ffn(): hg = lax.all_gather(hidden, 'cz', axis=0, tiled=True)]
    ppermute x1, waiting for transfers between devices: 13.9 us -> 0.01 us  [ffn(): recv = lax.ppermute(theirs, 'cx', SWAP)]
    ppermute x0 -> x14, waiting for transfers between devices: none -> 13.7 us  [the longest x7 8.51 us: gather_row(): lax.ppermute(x, 'row', [(j, (j + s) % n) for j in range(n)])]
    all_gather x1 -> x0, blocking collectives: 13.6 us -> none  [ffn(): xg = lax.all_gather(xa, 'row', axis=0, tiled=True)]
    all_to_all x1, waiting for transfers between devices: 24.7 us -> 20.9 us  [handover(): both = lax.all_to_all(rows, 'req', split_axis=0, concat_axis=1, tiled=True)]
  transfers between devices with their start and end apart: 11 -> 24, of which waited for: 7 -> 12; matrix products, arithmetic and copies ran while one was open for 9% -> 14% of each run, Pallas kernels for 0% -> 0%
where the time goes in v5:
time: 269 us; the launch traced here: 266 us
  waiting for transfers between devices  160 us (59%)
  starting transfers between devices  39.9 us (15%)
  local copies, waits for them, and re-layouts  31.9 us (12%)
  between operations  14.4 us (5%)
  matrix products  11.9 us (4%)
  other arithmetic  7.81 us (3%)
    reduce_scatter x1, waiting for transfers between devices, ffn(): preact = lax.psum_scatter(partial, 'cz', scatter_dimension=0, tiled=True)  95.3 us
    all_to_all x1, waiting for transfers between devices, handover(): both = lax.all_to_all(rows, 'req', split_axis=0, concat_axis=1, tiled=True)  20.9 us
    ppermute x2, waiting for transfers between devices, fetch_partner(): lax.ppermute(near, 'cx', SWAP)  14 us
    ppermute x7, starting transfers between devices, scatter_row(): lax.ppermute(part, 'row', [(j, (j + s) % n) for j in range(n)])  13.5 us
    all_gather x1, waiting for transfers between devices, ffn(): hg = lax.all_gather(hidden, 'cz', axis=0, tiled=True)  13.3 us
    ppermute x7, waiting for transfers between devices, gather_row(): lax.ppermute(x, 'row', [(j, (j + s) % n) for j in range(n)])  8.51 us
    ppermute x7, starting transfers between devices, gather_row(): lax.ppermute(x, 'row', [(j, (j + s) % n) for j in range(n)])  7.26 us
    all_to_all x2, local copies, waits for them, and re-layouts, handover(): lax.all_to_all(picked, 'row', split_axis=3, concat_axis=0, tiled=True)  7.19 us
  transfers between devices with their start and end apart: 24, of which 12 were waited for; matrix products, arithmetic and copies ran while one was open for 14% of the time, Pallas kernels for 0%

profile of v5, /device:TPU:8, one launch (start us, length us, event | category | flops | bytes accessed | tf_op | source)
XLA Modules:
  0.0 265.5 jit_solution(408125374881988652)
XLA Ops:
  7.2 0.9 dynamic-slice_bitcast_fusion.8
  8.1 1.6 collective-permute-start
  9.7 1.8 copy.43
  12.2 2.8 %collective-permute-start.9 = (bf16[256,1344]{0,1:T(8,128)(2,1)S(1)}, bf16[256,1344]{0,1:T(8,128)(2,1)}, u32[]{:S(2)}, u32[]{:S(2)}) collective-permute-start(bf16[256,1344]{0,1:T(8,128)(2,1)S(1)} %get-tuple-element.36), channel_id=1, source_target_pairs={{0,17},{17,0},{1,16},{16,1},{2,19},{19,2},{3,18},{18,3},{4,21},{21... | collective-permute-start | bytes 2064392 | tf_op jit(solution)/shard_map/ppermute | solution.py:18
  15.0 2.0 collective-permute-start.2
  17.0 0.8 collective-permute-start.3
  18.2 2.0 collective-permute-start.4
  20.2 2.1 collective-permute-done.2
  22.3 1.7 collective-permute-start.6
  24.0 1.7 collective-permute-done.4
  25.7 0.7 collective-permute-start.7
  26.4 1.4 collective-permute-done.5
  27.8 1.1 collective-permute-done.6
  29.0 1.8 collective-permute-done.7
  31.0 7.0 %fusion = f32[768,2688]{1,0:T(8,128)} fusion(bf16[768,512]{1,0:T(8,128)(2,1)S(1)} %bitcast.101, bf16[256,1344]{0,1:T(8,128)(2,1)} %collective-permute-done.9, bf16[256,1344]{0,1:T(8,128)(2,1)} %collective-permute-done.8, bf16[256,2688]{0,1:T(8,128)(2,1)S(1)} %copy.43), kind=kOutput, calls=%fused_computation.7 | convolution fusion | flops 2122186752 | bytes 11796480 | tf_op jit(solution)/shard_map/dot_general | solution.py:78
  38.3 95.3 %reduce-scatter.2.cloned.1.call-done = f32[96,2688]{1,0:T(8,128)} async-done(((f32[768,2688]{1,0:T(8,128)}), f32[96,2688]{1,0:T(8,128)}) %reduce-scatter.2.cloned.1.call-update) | async-done | bytes 1032208 | tf_op jit(solution)/shard_map/reduce_scatter | solution.py:79
  133.6 2.1 multiply_convert_fusion
  135.9 0.7 gather_fusion.2
  136.7 0.7 gather_fusion.3
  138.2 0.7 copy.44
  138.9 4.8 %gather_fusion = f32[8,8,64,128]{3,2,1,0:T(8,128)} fusion(f32[24,8,64,128]{3,2,1,0:T(8,128)} %bitcast.102, s32[1024]{0:T(1024)S(1)} %get-tuple-element.42), kind=kCustom, calls=%fused_computation | custom fusion | bytes 4194336 | tf_op jit(solution)/shard_map/gather | solution.py:36
  143.7 2.1 pad_maximum_fusion
  145.8 4.5 %copy.45 = f32[8,1,8,64,131]{4,2,0,1,3:T(8,128)} copy(f32[8,1,8,64,131]{4,3,2,0,1:T(8,128)S(1)} %pad_maximum_fusion) | data formatting | bytes 4292608 | tf_op jit(solution)/shard_map/concatenate | solution.py:36
  150.2 5.1 %all-to-all-start = ((f32[8,1,8,64,131]{4,2,0,1,3:T(8,128)}), f32[8,1,8,64,131]{4,2,0,1,3:T(8,128)}, u32[]{:S(2)}, u32[]{:S(2)}) async-start(f32[8,1,8,64,131]{4,2,0,1,3:T(8,128)} %copy.45), calls=%async_computation.1 | async-start | bytes 8388608 | tf_op jit(solution)/shard_map/all_to_all | solution.py:37
  155.4 1.5 collective-permute-start.10
  157.0 2.1 collective-permute-start.11
  159.1 14.0 %collective-permute-done.10 = bf16[1344,256]{1,0:T(8,128)(2,1)} collective-permute-done((bf16[1344,256]{1,0:T(8,128)(2,1)S(1)}, bf16[1344,256]{1,0:T(8,128)(2,1)}, u32[]{:S(2)}, u32[]{:S(2)}) %collective-permute-start.10) | collective-permute-done | bytes 688160 | tf_op jit(solution)/shard_map/ppermute | solution.py:18
  173.1 2.4 collective-permute-done.11
  175.5 13.3 %all-gather.2.cloned.1.call-done = bf16[768,2688]{1,0:T(8,128)(2,1)} async-done(((bf16[96,2688]{1,0:T(8,128)(2,1)}), bf16[768,2688]{1,0:T(8,128)(2,1)}) %all-gather.2.cloned.1.call-update) | async-done | bytes 4128784 | tf_op jit(solution)/shard_map/all_gather | solution.py:82
  188.8 4.9 %fusion.6 = f32[768,512]{1,0:T(8,128)S(1)} fusion(bf16[768,2688]{1,0:T(8,128)(2,1)} %all-gather.2.cloned.1.call-done, bf16[1344,256]{1,0:T(8,128)(2,1)} %collective-permute-done.11, bf16[1344,256]{1,0:T(8,128)(2,1)} %collective-permute-done.10, bf16[2688,256]{1,0:T(8,128)(2,1)S(1)} %copy-done.3), kind=kOutput, calls=%fused_computation.13 | convolution fusion | flops 2122186752 | bytes 8454144 | tf_op jit(solution)/shard_map/dot_general | solution.py:85
  193.7 1.2 copy-done.2
  195.1 1.6 collective-permute-start.13
  196.6 1.0 collective-permute-start.14
  197.6 2.4 collective-permute-start.15
  200.7 5.1 %collective-permute-done.12 = f32[96,512]{1,0:T(8,128)S(1)} collective-permute-done((f32[96,512]{1,0:T(8,128)S(1)}, f32[96,512]{1,0:T(8,128)S(1)}, u32[]{:S(2)}, u32[]{:S(2)}) %collective-permute-start.12) | collective-permute-done | bytes 196640 | tf_op jit(solution)/shard_map/ppermute | solution.py:62
  205.9 3.3 %collective-permute-start.17 = (f32[96,512]{1,0:T(8,128)S(1)}, f32[96,512]{1,0:T(8,128)}, u32[]{:S(2)}, u32[]{:S(2)}) collective-permute-start(f32[96,512]{1,0:T(8,128)S(1)} %get-tuple-element.28), channel_id=1, source_target_pairs={{0,192},{32,224},{64,0},{96,32},{128,64},{160,96},{192,128},{224,1... | collective-permute-start | bytes 589832 | tf_op jit(solution)/shard_map/ppermute | solution.py:62
  209.2 0.7 copy-done.5
  209.8 4.5 %collective-permute-start.18 = (f32[96,512]{1,0:T(8,128)S(1)}, f32[96,512]{1,0:T(8,128)}, u32[]{:S(2)}, u32[]{:S(2)}) collective-permute-start(f32[96,512]{1,0:T(8,128)S(1)} %get-tuple-element.27), channel_id=1, source_target_pairs={{0,224},{32,0},{64,32},{96,64},{128,96},{160,128},{192,160},{224,1... | collective-permute-start | bytes 589832 | tf_op jit(solution)/shard_map/ppermute | solution.py:62
  214.3 4.6 %copy.52 = f32[8,1,8,64,131]{4,3,2,0,1:T(8,128)S(1)} copy(f32[8,1,8,64,131]{4,2,0,1,3:T(8,128)} %all-to-all-done) | data formatting | bytes 4292608 | tf_op jit(solution)/shard_map/all_to_all | solution.py:37
  219.0 2.6 copy.47
  221.5 4.2 %gather_fusion.4 = f32[32,8,8,131]{3,2,1,0:T(8,128)} fusion(f32[64,8,8,131]{3,2,1,0:T(8,128)} %bitcast.93, s32[1024]{0:T(1024)S(1)} %get-tuple-element.41), kind=kCustom, calls=%fused_computation.4 | custom fusion | bytes 2146432 | tf_op jit(solution)/shard_map/gather | solution.py:39
  225.8 4.2 %all-to-all-start.1 = ((f32[32,1,8,8,131]{4,3,2,1,0:T(8,128)}), f32[32,1,8,8,131]{4,3,2,1,0:T(8,128)S(1)}, u32[]{:S(2)}, u32[]{:S(2)}) async-start(f32[32,1,8,8,131]{4,3,2,1,0:T(8,128)} %bitcast.96), calls=%async_computation.2 | async-start | bytes 4194304 | tf_op jit(solution)/shard_map/all_to_all | solution.py:40
  230.0 1.5 fusion.19
  232.2 1.0 collective-permute-start.19
  233.3 20.9 %all-to-all-done.1 = f32[32,1,8,8,131]{4,3,2,1,0:T(8,128)S(1)} async-done(((f32[32,1,8,8,131]{4,3,2,1,0:T(8,128)}), f32[32,1,8,8,131]{4,3,2,1,0:T(8,128)S(1)}, u32[]{:S(2)}, u32[]{:S(2)}) %all-to-all-start.1) | async-done | bytes 1073184 | tf_op jit(solution)/shard_map/all_to_all | solution.py:40
  254.4 1.1 copy.49
  255.5 1.5 copy.50
  257.0 1.6 fusion.13
  (71 shorter events, 4.3 us)
Async XLA Ops:
  7.2 130.4 %copy-start = (f32[24,1,8,64,3]{3,2,4,1,0:T(8,128)S(1)}, f32[24,1,8,64,3]{3,2,4,1,0:T(8,128)}, u32[]{:S(2)}) copy-start(f32[24,1,8,64,3]{3,2,4,1,0:T(8,128)} %param.11) | copy-start | bytes 442372
  7.2 126.4 %reduce-scatter.2.cloned.1.call-start = ((), (), s32[]{:S(2)}) async-start(), calls=%async_computation.3 | async-start | bytes 9289728 | tf_op jit(solution)/shard_map/reduce_scatter | solution.py:79
  8.1 6.8 %collective-permute-start = (bf16[96,256]{1,0:T(8,128)(2,1)S(1)}, bf16[96,256]{1,0:T(8,128)(2,1)S(1)}, u32[]{:S(2)}, u32[]{:S(2)}) collective-permute-start(bf16[96,256]{1,0:T(8,128)(2,1)S(1)} %get-tuple-element.40), channel_id=1, source_target_pairs={{0,16},{16,0},{1,17},{17,1},{2,18},{18,2},{3,19},{19,3},{4,20},{20... | collective-permute-start | bytes 147464 | tf_op jit(solution)/shard_map/ppermute | solution.py:73
  11.6 19.5 %collective-permute-start.8 = (bf16[256,1344]{0,1:T(8,128)(2,1)S(1)}, bf16[256,1344]{0,1:T(8,128)(2,1)}, u32[]{:S(2)}, u32[]{:S(2)}) collective-permute-start(bf16[256,1344]{0,1:T(8,128)(2,1)S(1)} %get-tuple-element.35), channel_id=1, source_target_pairs={{0,16},{16,0},{1,17},{17,1},{2,18},{18,2},{3,19},{19,3},{4,20},{20... | collective-permute-start | bytes 2064392 | tf_op jit(solution)/shard_map/ppermute | solution.py:18
  12.2 18.9 %collective-permute-start.9 = (bf16[256,1344]{0,1:T(8,128)(2,1)S(1)}, bf16[256,1344]{0,1:T(8,128)(2,1)}, u32[]{:S(2)}, u32[]{:S(2)}) collective-permute-start(bf16[256,1344]{0,1:T(8,128)(2,1)S(1)} %get-tuple-element.36), channel_id=1, source_target_pairs={{0,17},{17,0},{1,16},{16,1},{2,19},{19,2},{3,18},{18,3},{4,21},{21... | collective-permute-start | bytes 2064392 | tf_op jit(solution)/shard_map/ppermute | solution.py:18
  15.0 3.2 %collective-permute-start.1 = (bf16[96,512]{1,0:T(8,128)(2,1)S(1)}, bf16[96,512]{1,0:T(8,128)(2,1)S(1)}, u32[]{:S(2)}, u32[]{:S(2)}) collective-permute-start(bf16[96,512]{1,0:T(8,128)(2,1)S(1)} %pad_maximum_fusion.1), channel_id=1, source_target_pairs={{0,224},{32,0},{64,32},{96,64},{128,96},{160,128},{192,160},{224,1... | collective-permute-start | bytes 294920 | tf_op jit(solution)/shard_map/ppermute | solution.py:49
  15.0 7.3 %collective-permute-start.2 = (bf16[96,512]{1,0:T(8,128)(2,1)S(1)}, bf16[96,512]{1,0:T(8,128)(2,1)S(1)}, u32[]{:S(2)}, u32[]{:S(2)}) collective-permute-start(bf16[96,512]{1,0:T(8,128)(2,1)S(1)} %pad_maximum_fusion.1), channel_id=1, source_target_pairs={{0,192},{32,224},{64,0},{96,32},{128,64},{160,96},{192,128},{224,1... | collective-permute-start | bytes 294920 | tf_op jit(solution)/shard_map/ppermute | solution.py:49
  17.0 5.3 %collective-permute-start.3 = (bf16[96,512]{1,0:T(8,128)(2,1)S(1)}, bf16[96,512]{1,0:T(8,128)(2,1)S(1)}, u32[]{:S(2)}, u32[]{:S(2)}) collective-permute-start(bf16[96,512]{1,0:T(8,128)(2,1)S(1)} %pad_maximum_fusion.1), channel_id=1, source_target_pairs={{0,160},{32,192},{64,224},{96,0},{128,32},{160,64},{192,96},{224,1... | collective-permute-start | bytes 294920 | tf_op jit(solution)/shard_map/ppermute | solution.py:49
  18.2 7.6 %collective-permute-start.4 = (bf16[96,512]{1,0:T(8,128)(2,1)S(1)}, bf16[96,512]{1,0:T(8,128)(2,1)S(1)}, u32[]{:S(2)}, u32[]{:S(2)}) collective-permute-start(bf16[96,512]{1,0:T(8,128)(2,1)S(1)} %pad_maximum_fusion.1), channel_id=1, source_target_pairs={{0,128},{32,160},{64,192},{96,224},{128,0},{160,32},{192,64},{224,... | collective-permute-start | bytes 294920 | tf_op jit(solution)/shard_map/ppermute | solution.py:49
  22.3 5.5 %collective-permute-start.5 = (bf16[96,512]{1,0:T(8,128)(2,1)S(1)}, bf16[96,512]{1,0:T(8,128)(2,1)S(1)}, u32[]{:S(2)}, u32[]{:S(2)}) collective-permute-start(bf16[96,512]{1,0:T(8,128)(2,1)S(1)} %pad_maximum_fusion.1), channel_id=1, source_target_pairs={{0,96},{32,128},{64,160},{96,192},{128,224},{160,0},{192,32},{224,... | collective-permute-start | bytes 294920 | tf_op jit(solution)/shard_map/ppermute | solution.py:49
  22.3 6.7 %collective-permute-start.6 = (bf16[96,512]{1,0:T(8,128)(2,1)S(1)}, bf16[96,512]{1,0:T(8,128)(2,1)S(1)}, u32[]{:S(2)}, u32[]{:S(2)}) collective-permute-start(bf16[96,512]{1,0:T(8,128)(2,1)S(1)} %pad_maximum_fusion.1), channel_id=1, source_target_pairs={{0,64},{32,96},{64,128},{96,160},{128,192},{160,224},{192,0},{224,... | collective-permute-start | bytes 294920 | tf_op jit(solution)/shard_map/ppermute | solution.py:49
  25.7 5.1 %collective-permute-start.7 = (bf16[96,512]{1,0:T(8,128)(2,1)S(1)}, bf16[96,512]{1,0:T(8,128)(2,1)S(1)}, u32[]{:S(2)}, u32[]{:S(2)}) collective-permute-start(bf16[96,512]{1,0:T(8,128)(2,1)S(1)} %pad_maximum_fusion.1), channel_id=1, source_target_pairs={{0,32},{32,64},{64,96},{96,128},{128,160},{160,192},{192,224},{224... | collective-permute-start | bytes 294920 | tf_op jit(solution)/shard_map/ppermute | solution.py:49
  38.0 97.6 %copy-start.7 = (s32[32]{0:T(128)S(1)}, s32[32]{0:T(128)}, u32[]{:S(2)}) copy-start(s32[32]{0:T(128)} %param.13) | copy-start | bytes 388
  38.1 97.8 %copy-start.6 = (s32[32]{0:T(128)S(1)}, s32[32]{0:T(128)}, u32[]{:S(2)}) copy-start(s32[32]{0:T(128)} %param.12) | copy-start | bytes 388
  38.1 150.7 %all-gather.2.cloned.1.call-start = ((), (), s32[]{:S(2)}) async-start(), calls=%async_computation.4 | async-start | bytes 4644864 | tf_op jit(solution)/shard_map/all_gather | solution.py:82
  150.2 5.1 %copy-start.3 = (bf16[2688,256]{1,0:T(8,128)(2,1)S(1)}, bf16[2688,256]{1,0:T(8,128)(2,1)}, u32[]{:S(2)}) copy-start(bf16[2688,256]{1,0:T(8,128)(2,1)} %param.9) | copy-start | bytes 4128772
  150.2 64.1 %all-to-all-start = ((f32[8,1,8,64,131]{4,2,0,1,3:T(8,128)}), f32[8,1,8,64,131]{4,2,0,1,3:T(8,128)}, u32[]{:S(2)}, u32[]{:S(2)}) async-start(f32[8,1,8,64,131]{4,2,0,1,3:T(8,128)} %copy.45), calls=%async_computation.1 | async-start | bytes 8388608 | tf_op jit(solution)/shard_map/all_to_all | solution.py:37
  155.4 17.7 %collective-permute-start.10 = (bf16[1344,256]{1,0:T(8,128)(2,1)S(1)}, bf16[1344,256]{1,0:T(8,128)(2,1)}, u32[]{:S(2)}, u32[]{:S(2)}) collective-permute-start(bf16[1344,256]{1,0:T(8,128)(2,1)S(1)} %get-tuple-element.33), channel_id=1, source_target_pairs={{0,16},{16,0},{1,17},{17,1},{2,18},{18,2},{3,19},{19,3},{4,20},{20... | collective-permute-start | bytes 2064392 | tf_op jit(solution)/shard_map/ppermute | solution.py:18
  157.0 18.5 %collective-permute-start.11 = (bf16[1344,256]{1,0:T(8,128)(2,1)S(1)}, bf16[1344,256]{1,0:T(8,128)(2,1)}, u32[]{:S(2)}, u32[]{:S(2)}) collective-permute-start(bf16[1344,256]{1,0:T(8,128)(2,1)S(1)} %get-tuple-element.34), channel_id=1, source_target_pairs={{0,17},{17,0},{1,16},{16,1},{2,19},{19,2},{3,18},{18,3},{4,21},{21... | collective-permute-start | bytes 2064392 | tf_op jit(solution)/shard_map/ppermute | solution.py:18
  193.7 1.2 copy-start.2
  195.0 10.8 %collective-permute-start.12 = (f32[96,512]{1,0:T(8,128)S(1)}, f32[96,512]{1,0:T(8,128)S(1)}, u32[]{:S(2)}, u32[]{:S(2)}) collective-permute-start(f32[96,512]{1,0:T(8,128)S(1)} %get-tuple-element.26), channel_id=1, source_target_pairs={{0,32},{32,64},{64,96},{96,128},{128,160},{160,192},{192,224},{224... | collective-permute-start | bytes 589832 | tf_op jit(solution)/shard_map/ppermute | solution.py:62
  195.1 14.1 %collective-permute-start.13 = (f32[96,512]{1,0:T(8,128)S(1)}, f32[96,512]{1,0:T(8,128)S(1)}, u32[]{:S(2)}, u32[]{:S(2)}) collective-permute-start(f32[96,512]{1,0:T(8,128)S(1)} %get-tuple-element.32), channel_id=1, source_target_pairs={{0,64},{32,96},{64,128},{96,160},{128,192},{160,224},{192,0},{224,... | collective-permute-start | bytes 589832 | tf_op jit(solution)/shard_map/ppermute | solution.py:62
  196.6 33.4 %collective-permute-start.14 = (f32[96,512]{1,0:T(8,128)S(1)}, f32[96,512]{1,0:T(8,128)}, u32[]{:S(2)}, u32[]{:S(2)}) collective-permute-start(f32[96,512]{1,0:T(8,128)S(1)} %get-tuple-element.31), channel_id=1, source_target_pairs={{0,96},{32,128},{64,160},{96,192},{128,224},{160,0},{192,32},{224,... | collective-permute-start | bytes 589832 | tf_op jit(solution)/shard_map/ppermute | solution.py:62
  197.6 32.4 %collective-permute-start.15 = (f32[96,512]{1,0:T(8,128)S(1)}, f32[96,512]{1,0:T(8,128)}, u32[]{:S(2)}, u32[]{:S(2)}) collective-permute-start(f32[96,512]{1,0:T(8,128)S(1)} %get-tuple-element.30), channel_id=1, source_target_pairs={{0,128},{32,160},{64,192},{96,224},{128,0},{160,32},{192,64},{224,... | collective-permute-start | bytes 589832 | tf_op jit(solution)/shard_map/ppermute | solution.py:62
  200.1 30.0 %collective-permute-start.16 = (f32[96,512]{1,0:T(8,128)S(1)}, f32[96,512]{1,0:T(8,128)}, u32[]{:S(2)}, u32[]{:S(2)}) collective-permute-start(f32[96,512]{1,0:T(8,128)S(1)} %get-tuple-element.29), channel_id=1, source_target_pairs={{0,160},{32,192},{64,224},{96,0},{128,32},{160,64},{192,96},{224,1... | collective-permute-start | bytes 589832 | tf_op jit(solution)/shard_map/ppermute | solution.py:62
  205.9 24.2 %collective-permute-start.17 = (f32[96,512]{1,0:T(8,128)S(1)}, f32[96,512]{1,0:T(8,128)}, u32[]{:S(2)}, u32[]{:S(2)}) collective-permute-start(f32[96,512]{1,0:T(8,128)S(1)} %get-tuple-element.28), channel_id=1, source_target_pairs={{0,192},{32,224},{64,0},{96,32},{128,64},{160,96},{192,128},{224,1... | collective-permute-start | bytes 589832 | tf_op jit(solution)/shard_map/ppermute | solution.py:62
  209.2 0.7 copy-start.5
  209.8 20.2 %collective-permute-start.18 = (f32[96,512]{1,0:T(8,128)S(1)}, f32[96,512]{1,0:T(8,128)}, u32[]{:S(2)}, u32[]{:S(2)}) collective-permute-start(f32[96,512]{1,0:T(8,128)S(1)} %get-tuple-element.27), channel_id=1, source_target_pairs={{0,224},{32,0},{64,32},{96,64},{128,96},{160,128},{192,160},{224,1... | collective-permute-start | bytes 589832 | tf_op jit(solution)/shard_map/ppermute | solution.py:62
  225.8 28.4 %all-to-all-start.1 = ((f32[32,1,8,8,131]{4,3,2,1,0:T(8,128)}), f32[32,1,8,8,131]{4,3,2,1,0:T(8,128)S(1)}, u32[]{:S(2)}, u32[]{:S(2)}) async-start(f32[32,1,8,8,131]{4,3,2,1,0:T(8,128)} %bitcast.96), calls=%async_computation.2 | async-start | bytes 4194304 | tf_op jit(solution)/shard_map/all_to_all | solution.py:40
  232.2 24.8 %collective-permute-start.19 = (f32[96,256]{1,0:T(8,128)}, f32[96,256]{1,0:T(8,128)}, u32[]{:S(2)}, u32[]{:S(2)}) collective-permute-start(f32[96,256]{1,0:T(8,128)} %get-tuple-element.38), channel_id=1, source_target_pairs={{0,16},{16,0},{1,17},{17,1},{2,18},{18,2},{3,19},{19,3},{4,20},{20... | collective-permute-start | bytes 294920 | tf_op jit(solution)/shard_map/ppermute | solution.py:88
  254.3 4.4 %copy-start.1 = (f32[24,1,8,64,3]{3,2,4,1,0:T(8,128)S(1)}, f32[24,1,8,64,3]{3,2,4,1,0:T(8,128)}, u32[]{:S(2)}) copy-start(f32[24,1,8,64,3]{3,2,4,1,0:T(8,128)} %param.11) | copy-start | bytes 442372
  254.4 2.7 copy-start.4
Sparse Core Ops, SparseCore 0:
  38.2 95.3 reduce-scatter.1
  135.9 52.7 all-gather.1

commit v6 on v4

--- a/solution.py
+++ b/solution.py
@@ -42,6 +42,25 @@
     return both[..., :n], both[..., n:]
 
 
+def down_scatter(hidden, w2):
+    n = lax.axis_size("row")
+    r = lax.axis_index("row")
+    blocks = hidden.reshape(n, hidden.shape[0] // n, hidden.shape[1])
+
+    def part(j):
+        block = lax.dynamic_index_in_dim(blocks, j, 0, keepdims=False)
+        return jnp.dot(block, w2, preferred_element_type=jnp.float32)
+
+    arrived = [
+        lax.ppermute(part((r + s) % n), "row", [(j, (j + s) % n) for j in range(n)])
+        for s in range(1, n)
+    ]
+    total = part(r)
+    for piece in arrived:
+        total = total + piece
+    return total
+
+
 def ffn(tokens, up_weight, down_weight):
     i = lax.axis_index("cx")
     block, width = tokens.shape
@@ -61,8 +80,7 @@
     hg = lax.all_gather(hidden, "cz", axis=0, tiled=True)
     w2p = fetch_partner(down_weight, 0)
     w2 = jnp.concatenate([down_weight, w2p], axis=1)
-    products = jnp.dot(hg, w2, preferred_element_type=jnp.float32)
-    summed = lax.psum_scatter(products, "row", scatter_dimension=0, tiled=True)
+    summed = down_scatter(hg, w2)
     own = summed[:, :width]
     other = lax.ppermute(summed[:, width:], "cx", SWAP)
     full = jnp.where(i == 0, jnp.concatenate([own, other], 0), jnp.concatenate([other, own], 0))

time: 331 us -> 282 us (0.85)
  waiting for transfers between devices: 235 us -> 164 us
  matrix products: 13.1 us -> 25.8 us
  starting transfers between devices: 18.5 us -> 25.2 us
    all_to_all x1, waiting for transfers between devices: 50.5 us -> 0.01 us  [handover(): lax.all_to_all(picked, 'row', split_axis=3, concat_axis=0, tiled=True)]
    ppermute x2, waiting for transfers between devices: 13.7 us -> 0.01 us  [fetch_partner(): lax.ppermute(near, 'cx', SWAP)]
    dot_general x1 -> x8, matrix products: 6.14 us -> 18.9 us  [part(): return jnp.dot(block, w2, preferred_element_type=jnp.float32)]
    ppermute x0 -> x7, starting transfers between devices: none -> 7.17 us  [down_scatter(): lax.ppermute(part((r + s) % n), 'row', [(j, (j + s) % n) for j in range(n)])]
    all_gather x1, waiting for transfers between devices: 33.2 us -> 29.3 us  [ffn(): hg = lax.all_gather(hidden, 'cz', axis=0, tiled=True)]
  transfers between devices with their start and end apart: 11 -> 17, of which waited for: 7 -> 5; matrix products, arithmetic and copies ran while one was open for 9% -> 18% of each run, Pallas kernels for 0% -> 0%
where the time goes in v6:
time: 282 us; the launch traced here: 279 us
  waiting for transfers between devices  164 us (58%)
  local copies, waits for them, and re-layouts  30.2 us (11%)
  matrix products  25.8 us (9%)
  starting transfers between devices  25.2 us (9%)
  between operations  14.4 us (5%)
  blocking collectives  13.6 us (5%)
  other arithmetic  6.24 us (2%)
    reduce_scatter x1, waiting for transfers between devices, ffn(): preact = lax.psum_scatter(partial, 'cz', scatter_dimension=0, tiled=True)  94 us
    all_gather x1, waiting for transfers between devices, ffn(): hg = lax.all_gather(hidden, 'cz', axis=0, tiled=True)  29.3 us
    all_to_all x1, waiting for transfers between devices, handover(): both = lax.all_to_all(rows, 'req', split_axis=0, concat_axis=1, tiled=True)  22.8 us
    dot_general x8, matrix products, part(): return jnp.dot(block, w2, preferred_element_type=jnp.float32)  18.9 us
    ppermute x1, waiting for transfers between devices, ffn(): recv = lax.ppermute(theirs, 'cx', SWAP)  15.8 us
    all_gather x1, blocking collectives, ffn(): xg = lax.all_gather(xa, 'row', axis=0, tiled=True)  13.6 us
    all_to_all x2, local copies, waits for them, and re-layouts, handover(): lax.all_to_all(picked, 'row', split_axis=3, concat_axis=0, tiled=True)  7.18 us
    ppermute x7, starting transfers between devices, down_scatter(): lax.ppermute(part((r + s) % n), 'row', [(j, (j + s) % n) for j in range(n)])  7.17 us
  transfers between devices with their start and end apart: 17, of which 5 were waited for; matrix products, arithmetic and copies ran while one was open for 18% of the time, Pallas kernels for 0%

profile of v6, /device:TPU:8, one launch (start us, length us, event | category | flops | bytes accessed | tf_op | source)
XLA Modules:
  0.0 279.2 jit_solution(131255474805871532)
XLA Ops:
  7.2 1.8 copy.43
  9.2 2.8 %collective-permute-start.2 = (bf16[256,1344]{0,1:T(8,128)(2,1)S(1)}, bf16[256,1344]{0,1:T(8,128)(2,1)}, u32[]{:S(2)}, u32[]{:S(2)}) collective-permute-start(bf16[256,1344]{0,1:T(8,128)(2,1)S(1)} %get-tuple-element.29), channel_id=1, source_target_pairs={{0,17},{17,0},{1,16},{16,1},{2,19},{19,2},{3,18},{18,3},{4,21},{21... | collective-permute-start | bytes 2064392 | tf_op jit(solution)/shard_map/ppermute | solution.py:18
  12.0 0.2 collective-permute-start.1
  12.3 1.9 collective-permute-start
  14.2 15.8 %collective-permute-done = bf16[96,256]{1,0:T(8,128)(2,1)S(1)} collective-permute-done((bf16[96,256]{1,0:T(8,128)(2,1)S(1)}, bf16[96,256]{1,0:T(8,128)(2,1)S(1)}, u32[]{:S(2)}, u32[]{:S(2)}) %collective-permute-start) | collective-permute-done | bytes 49184 | tf_op jit(solution)/shard_map/ppermute | solution.py:71
  30.0 13.6 %all_gather.6 = bf16[768,512]{1,0:T(8,128)(2,1)S(1)} all-gather(bf16[96,512]{1,0:T(8,128)(2,1)S(1)} %pad_maximum_fusion.1), channel_id=1, replica_groups=mesh['row'=8,'cx'=2,'cz'=8,'req'=2] {'row'}, dimensions={0}, use_global_device_ids=true | all-gather | bytes 884736 | tf_op jit(solution)/shard_map/all_gather | solution.py:73
  43.6 6.9 %fusion = f32[768,2688]{1,0:T(8,128)} fusion(bf16[768,512]{1,0:T(8,128)(2,1)S(1)} %all_gather.6, bf16[256,1344]{0,1:T(8,128)(2,1)} %collective-permute-done.2, bf16[256,1344]{0,1:T(8,128)(2,1)} %collective-permute-done.1, bf16[256,2688]{0,1:T(8,128)(2,1)S(1)} %copy.43), kind=kOutput, calls=%fused_computation.7 | convolution fusion | flops 2122186752 | bytes 11796480 | tf_op jit(solution)/shard_map/dot_general | solution.py:76
  50.7 94.0 %reduce-scatter.2.cloned.1.call-done = f32[96,2688]{1,0:T(8,128)} async-done(((f32[768,2688]{1,0:T(8,128)}), f32[96,2688]{1,0:T(8,128)}) %reduce-scatter.2.cloned.1.call-update) | async-done | bytes 1032208 | tf_op jit(solution)/shard_map/reduce_scatter | solution.py:77
  144.7 2.1 multiply_convert_fusion
  146.8 0.9 fusion.51
  147.7 2.7 collective-permute-start.4
  150.4 0.2 collective-permute-start.3
  150.7 0.2 select_reduce_fusion.1
  150.9 0.1 select_reduce_fusion.2
  151.0 0.6 gather_fusion.1
  151.6 0.7 copy.44
  152.3 4.8 %gather_fusion = f32[8,8,64,128]{3,2,1,0:T(8,128)} fusion(f32[24,8,64,128]{3,2,1,0:T(8,128)} %bitcast.69, s32[1024]{0:T(1024)S(1)} %pad_clamp_fusion.2), kind=kCustom, calls=%fused_computation | custom fusion | bytes 4194336 | tf_op jit(solution)/shard_map/gather | solution.py:36
  157.1 2.0 pad_maximum_fusion
  159.2 4.4 %copy.45 = f32[8,1,8,64,131]{4,2,0,1,3:T(8,128)} copy(f32[8,1,8,64,131]{4,3,2,0,1:T(8,128)S(1)} %pad_maximum_fusion) | data formatting | bytes 4292608 | tf_op jit(solution)/shard_map/concatenate | solution.py:36
  163.6 5.1 %all-to-all-start = ((f32[8,1,8,64,131]{4,2,0,1,3:T(8,128)}), f32[8,1,8,64,131]{4,2,0,1,3:T(8,128)}, u32[]{:S(2)}, u32[]{:S(2)}) async-start(f32[8,1,8,64,131]{4,2,0,1,3:T(8,128)} %copy.45), calls=%async_computation.1 | async-start | bytes 8388608 | tf_op jit(solution)/shard_map/all_to_all | solution.py:37
  169.0 0.7 gather_fusion.3
  169.7 0.7 gather_fusion.2
  170.4 29.3 %all-gather.2.cloned.1.call-done = bf16[768,2688]{1,0:T(8,128)(2,1)} async-done(((bf16[96,2688]{1,0:T(8,128)(2,1)}), bf16[768,2688]{1,0:T(8,128)(2,1)}) %all-gather.2.cloned.1.call-update) | async-done | bytes 4128784 | tf_op jit(solution)/shard_map/all_gather | solution.py:80
  199.7 2.2 fusion.12
  202.0 0.5 copy-done.7
  202.5 1.9 fusion.14
  204.4 2.3 collective-permute-start.10
  206.7 1.9 fusion.16
  208.6 0.3 collective-permute-start.9
  208.9 2.6 fusion.18
  211.4 1.1 collective-permute-start.8
  212.6 2.6 fusion.20
  215.1 1.6 collective-permute-start.7
  216.8 2.6 fusion.22
  219.3 2.6 fusion.24
  221.9 1.8 collective-permute-start.6
  223.7 1.6 collective-permute-done.10
  225.4 4.6 %copy.52 = f32[8,1,8,64,131]{4,3,2,0,1:T(8,128)S(1)} copy(f32[8,1,8,64,131]{4,2,0,1,3:T(8,128)} %all-to-all-done) | data formatting | bytes 4292608 | tf_op jit(solution)/shard_map/all_to_all | solution.py:37
  230.0 2.6 copy.47
  232.6 4.2 %gather_fusion.4 = f32[32,8,8,131]{3,2,1,0:T(8,128)} fusion(f32[64,8,8,131]{3,2,1,0:T(8,128)} %bitcast.63, s32[1024]{0:T(1024)S(1)} %pad_clamp_fusion), kind=kCustom, calls=%fused_computation.4 | custom fusion | bytes 2146432 | tf_op jit(solution)/shard_map/gather | solution.py:39
  236.8 3.8 %all-to-all-start.1 = ((f32[32,1,8,8,131]{4,3,2,1,0:T(8,128)}), f32[32,1,8,8,131]{4,3,2,1,0:T(8,128)S(1)}, u32[]{:S(2)}, u32[]{:S(2)}) async-start(f32[32,1,8,8,131]{4,3,2,1,0:T(8,128)} %bitcast.66), calls=%async_computation.2 | async-start | bytes 4194304 | tf_op jit(solution)/shard_map/all_to_all | solution.py:40
  240.6 2.6 fusion.11
  243.2 0.7 fusion.53
  243.9 1.2 collective-permute-start.12
  245.1 22.8 %all-to-all-done.1 = f32[32,1,8,8,131]{4,3,2,1,0:T(8,128)S(1)} async-done(((f32[32,1,8,8,131]{4,3,2,1,0:T(8,128)}), f32[32,1,8,8,131]{4,3,2,1,0:T(8,128)S(1)}, u32[]{:S(2)}, u32[]{:S(2)}) %all-to-all-start.1) | async-done | bytes 1073184 | tf_op jit(solution)/shard_map/all_to_all | solution.py:40
  268.1 1.1 copy.49
  269.2 1.5 copy.50
  270.8 1.6 fusion.36
  (49 shorter events, 0.7 us)
Async XLA Ops:
  7.2 143.8 %copy-start = (f32[24,1,8,64,3]{3,2,4,1,0:T(8,128)S(1)}, f32[24,1,8,64,3]{3,2,4,1,0:T(8,128)}, u32[]{:S(2)}) copy-start(f32[24,1,8,64,3]{3,2,4,1,0:T(8,128)} %param.11) | copy-start | bytes 442372
  7.2 5.1 %copy-start.4 = (bf16[192,256]{1,0:T(8,128)(2,1)S(1)}, bf16[192,256]{1,0:T(8,128)(2,1)}, u32[]{:S(2)}) copy-start(bf16[192,256]{1,0:T(8,128)(2,1)} %param.7) | copy-start | bytes 294916
  7.2 137.5 %reduce-scatter.2.cloned.1.call-start = ((), (), s32[]{:S(2)}) async-start(), calls=%async_computation.3 | async-start | bytes 9289728 | tf_op jit(solution)/shard_map/reduce_scatter | solution.py:77
  9.2 34.4 %collective-permute-start.2 = (bf16[256,1344]{0,1:T(8,128)(2,1)S(1)}, bf16[256,1344]{0,1:T(8,128)(2,1)}, u32[]{:S(2)}, u32[]{:S(2)}) collective-permute-start(bf16[256,1344]{0,1:T(8,128)(2,1)S(1)} %get-tuple-element.29), channel_id=1, source_target_pairs={{0,17},{17,0},{1,16},{16,1},{2,19},{19,2},{3,18},{18,3},{4,21},{21... | collective-permute-start | bytes 2064392 | tf_op jit(solution)/shard_map/ppermute | solution.py:18
  12.0 31.6 %collective-permute-start.1 = (bf16[256,1344]{0,1:T(8,128)(2,1)S(1)}, bf16[256,1344]{0,1:T(8,128)(2,1)}, u32[]{:S(2)}, u32[]{:S(2)}) collective-permute-start(bf16[256,1344]{0,1:T(8,128)(2,1)S(1)} %get-tuple-element.28), channel_id=1, source_target_pairs={{0,16},{16,0},{1,17},{17,1},{2,18},{18,2},{3,19},{19,3},{4,20},{20... | collective-permute-start | bytes 2064392 | tf_op jit(solution)/shard_map/ppermute | solution.py:18
  12.3 17.7 %collective-permute-start = (bf16[96,256]{1,0:T(8,128)(2,1)S(1)}, bf16[96,256]{1,0:T(8,128)(2,1)S(1)}, u32[]{:S(2)}, u32[]{:S(2)}) collective-permute-start(bf16[96,256]{1,0:T(8,128)(2,1)S(1)} %get-tuple-element.33), channel_id=1, source_target_pairs={{0,16},{16,0},{1,17},{17,1},{2,18},{18,2},{3,19},{19,3},{4,20},{20... | collective-permute-start | bytes 147464 | tf_op jit(solution)/shard_map/ppermute | solution.py:71
  50.6 96.2 %copy-start.2 = (bf16[2688,256]{1,0:T(8,128)(2,1)S(1)}, bf16[2688,256]{1,0:T(8,128)(2,1)}, u32[]{:S(2)}) copy-start(bf16[2688,256]{1,0:T(8,128)(2,1)} %param.9) | copy-start | bytes 4128772
  50.6 100.1 %copy-start.6 = (s32[32]{0:T(128)S(1)}, s32[32]{0:T(128)}, u32[]{:S(2)}) copy-start(s32[32]{0:T(128)} %param.12) | copy-start | bytes 388
  50.6 149.1 %all-gather.2.cloned.1.call-start = ((), (), s32[]{:S(2)}) async-start(), calls=%async_computation.4 | async-start | bytes 4644864 | tf_op jit(solution)/shard_map/all_gather | solution.py:80
  147.7 22.6 %collective-permute-start.4 = (bf16[1344,256]{1,0:T(8,128)(2,1)}, bf16[1344,256]{1,0:T(8,128)(2,1)}, u32[]{:S(2)}, u32[]{:S(2)}) collective-permute-start(bf16[1344,256]{1,0:T(8,128)(2,1)} %get-tuple-element.27), channel_id=1, source_target_pairs={{0,17},{17,0},{1,16},{16,1},{2,19},{19,2},{3,18},{18,3},{4,21},{21... | collective-permute-start | bytes 2064392 | tf_op jit(solution)/shard_map/ppermute | solution.py:18
  150.4 20.0 %collective-permute-start.3 = (bf16[1344,256]{1,0:T(8,128)(2,1)S(1)}, bf16[1344,256]{1,0:T(8,128)(2,1)}, u32[]{:S(2)}, u32[]{:S(2)}) collective-permute-start(bf16[1344,256]{1,0:T(8,128)(2,1)S(1)} %get-tuple-element.26), channel_id=1, source_target_pairs={{0,16},{16,0},{1,17},{17,1},{2,18},{18,2},{3,19},{19,3},{4,20},{20... | collective-permute-start | bytes 2064392 | tf_op jit(solution)/shard_map/ppermute | solution.py:18
  163.6 5.1 %copy-start.8 = (s32[32]{0:T(128)S(1)}, s32[32]{0:T(128)}, u32[]{:S(2)}) copy-start(s32[32]{0:T(128)} %param.13) | copy-start | bytes 388
  163.6 36.1 %copy-start.3 = (bf16[2688,256]{1,0:T(8,128)(2,1)S(1)}, bf16[2688,256]{1,0:T(8,128)(2,1)}, u32[]{:S(2)}) copy-start(bf16[2688,256]{1,0:T(8,128)(2,1)} %param.9) | copy-start | bytes 4128772
  163.6 61.8 %all-to-all-start = ((f32[8,1,8,64,131]{4,2,0,1,3:T(8,128)}), f32[8,1,8,64,131]{4,2,0,1,3:T(8,128)}, u32[]{:S(2)}, u32[]{:S(2)}) async-start(f32[8,1,8,64,131]{4,2,0,1,3:T(8,128)} %copy.45), calls=%async_computation.1 | async-start | bytes 8388608 | tf_op jit(solution)/shard_map/all_to_all | solution.py:37
  199.7 2.7 copy-start.7
  201.9 20.0 %collective-permute-start.11 = (f32[96,512]{1,0:T(8,128)S(1)}, f32[96,512]{1,0:T(8,128)S(1)}, u32[]{:S(2)}, u32[]{:S(2)}) collective-permute-start(f32[96,512]{1,0:T(8,128)S(1)} %fusion.12), channel_id=1, source_target_pairs={{0,224},{32,0},{64,32},{96,64},{128,96},{160,128},{192,160},{224,1... | collective-permute-start | bytes 589832 | tf_op jit(solution)/shard_map/ppermute | solution.py:55
  204.4 21.0 %collective-permute-start.10 = (f32[96,512]{1,0:T(8,128)S(1)}, f32[96,512]{1,0:T(8,128)S(1)}, u32[]{:S(2)}, u32[]{:S(2)}) collective-permute-start(f32[96,512]{1,0:T(8,128)S(1)} %fusion.14), channel_id=1, source_target_pairs={{0,192},{32,224},{64,0},{96,32},{128,64},{160,96},{192,128},{224,1... | collective-permute-start | bytes 589832 | tf_op jit(solution)/shard_map/ppermute | solution.py:55
  208.6 32.0 %collective-permute-start.9 = (f32[96,512]{1,0:T(8,128)S(1)}, f32[96,512]{1,0:T(8,128)S(1)}, u32[]{:S(2)}, u32[]{:S(2)}) collective-permute-start(f32[96,512]{1,0:T(8,128)S(1)} %fusion.16), channel_id=1, source_target_pairs={{0,160},{32,192},{64,224},{96,0},{128,32},{160,64},{192,96},{224,1... | collective-permute-start | bytes 589832 | tf_op jit(solution)/shard_map/ppermute | solution.py:55
  211.4 29.1 %collective-permute-start.8 = (f32[96,512]{1,0:T(8,128)}, f32[96,512]{1,0:T(8,128)S(1)}, u32[]{:S(2)}, u32[]{:S(2)}) collective-permute-start(f32[96,512]{1,0:T(8,128)} %fusion.18), channel_id=1, source_target_pairs={{0,128},{32,160},{64,192},{96,224},{128,0},{160,32},{192,64},{224,... | collective-permute-start | bytes 589832 | tf_op jit(solution)/shard_map/ppermute | solution.py:55
  215.1 25.4 %collective-permute-start.7 = (f32[96,512]{1,0:T(8,128)}, f32[96,512]{1,0:T(8,128)S(1)}, u32[]{:S(2)}, u32[]{:S(2)}) collective-permute-start(f32[96,512]{1,0:T(8,128)} %fusion.20), channel_id=1, source_target_pairs={{0,96},{32,128},{64,160},{96,192},{128,224},{160,0},{192,32},{224,... | collective-permute-start | bytes 589832 | tf_op jit(solution)/shard_map/ppermute | solution.py:55
  221.9 18.7 %collective-permute-start.6 = (f32[96,512]{1,0:T(8,128)}, f32[96,512]{1,0:T(8,128)}, u32[]{:S(2)}, u32[]{:S(2)}) collective-permute-start(f32[96,512]{1,0:T(8,128)} %fusion.22), channel_id=1, source_target_pairs={{0,64},{32,96},{64,128},{96,160},{128,192},{160,224},{192,0},{224,... | collective-permute-start | bytes 589832 | tf_op jit(solution)/shard_map/ppermute | solution.py:55
  225.3 15.2 %collective-permute-start.5 = (f32[96,512]{1,0:T(8,128)}, f32[96,512]{1,0:T(8,128)}, u32[]{:S(2)}, u32[]{:S(2)}) collective-permute-start(f32[96,512]{1,0:T(8,128)} %fusion.24), channel_id=1, source_target_pairs={{0,32},{32,64},{64,96},{96,128},{128,160},{160,192},{192,224},{224... | collective-permute-start | bytes 589832 | tf_op jit(solution)/shard_map/ppermute | solution.py:55
  236.8 31.2 %all-to-all-start.1 = ((f32[32,1,8,8,131]{4,3,2,1,0:T(8,128)}), f32[32,1,8,8,131]{4,3,2,1,0:T(8,128)S(1)}, u32[]{:S(2)}, u32[]{:S(2)}) async-start(f32[32,1,8,8,131]{4,3,2,1,0:T(8,128)} %bitcast.66), calls=%async_computation.2 | async-start | bytes 4194304 | tf_op jit(solution)/shard_map/all_to_all | solution.py:40
  243.9 26.9 %collective-permute-start.12 = (f32[96,256]{1,0:T(8,128)}, f32[96,256]{1,0:T(8,128)}, u32[]{:S(2)}, u32[]{:S(2)}) collective-permute-start(f32[96,256]{1,0:T(8,128)} %get-tuple-element.31), channel_id=1, source_target_pairs={{0,16},{16,0},{1,17},{17,1},{2,18},{18,2},{3,19},{19,3},{4,20},{20... | collective-permute-start | bytes 294920 | tf_op jit(solution)/shard_map/ppermute | solution.py:85
  267.9 4.5 %copy-start.1 = (f32[24,1,8,64,3]{3,2,4,1,0:T(8,128)S(1)}, f32[24,1,8,64,3]{3,2,4,1,0:T(8,128)}, u32[]{:S(2)}) copy-start(f32[24,1,8,64,3]{3,2,4,1,0:T(8,128)} %param.11) | copy-start | bytes 442372
  268.1 2.7 copy-start.5
Sparse Core Ops, SparseCore 0:
  50.7 93.9 reduce-scatter.1
  146.9 52.7 all-gather.1

commit v7 on v4

--- a/solution.py
+++ b/solution.py
@@ -42,6 +42,25 @@
     return both[..., :n], both[..., n:]
 
 
+def scatter_out(x, width):
+    rows = lax.axis_size("row")
+    n = 2 * rows
+    place = lax.axis_index("row") * 2 + lax.axis_index("cx")
+    blocks = x.reshape(rows, x.shape[0] // rows, x.shape[1])
+    same, other = None, None
+    for s in range(n):
+        dest = (place + s) % n
+        chunk = lax.dynamic_index_in_dim(blocks, dest // 2, 0, keepdims=False)
+        chunk = chunk[:, (s % 2) * width:(s % 2 + 1) * width]
+        if s:
+            chunk = lax.ppermute(chunk, ("row", "cx"), [(j, (j + s) % n) for j in range(n)])
+        if s % 2:
+            other = chunk if other is None else other + chunk
+        else:
+            same = chunk if same is None else same + chunk
+    return same, other
+
+
 def ffn(tokens, up_weight, down_weight):
     i = lax.axis_index("cx")
     block, width = tokens.shape
@@ -62,9 +81,7 @@
     w2p = fetch_partner(down_weight, 0)
     w2 = jnp.concatenate([down_weight, w2p], axis=1)
     products = jnp.dot(hg, w2, preferred_element_type=jnp.float32)
-    summed = lax.psum_scatter(products, "row", scatter_dimension=0, tiled=True)
-    own = summed[:, :width]
-    other = lax.ppermute(summed[:, width:], "cx", SWAP)
+    own, other = scatter_out(products, width)
     full = jnp.where(i == 0, jnp.concatenate([own, other], 0), jnp.concatenate([other, own], 0))
     return (tokens.astype(jnp.float32) + full).astype(jnp.bfloat16)
 

time: 331 us -> 294 us (0.89)
  waiting for transfers between devices: 235 us -> 173 us
  starting transfers between devices: 18.5 us -> 35.7 us
  local copies, waits for them, and re-layouts: 29.7 us -> 33.7 us
    all_gather x1, waiting for transfers between devices: 33.2 us -> 0.01 us  [ffn(): hg = lax.all_gather(hidden, 'cz', axis=0, tiled=True)]
    all_to_all x1, waiting for transfers between devices: 24.7 us -> 0.01 us  [handover(): both = lax.all_to_all(rows, 'req', split_axis=0, concat_axis=1, tiled=True)]
    ppermute x1 -> x15, waiting for transfers between devices: 0.01 us -> 20.6 us  [scatter_out(): lax.ppermute(chunk, ('row', 'cx'), [(j, (j + s) % n) for j in range(n)])]
    ppermute x1 -> x15, starting transfers between devices: 1.02 us -> 18.4 us  [scatter_out(): lax.ppermute(chunk, ('row', 'cx'), [(j, (j + s) % n) for j in range(n)])]
    ppermute x2, waiting for transfers between devices: 13.7 us -> 0.01 us  [fetch_partner(): lax.ppermute(near, 'cx', SWAP)]
    all_to_all x1, waiting for transfers between devices: 50.5 us -> 42.5 us  [handover(): lax.all_to_all(picked, 'row', split_axis=3, concat_axis=0, tiled=True)]
  transfers between devices with their start and end apart: 11 -> 24, of which waited for: 7 -> 11; matrix products, arithmetic and copies ran while one was open for 9% -> 14% of each run, Pallas kernels for 0% -> 0%
where the time goes in v7:
time: 294 us; the launch traced here: 291 us
  waiting for transfers between devices  173 us (59%)
  starting transfers between devices  35.7 us (12%)
  local copies, waits for them, and re-layouts  33.7 us (11%)
  between operations  14.9 us (5%)
  blocking collectives  13.6 us (5%)
  matrix products  12.4 us (4%)
  other arithmetic  7.42 us (3%)
    reduce_scatter x1, waiting for transfers between devices, ffn(): preact = lax.psum_scatter(partial, 'cz', scatter_dimension=0, tiled=True)  94.1 us
    all_to_all x1, waiting for transfers between devices, handover(): lax.all_to_all(picked, 'row', split_axis=3, concat_axis=0, tiled=True)  42.5 us
    ppermute x15, waiting for transfers between devices, scatter_out(): lax.ppermute(chunk, ('row', 'cx'), [(j, (j + s) % n) for j in range(n)])  20.6 us
    ppermute x15, starting transfers between devices, scatter_out(): lax.ppermute(chunk, ('row', 'cx'), [(j, (j + s) % n) for j in range(n)])  18.4 us
    ppermute x1, waiting for transfers between devices, ffn(): recv = lax.ppermute(theirs, 'cx', SWAP)  15.8 us
    all_gather x1, blocking collectives, ffn(): xg = lax.all_gather(xa, 'row', axis=0, tiled=True)  13.6 us
    all_to_all x2, local copies, waits for them, and re-layouts, handover(): lax.all_to_all(picked, 'row', split_axis=3, concat_axis=0, tiled=True)  7.2 us
    dot_general x1, matrix products, ffn(): partial = jnp.dot(xg, w1, preferred_element_type=jnp.float32)  6.99 us
  transfers between devices with their start and end apart: 24, of which 11 were waited for; matrix products, arithmetic and copies ran while one was open for 14% of the time, Pallas kernels for 0%

profile of v7, /device:TPU:8, one launch (start us, length us, event | category | flops | bytes accessed | tf_op | source)
XLA Modules:
  0.0 290.7 jit_solution(12779741807444566972)
XLA Ops:
  7.2 1.8 copy.43
  9.2 2.8 collective-permute-start.2
  12.3 1.9 collective-permute-start
  14.2 15.8 %collective-permute-done = bf16[96,256]{1,0:T(8,128)(2,1)S(1)} collective-permute-done((bf16[96,256]{1,0:T(8,128)(2,1)S(1)}, bf16[96,256]{1,0:T(8,128)(2,1)S(1)}, u32[]{:S(2)}, u32[]{:S(2)}) %collective-permute-start) | collective-permute-done | bytes 49184 | tf_op jit(solution)/shard_map/ppermute | solution.py:71
  30.0 13.6 %all_gather.6 = bf16[768,512]{1,0:T(8,128)(2,1)S(1)} all-gather(bf16[96,512]{1,0:T(8,128)(2,1)S(1)} %pad_maximum_fusion.1), channel_id=1, replica_groups=mesh['row'=8,'cx'=2,'cz'=8,'req'=2] {'row'}, dimensions={0}, use_global_device_ids=true | all-gather | bytes 884736 | tf_op jit(solution)/shard_map/all_gather | solution.py:73
  43.6 7.0 %fusion = f32[768,2688]{1,0:T(8,128)} fusion(bf16[768,512]{1,0:T(8,128)(2,1)S(1)} %all_gather.6, bf16[256,1344]{0,1:T(8,128)(2,1)} %collective-permute-done.2, bf16[256,1344]{0,1:T(8,128)(2,1)} %collective-permute-done.1, bf16[256,2688]{0,1:T(8,128)(2,1)S(1)} %copy.43), kind=kOutput, calls=%fused_computation.7 | convolution fusion | flops 2122186752 | bytes 11796480 | tf_op jit(solution)/shard_map/dot_general | solution.py:76
  50.7 94.1 %reduce-scatter.2.cloned.1.call-done = f32[96,2688]{1,0:T(8,128)} async-done(((f32[768,2688]{1,0:T(8,128)}), f32[96,2688]{1,0:T(8,128)}) %reduce-scatter.2.cloned.1.call-update) | async-done | bytes 1032208 | tf_op jit(solution)/shard_map/reduce_scatter | solution.py:77
  144.7 2.1 multiply_convert_fusion
  147.8 0.7 copy.44
  148.5 4.8 %gather_fusion = f32[8,8,64,128]{3,2,1,0:T(8,128)} fusion(f32[24,8,64,128]{3,2,1,0:T(8,128)} %bitcast.79, s32[1024]{0:T(1024)S(1)} %pad_clamp_fusion.2), kind=kCustom, calls=%fused_computation | custom fusion | bytes 4194336 | tf_op jit(solution)/shard_map/gather | solution.py:36
  153.3 2.1 pad_maximum_fusion
  155.4 4.5 %copy.45 = f32[8,1,8,64,131]{4,2,0,1,3:T(8,128)} copy(f32[8,1,8,64,131]{4,3,2,0,1:T(8,128)S(1)} %pad_maximum_fusion) | data formatting | bytes 4292608 | tf_op jit(solution)/shard_map/concatenate | solution.py:36
  159.9 5.1 %all-to-all-start = ((f32[8,1,8,64,131]{4,2,0,1,3:T(8,128)}), f32[8,1,8,64,131]{4,2,0,1,3:T(8,128)}, u32[]{:S(2)}, u32[]{:S(2)}) async-start(f32[8,1,8,64,131]{4,2,0,1,3:T(8,128)} %copy.45), calls=%async_computation.1 | async-start | bytes 8388608 | tf_op jit(solution)/shard_map/all_to_all | solution.py:37
  165.0 0.9 fusion.27
  165.9 2.7 collective-permute-start.4
  169.3 0.7 gather_fusion.3
  170.0 0.7 gather_fusion.2
  170.8 42.5 %all-to-all-done = f32[8,1,8,64,131]{4,2,0,1,3:T(8,128)} async-done(((f32[8,1,8,64,131]{4,2,0,1,3:T(8,128)}), f32[8,1,8,64,131]{4,2,0,1,3:T(8,128)}, u32[]{:S(2)}, u32[]{:S(2)}) %all-to-all-start) | async-done | bytes 2146336 | tf_op jit(solution)/shard_map/all_to_all | solution.py:37
  213.3 4.6 %copy.52 = f32[8,1,8,64,131]{4,3,2,0,1:T(8,128)S(1)} copy(f32[8,1,8,64,131]{4,2,0,1,3:T(8,128)} %all-to-all-done) | data formatting | bytes 4292608 | tf_op jit(solution)/shard_map/all_to_all | solution.py:37
  217.9 2.6 copy.47
  220.5 4.2 %gather_fusion.4 = f32[32,8,8,131]{3,2,1,0:T(8,128)} fusion(f32[64,8,8,131]{3,2,1,0:T(8,128)} %bitcast.72, s32[1024]{0:T(1024)S(1)} %pad_clamp_fusion), kind=kCustom, calls=%fused_computation.4 | custom fusion | bytes 2146432 | tf_op jit(solution)/shard_map/gather | solution.py:39
  224.7 4.3 %all-to-all-start.1 = ((f32[32,1,8,8,131]{4,3,2,1,0:T(8,128)}), f32[32,1,8,8,131]{4,3,2,1,0:T(8,128)S(1)}, u32[]{:S(2)}, u32[]{:S(2)}) async-start(f32[32,1,8,8,131]{4,3,2,1,0:T(8,128)} %bitcast.75), calls=%async_computation.2 | async-start | bytes 4194304 | tf_op jit(solution)/shard_map/all_to_all | solution.py:40
  229.0 5.4 %fusion.6 = f32[768,512]{1,0:T(8,128)S(1)} fusion(bf16[768,2688]{1,0:T(8,128)(2,1)} %all-gather.2.cloned.1.call-done, bf16[1344,256]{1,0:T(8,128)(2,1)} %collective-permute-done.4, bf16[1344,256]{1,0:T(8,128)(2,1)} %collective-permute-done.3, bf16[2688,256]{1,0:T(8,128)(2,1)} %param.9), kind=kOutput, calls=%fused_computation.13 | convolution fusion | flops 2122186752 | bytes 8454144 | tf_op jit(solution)/shard_map/dot_general | solution.py:83
  234.4 1.2 dynamic-slice_bitcast_fusion.15
  235.6 1.1 collective-permute-start.19
  236.8 1.9 collective-permute-start.18
  238.8 3.0 %collective-permute-start.16 = (f32[96,256]{1,0:T(8,128)S(1)}, f32[96,256]{1,0:T(8,128)S(1)}, u32[]{:S(2)}, u32[]{:S(2)}) collective-permute-start(f32[96,256]{1,0:T(8,128)S(1)} %slice.94), channel_id=1, source_target_pairs={{0,144},{16,160},{32,176},{48,192},{64,208},{80,224},{96,240},{112... | collective-permute-start | bytes 294920 | tf_op jit(solution)/shard_map/ppermute | solution.py:56
  244.5 0.7 slice.88
  245.2 11.1 %collective-permute-done.19 = f32[96,256]{1,0:T(8,128)S(1)} collective-permute-done((f32[96,256]{1,0:T(8,128)S(1)}, f32[96,256]{1,0:T(8,128)S(1)}, u32[]{:S(2)}, u32[]{:S(2)}) %collective-permute-start.19) | collective-permute-done | bytes 98336 | tf_op jit(solution)/shard_map/ppermute | solution.py:56
  256.3 0.7 collective-permute-done.18
  257.0 1.7 collective-permute-start.12
  258.6 1.1 collective-permute-done.17
  259.7 2.4 collective-permute-start.13
  262.1 1.2 collective-permute-start.11
  263.3 2.3 collective-permute-done.15
  265.6 1.0 collective-permute-start.10
  266.9 1.1 copy.49
  268.0 1.6 copy.50
  269.8 2.9 %collective-permute-start.8 = (f32[96,256]{1,0:T(8,128)S(1)}, f32[96,256]{1,0:T(8,128)S(1)}, u32[]{:S(2)}, u32[]{:S(2)}) collective-permute-start(f32[96,256]{1,0:T(8,128)S(1)} %slice.86), channel_id=1, source_target_pairs={{0,128},{16,144},{32,160},{48,176},{64,192},{80,208},{96,224},{112... | collective-permute-start | bytes 294920 | tf_op jit(solution)/shard_map/ppermute | solution.py:56
  272.7 2.0 collective-permute-start.7
  274.7 0.9 collective-permute-start.6
  275.7 1.1 add_add_fusion
  276.7 1.6 collective-permute-done.8
  278.4 1.1 collective-permute-done.7
  279.4 1.8 collective-permute-done.6
  281.3 0.9 collective-permute-done.5
  282.1 1.0 fusion.19
  283.1 0.7 fusion.13
  (99 shorter events, 4.9 us)
Async XLA Ops:
  7.2 140.1 %copy-start = (f32[24,1,8,64,3]{3,2,4,1,0:T(8,128)S(1)}, f32[24,1,8,64,3]{3,2,4,1,0:T(8,128)}, u32[]{:S(2)}) copy-start(f32[24,1,8,64,3]{3,2,4,1,0:T(8,128)} %param.11) | copy-start | bytes 442372
  7.2 5.1 %copy-start.9 = (bf16[192,256]{1,0:T(8,128)(2,1)S(1)}, bf16[192,256]{1,0:T(8,128)(2,1)}, u32[]{:S(2)}) copy-start(bf16[192,256]{1,0:T(8,128)(2,1)} %param.7) | copy-start | bytes 294916
  7.2 137.5 %reduce-scatter.2.cloned.1.call-start = ((), (), s32[]{:S(2)}) async-start(), calls=%async_computation.3 | async-start | bytes 9289728 | tf_op jit(solution)/shard_map/reduce_scatter | solution.py:77
  9.2 34.4 %collective-permute-start.2 = (bf16[256,1344]{0,1:T(8,128)(2,1)S(1)}, bf16[256,1344]{0,1:T(8,128)(2,1)}, u32[]{:S(2)}, u32[]{:S(2)}) collective-permute-start(bf16[256,1344]{0,1:T(8,128)(2,1)S(1)} %get-tuple-element.45), channel_id=1, source_target_pairs={{0,17},{17,0},{1,16},{16,1},{2,19},{19,2},{3,18},{18,3},{4,21},{21... | collective-permute-start | bytes 2064392 | tf_op jit(solution)/shard_map/ppermute | solution.py:18
  12.0 31.6 %collective-permute-start.1 = (bf16[256,1344]{0,1:T(8,128)(2,1)S(1)}, bf16[256,1344]{0,1:T(8,128)(2,1)}, u32[]{:S(2)}, u32[]{:S(2)}) collective-permute-start(bf16[256,1344]{0,1:T(8,128)(2,1)S(1)} %get-tuple-element.44), channel_id=1, source_target_pairs={{0,16},{16,0},{1,17},{17,1},{2,18},{18,2},{3,19},{19,3},{4,20},{20... | collective-permute-start | bytes 2064392 | tf_op jit(solution)/shard_map/ppermute | solution.py:18
  12.3 17.7 %collective-permute-start = (bf16[96,256]{1,0:T(8,128)(2,1)S(1)}, bf16[96,256]{1,0:T(8,128)(2,1)S(1)}, u32[]{:S(2)}, u32[]{:S(2)}) collective-permute-start(bf16[96,256]{1,0:T(8,128)(2,1)S(1)} %get-tuple-element.47), channel_id=1, source_target_pairs={{0,16},{16,0},{1,17},{17,1},{2,18},{18,2},{3,19},{19,3},{4,20},{20... | collective-permute-start | bytes 147464 | tf_op jit(solution)/shard_map/ppermute | solution.py:71
  50.6 96.3 %copy-start.20 = (s32[32]{0:T(128)S(1)}, s32[32]{0:T(128)}, u32[]{:S(2)}) copy-start(s32[32]{0:T(128)} %param.12) | copy-start | bytes 388
  50.6 178.4 %all-gather.2.cloned.1.call-start = ((), (), s32[]{:S(2)}) async-start(), calls=%async_computation.4 | async-start | bytes 4644864 | tf_op jit(solution)/shard_map/all_gather | solution.py:80
  159.9 5.1 %copy-start.2 = (bf16[2688,256]{1,0:T(8,128)(2,1)S(1)}, bf16[2688,256]{1,0:T(8,128)(2,1)}, u32[]{:S(2)}) copy-start(bf16[2688,256]{1,0:T(8,128)(2,1)} %param.9) | copy-start | bytes 4128772
  159.9 53.4 %all-to-all-start = ((f32[8,1,8,64,131]{4,2,0,1,3:T(8,128)}), f32[8,1,8,64,131]{4,2,0,1,3:T(8,128)}, u32[]{:S(2)}, u32[]{:S(2)}) async-start(f32[8,1,8,64,131]{4,2,0,1,3:T(8,128)} %copy.45), calls=%async_computation.1 | async-start | bytes 8388608 | tf_op jit(solution)/shard_map/all_to_all | solution.py:37
  165.0 3.9 %copy-start.21 = (s32[32]{0:T(128)S(1)}, s32[32]{0:T(128)}, u32[]{:S(2)}) copy-start(s32[32]{0:T(128)} %param.13) | copy-start | bytes 388
  165.9 63.1 %collective-permute-start.4 = (bf16[1344,256]{1,0:T(8,128)(2,1)}, bf16[1344,256]{1,0:T(8,128)(2,1)}, u32[]{:S(2)}, u32[]{:S(2)}) collective-permute-start(bf16[1344,256]{1,0:T(8,128)(2,1)} %get-tuple-element.43), channel_id=1, source_target_pairs={{0,17},{17,0},{1,16},{16,1},{2,19},{19,2},{3,18},{18,3},{4,21},{21... | collective-permute-start | bytes 2064392 | tf_op jit(solution)/shard_map/ppermute | solution.py:18
  168.6 60.4 %collective-permute-start.3 = (bf16[1344,256]{1,0:T(8,128)(2,1)S(1)}, bf16[1344,256]{1,0:T(8,128)(2,1)}, u32[]{:S(2)}, u32[]{:S(2)}) collective-permute-start(bf16[1344,256]{1,0:T(8,128)(2,1)S(1)} %get-tuple-element.42), channel_id=1, source_target_pairs={{0,16},{16,0},{1,17},{17,1},{2,18},{18,2},{3,19},{19,3},{4,20},{20... | collective-permute-start | bytes 2064392 | tf_op jit(solution)/shard_map/ppermute | solution.py:18
  224.7 41.9 %all-to-all-start.1 = ((f32[32,1,8,8,131]{4,3,2,1,0:T(8,128)}), f32[32,1,8,8,131]{4,3,2,1,0:T(8,128)S(1)}, u32[]{:S(2)}, u32[]{:S(2)}) async-start(f32[32,1,8,8,131]{4,3,2,1,0:T(8,128)} %bitcast.75), calls=%async_computation.2 | async-start | bytes 4194304 | tf_op jit(solution)/shard_map/all_to_all | solution.py:40
  235.6 20.7 %collective-permute-start.19 = (f32[96,256]{1,0:T(8,128)S(1)}, f32[96,256]{1,0:T(8,128)S(1)}, u32[]{:S(2)}, u32[]{:S(2)}) collective-permute-start(f32[96,256]{1,0:T(8,128)S(1)} %slice.97), channel_id=1, source_target_pairs={{0,240},{16,0},{32,16},{48,32},{64,48},{80,64},{96,80},{112,96},{1... | collective-permute-start | bytes 294920 | tf_op jit(solution)/shard_map/ppermute | solution.py:56
  236.8 20.2 %collective-permute-start.18 = (f32[96,256]{1,0:T(8,128)S(1)}, f32[96,256]{1,0:T(8,128)S(1)}, u32[]{:S(2)}, u32[]{:S(2)}) collective-permute-start(f32[96,256]{1,0:T(8,128)S(1)} %slice.96), channel_id=1, source_target_pairs={{0,208},{16,224},{32,240},{48,0},{64,16},{80,32},{96,48},{112,64},... | collective-permute-start | bytes 294920 | tf_op jit(solution)/shard_map/ppermute | solution.py:56
  238.7 21.0 %collective-permute-start.17 = (f32[96,256]{1,0:T(8,128)S(1)}, f32[96,256]{1,0:T(8,128)S(1)}, u32[]{:S(2)}, u32[]{:S(2)}) collective-permute-start(f32[96,256]{1,0:T(8,128)S(1)} %slice.95), channel_id=1, source_target_pairs={{0,176},{16,192},{32,208},{48,224},{64,240},{80,0},{96,16},{112,32... | collective-permute-start | bytes 294920 | tf_op jit(solution)/shard_map/ppermute | solution.py:56
  238.8 23.3 %collective-permute-start.16 = (f32[96,256]{1,0:T(8,128)S(1)}, f32[96,256]{1,0:T(8,128)S(1)}, u32[]{:S(2)}, u32[]{:S(2)}) collective-permute-start(f32[96,256]{1,0:T(8,128)S(1)} %slice.94), channel_id=1, source_target_pairs={{0,144},{16,160},{32,176},{48,192},{64,208},{80,224},{96,240},{112... | collective-permute-start | bytes 294920 | tf_op jit(solution)/shard_map/ppermute | solution.py:56
  241.9 23.7 %collective-permute-start.15 = (f32[96,256]{1,0:T(8,128)S(1)}, f32[96,256]{1,0:T(8,128)S(1)}, u32[]{:S(2)}, u32[]{:S(2)}) collective-permute-start(f32[96,256]{1,0:T(8,128)S(1)} %slice.93), channel_id=1, source_target_pairs={{0,112},{16,128},{32,144},{48,160},{64,176},{80,192},{96,208},{112... | collective-permute-start | bytes 294920 | tf_op jit(solution)/shard_map/ppermute | solution.py:56
  256.3 10.3 %copy-start.10 = (f32[96,256]{1,0:T(8,128)}, f32[96,256]{1,0:T(8,128)S(1)}, u32[]{:S(2)}) copy-start(f32[96,256]{1,0:T(8,128)S(1)} %collective-permute-done.19) | copy-start | bytes 294916
  256.3 13.4 %collective-permute-start.14 = (f32[96,256]{1,0:T(8,128)}, f32[96,256]{1,0:T(8,128)}, u32[]{:S(2)}, u32[]{:S(2)}) collective-permute-start(f32[96,256]{1,0:T(8,128)} %slice.92), channel_id=1, source_target_pairs={{0,80},{16,96},{32,112},{48,128},{64,144},{80,160},{96,176},{112,1... | collective-permute-start | bytes 294920 | tf_op jit(solution)/shard_map/ppermute | solution.py:56
  257.0 9.6 %copy-start.12 = (f32[96,256]{1,0:T(8,128)}, f32[96,256]{1,0:T(8,128)S(1)}, u32[]{:S(2)}) copy-start(f32[96,256]{1,0:T(8,128)S(1)} %collective-permute-done.18) | copy-start | bytes 294916
  257.0 12.8 %collective-permute-start.12 = (f32[96,256]{1,0:T(8,128)}, f32[96,256]{1,0:T(8,128)}, u32[]{:S(2)}, u32[]{:S(2)}) collective-permute-start(f32[96,256]{1,0:T(8,128)} %slice.90), channel_id=1, source_target_pairs={{0,16},{16,32},{32,48},{48,64},{64,80},{80,96},{96,112},{112,128},... | collective-permute-start | bytes 294920 | tf_op jit(solution)/shard_map/ppermute | solution.py:56
  259.7 6.9 %copy-start.14 = (f32[96,256]{1,0:T(8,128)}, f32[96,256]{1,0:T(8,128)S(1)}, u32[]{:S(2)}) copy-start(f32[96,256]{1,0:T(8,128)S(1)} %collective-permute-done.17) | copy-start | bytes 294916
  259.7 13.0 %collective-permute-start.13 = (f32[96,256]{1,0:T(8,128)}, f32[96,256]{1,0:T(8,128)}, u32[]{:S(2)}, u32[]{:S(2)}) collective-permute-start(f32[96,256]{1,0:T(8,128)} %slice.91), channel_id=1, source_target_pairs={{0,48},{16,64},{32,80},{48,96},{64,112},{80,128},{96,144},{112,160... | collective-permute-start | bytes 294920 | tf_op jit(solution)/shard_map/ppermute | solution.py:56
  262.1 4.5 %copy-start.16 = (f32[96,256]{1,0:T(8,128)}, f32[96,256]{1,0:T(8,128)S(1)}, u32[]{:S(2)}) copy-start(f32[96,256]{1,0:T(8,128)S(1)} %collective-permute-done.16) | copy-start | bytes 294916
  262.1 12.6 %collective-permute-start.11 = (f32[96,256]{1,0:T(8,128)}, f32[96,256]{1,0:T(8,128)}, u32[]{:S(2)}, u32[]{:S(2)}) collective-permute-start(f32[96,256]{1,0:T(8,128)} %slice.89), channel_id=1, source_target_pairs={{0,224},{16,240},{32,0},{48,16},{64,32},{80,48},{96,64},{112,80},{... | collective-permute-start | bytes 294920 | tf_op jit(solution)/shard_map/ppermute | solution.py:56
  265.6 1.0 copy-start.18
  265.6 10.0 %collective-permute-start.10 = (f32[96,256]{1,0:T(8,128)}, f32[96,256]{1,0:T(8,128)}, u32[]{:S(2)}, u32[]{:S(2)}) collective-permute-start(f32[96,256]{1,0:T(8,128)} %slice.88), channel_id=1, source_target_pairs={{0,192},{16,208},{32,224},{48,240},{64,0},{80,16},{96,32},{112,48}... | collective-permute-start | bytes 294920 | tf_op jit(solution)/shard_map/ppermute | solution.py:56
  266.7 17.1 %copy-start.1 = (f32[24,1,8,64,3]{3,2,4,1,0:T(8,128)S(1)}, f32[24,1,8,64,3]{3,2,4,1,0:T(8,128)}, u32[]{:S(2)}) copy-start(f32[24,1,8,64,3]{3,2,4,1,0:T(8,128)} %param.11) | copy-start | bytes 442372
  266.8 2.8 copy-start.8
  266.8 2.8 copy-start.7
  266.8 2.8 copy-start.6
  266.9 2.8 copy-start.5
  266.9 2.8 copy-start.4
  266.9 8.7 %copy-start.11 = (f32[96,256]{1,0:T(8,128)S(1)}, f32[96,256]{1,0:T(8,128)}, u32[]{:S(2)}) copy-start(f32[96,256]{1,0:T(8,128)} %copy-done.10) | copy-start | bytes 294916
  266.9 8.7 %copy-start.13 = (f32[96,256]{1,0:T(8,128)S(1)}, f32[96,256]{1,0:T(8,128)}, u32[]{:S(2)}) copy-start(f32[96,256]{1,0:T(8,128)} %copy-done.12) | copy-start | bytes 294916
  266.9 8.7 %copy-start.15 = (f32[96,256]{1,0:T(8,128)S(1)}, f32[96,256]{1,0:T(8,128)}, u32[]{:S(2)}) copy-start(f32[96,256]{1,0:T(8,128)} %copy-done.14) | copy-start | bytes 294916
  266.9 8.7 %copy-start.17 = (f32[96,256]{1,0:T(8,128)S(1)}, f32[96,256]{1,0:T(8,128)}, u32[]{:S(2)}) copy-start(f32[96,256]{1,0:T(8,128)} %copy-done.16) | copy-start | bytes 294916
  266.9 8.7 %copy-start.19 = (f32[96,256]{1,0:T(8,128)S(1)}, f32[96,256]{1,0:T(8,128)}, u32[]{:S(2)}) copy-start(f32[96,256]{1,0:T(8,128)} %copy-done.18) | copy-start | bytes 294916
  266.9 15.2 %copy-start.3 = (f32[96,512]{1,0:T(8,128)S(1)}, f32[96,512]{1,0:T(8,128)}, u32[]{:S(2)}) copy-start(f32[96,512]{1,0:T(8,128)} %get-tuple-element.26) | copy-start | bytes 589828
  269.7 7.0 %collective-permute-start.9 = (f32[96,256]{1,0:T(8,128)S(1)}, f32[96,256]{1,0:T(8,128)S(1)}, u32[]{:S(2)}, u32[]{:S(2)}) collective-permute-start(f32[96,256]{1,0:T(8,128)S(1)} %slice.87), channel_id=1, source_target_pairs={{0,160},{16,176},{32,192},{48,208},{64,224},{80,240},{96,0},{112,1... | collective-permute-start | bytes 294920 | tf_op jit(solution)/shard_map/ppermute | solution.py:56
  269.8 8.6 %collective-permute-start.8 = (f32[96,256]{1,0:T(8,128)S(1)}, f32[96,256]{1,0:T(8,128)S(1)}, u32[]{:S(2)}, u32[]{:S(2)}) collective-permute-start(f32[96,256]{1,0:T(8,128)S(1)} %slice.86), channel_id=1, source_target_pairs={{0,128},{16,144},{32,160},{48,176},{64,192},{80,208},{96,224},{112... | collective-permute-start | bytes 294920 | tf_op jit(solution)/shard_map/ppermute | solution.py:56
  272.7 6.7 %collective-permute-start.7 = (f32[96,256]{1,0:T(8,128)S(1)}, f32[96,256]{1,0:T(8,128)S(1)}, u32[]{:S(2)}, u32[]{:S(2)}) collective-permute-start(f32[96,256]{1,0:T(8,128)S(1)} %slice.85), channel_id=1, source_target_pairs={{0,96},{16,112},{32,128},{48,144},{64,160},{80,176},{96,192},{112,... | collective-permute-start | bytes 294920 | tf_op jit(solution)/shard_map/ppermute | solution.py:56
  274.7 6.6 %collective-permute-start.6 = (f32[96,256]{1,0:T(8,128)S(1)}, f32[96,256]{1,0:T(8,128)S(1)}, u32[]{:S(2)}, u32[]{:S(2)}) collective-permute-start(f32[96,256]{1,0:T(8,128)S(1)} %slice.84), channel_id=1, source_target_pairs={{0,64},{16,80},{32,96},{48,112},{64,128},{80,144},{96,160},{112,17... | collective-permute-start | bytes 294920 | tf_op jit(solution)/shard_map/ppermute | solution.py:56
  275.6 6.5 %collective-permute-start.5 = (f32[96,256]{1,0:T(8,128)S(1)}, f32[96,256]{1,0:T(8,128)S(1)}, u32[]{:S(2)}, u32[]{:S(2)}) collective-permute-start(f32[96,256]{1,0:T(8,128)S(1)} %slice.83), channel_id=1, source_target_pairs={{0,32},{16,48},{32,64},{48,80},{64,96},{80,112},{96,128},{112,144}... | collective-permute-start | bytes 294920 | tf_op jit(solution)/shard_map/ppermute | solution.py:56
Sparse Core Ops, SparseCore 0:
  50.8 93.9 reduce-scatter.1
  147.0 52.7 all-gather.1

commit v8 on v4

--- a/solution.py
+++ b/solution.py
@@ -42,6 +42,17 @@
     return both[..., :n], both[..., n:]
 
 
+def scatter_row(x):
+    n = lax.axis_size("row")
+    r = lax.axis_index("row")
+    blocks = x.reshape(n, x.shape[0] // n, *x.shape[1:])
+    total = lax.dynamic_index_in_dim(blocks, r, 0, keepdims=False)
+    for s in sorted(range(1, n), key=lambda s: -min(s, n - s)):
+        part = lax.dynamic_index_in_dim(blocks, (r + s) % n, 0, keepdims=False)
+        total = total + lax.ppermute(part, "row", [(j, (j + s) % n) for j in range(n)])
+    return total
+
+
 def ffn(tokens, up_weight, down_weight):
     i = lax.axis_index("cx")
     block, width = tokens.shape
@@ -62,7 +73,7 @@
     w2p = fetch_partner(down_weight, 0)
     w2 = jnp.concatenate([down_weight, w2p], axis=1)
     products = jnp.dot(hg, w2, preferred_element_type=jnp.float32)
-    summed = lax.psum_scatter(products, "row", scatter_dimension=0, tiled=True)
+    summed = scatter_row(products)
     own = summed[:, :width]
     other = lax.ppermute(summed[:, width:], "cx", SWAP)
     full = jnp.where(i == 0, jnp.concatenate([own, other], 0), jnp.concatenate([other, own], 0))

time: 331 us -> 279 us (0.84)
  waiting for transfers between devices: 235 us -> 168 us
  starting transfers between devices: 18.5 us -> 30.4 us
    all_to_all x1, waiting for transfers between devices: 50.5 us -> 0.01 us  [handover(): lax.all_to_all(picked, 'row', split_axis=3, concat_axis=0, tiled=True)]
    ppermute x2, waiting for transfers between devices: 13.7 us -> 0.01 us  [fetch_partner(): lax.ppermute(near, 'cx', SWAP)]
    ppermute x0 -> x7, starting transfers between devices: none -> 11.7 us  [scatter_row(): lax.ppermute(part, 'row', [(j, (j + s) % n) for j in range(n)])]
    ppermute x0 -> x7, waiting for transfers between devices: none -> 4.6 us  [scatter_row(): lax.ppermute(part, 'row', [(j, (j + s) % n) for j in range(n)])]
  transfers between devices with their start and end apart: 11 -> 17, of which waited for: 7 -> 5; matrix products, arithmetic and copies ran while one was open for 9% -> 13% of each run, Pallas kernels for 0% -> 0%
where the time goes in v8:
time: 279 us; the launch traced here: 277 us
  waiting for transfers between devices  168 us (60%)
  local copies, waits for them, and re-layouts  31.1 us (11%)
  starting transfers between devices  30.4 us (11%)
  between operations  14.3 us (5%)
  blocking collectives  13.6 us (5%)
  matrix products  11.9 us (4%)
  other arithmetic  7.85 us (3%)
    reduce_scatter x1, waiting for transfers between devices, ffn(): preact = lax.psum_scatter(partial, 'cz', scatter_dimension=0, tiled=True)  94 us
    all_gather x1, waiting for transfers between devices, ffn(): hg = lax.all_gather(hidden, 'cz', axis=0, tiled=True)  30.8 us
    all_to_all x1, waiting for transfers between devices, handover(): both = lax.all_to_all(rows, 'req', split_axis=0, concat_axis=1, tiled=True)  22.7 us
    ppermute x1, waiting for transfers between devices, ffn(): recv = lax.ppermute(theirs, 'cx', SWAP)  15.8 us
    all_gather x1, blocking collectives, ffn(): xg = lax.all_gather(xa, 'row', axis=0, tiled=True)  13.6 us
    ppermute x7, starting transfers between devices, scatter_row(): lax.ppermute(part, 'row', [(j, (j + s) % n) for j in range(n)])  11.7 us
    all_to_all x2, local copies, waits for them, and re-layouts, handover(): lax.all_to_all(picked, 'row', split_axis=3, concat_axis=0, tiled=True)  7.19 us
    dot_general x1, matrix products, ffn(): partial = jnp.dot(xg, w1, preferred_element_type=jnp.float32)  6.96 us
  transfers between devices with their start and end apart: 17, of which 5 were waited for; matrix products, arithmetic and copies ran while one was open for 13% of the time, Pallas kernels for 0%

profile of v8, /device:TPU:8, one launch (start us, length us, event | category | flops | bytes accessed | tf_op | source)
XLA Modules:
  0.0 277.2 jit_solution(1138275579670335022)
XLA Ops:
  7.2 1.8 copy.43
  9.1 0.1 fusion.28
  9.2 2.8 %collective-permute-start.2 = (bf16[256,1344]{0,1:T(8,128)(2,1)S(1)}, bf16[256,1344]{0,1:T(8,128)(2,1)}, u32[]{:S(2)}, u32[]{:S(2)}) collective-permute-start(bf16[256,1344]{0,1:T(8,128)(2,1)S(1)} %get-tuple-element.36), channel_id=1, source_target_pairs={{0,17},{17,0},{1,16},{16,1},{2,19},{19,2},{3,18},{18,3},{4,21},{21... | collective-permute-start | bytes 2064392 | tf_op jit(solution)/shard_map/ppermute | solution.py:18
  12.0 0.2 collective-permute-start.1
  12.3 1.9 collective-permute-start
  14.2 15.8 %collective-permute-done = bf16[96,256]{1,0:T(8,128)(2,1)S(1)} collective-permute-done((bf16[96,256]{1,0:T(8,128)(2,1)S(1)}, bf16[96,256]{1,0:T(8,128)(2,1)S(1)}, u32[]{:S(2)}, u32[]{:S(2)}) %collective-permute-start) | collective-permute-done | bytes 49184 | tf_op jit(solution)/shard_map/ppermute | solution.py:63
  30.0 13.6 %all_gather.6 = bf16[768,512]{1,0:T(8,128)(2,1)S(1)} all-gather(bf16[96,512]{1,0:T(8,128)(2,1)S(1)} %pad_maximum_fusion.1), channel_id=1, replica_groups=mesh['row'=8,'cx'=2,'cz'=8,'req'=2] {'row'}, dimensions={0}, use_global_device_ids=true | all-gather | bytes 884736 | tf_op jit(solution)/shard_map/all_gather | solution.py:65
  43.6 7.0 %fusion = f32[768,2688]{1,0:T(8,128)} fusion(bf16[768,512]{1,0:T(8,128)(2,1)S(1)} %all_gather.6, bf16[256,1344]{0,1:T(8,128)(2,1)} %collective-permute-done.2, bf16[256,1344]{0,1:T(8,128)(2,1)} %collective-permute-done.1, bf16[256,2688]{0,1:T(8,128)(2,1)S(1)} %copy.43), kind=kOutput, calls=%fused_computation.7 | convolution fusion | flops 2122186752 | bytes 11796480 | tf_op jit(solution)/shard_map/dot_general | solution.py:68
  50.6 0.0 all-gather.2.cloned.1.call-start
  50.7 94.0 %reduce-scatter.2.cloned.1.call-done = f32[96,2688]{1,0:T(8,128)} async-done(((f32[768,2688]{1,0:T(8,128)}), f32[96,2688]{1,0:T(8,128)}) %reduce-scatter.2.cloned.1.call-update) | async-done | bytes 1032208 | tf_op jit(solution)/shard_map/reduce_scatter | solution.py:69
  144.7 2.1 multiply_convert_fusion
  146.8 0.9 fusion.27
  147.8 2.7 collective-permute-start.4
  150.5 0.2 collective-permute-start.3
  150.7 0.2 select_reduce_fusion.1
  150.9 0.1 select_reduce_fusion.2
  151.0 0.6 gather_fusion.1
  151.6 0.7 copy.44
  152.3 4.8 %gather_fusion = f32[8,8,64,128]{3,2,1,0:T(8,128)} fusion(f32[24,8,64,128]{3,2,1,0:T(8,128)} %bitcast.76, s32[1024]{0:T(1024)S(1)} %pad_clamp_fusion.2), kind=kCustom, calls=%fused_computation | custom fusion | bytes 4194336 | tf_op jit(solution)/shard_map/gather | solution.py:36
  157.1 2.1 pad_maximum_fusion
  159.2 4.5 %copy.45 = f32[8,1,8,64,131]{4,2,0,1,3:T(8,128)} copy(f32[8,1,8,64,131]{4,3,2,0,1:T(8,128)S(1)} %pad_maximum_fusion) | data formatting | bytes 4292608 | tf_op jit(solution)/shard_map/concatenate | solution.py:36
  163.7 5.1 %all-to-all-start = ((f32[8,1,8,64,131]{4,2,0,1,3:T(8,128)}), f32[8,1,8,64,131]{4,2,0,1,3:T(8,128)}, u32[]{:S(2)}, u32[]{:S(2)}) async-start(f32[8,1,8,64,131]{4,2,0,1,3:T(8,128)} %copy.45), calls=%async_computation.1 | async-start | bytes 8388608 | tf_op jit(solution)/shard_map/all_to_all | solution.py:37
  168.8 0.1 select_reduce_fusion
  168.9 30.8 %all-gather.2.cloned.1.call-done = bf16[768,2688]{1,0:T(8,128)(2,1)} async-done(((bf16[96,2688]{1,0:T(8,128)(2,1)}), bf16[768,2688]{1,0:T(8,128)(2,1)}) %all-gather.2.cloned.1.call-update) | async-done | bytes 4128784 | tf_op jit(solution)/shard_map/all_gather | solution.py:72
  199.7 4.9 %fusion.6 = f32[768,512]{1,0:T(8,128)S(1)} fusion(bf16[768,2688]{1,0:T(8,128)(2,1)} %all-gather.2.cloned.1.call-done, bf16[1344,256]{1,0:T(8,128)(2,1)} %collective-permute-done.4, bf16[1344,256]{1,0:T(8,128)(2,1)} %collective-permute-done.3, bf16[2688,256]{1,0:T(8,128)(2,1)S(1)} %copy-done.4), kind=kOutput, calls=%fused_computation.13 | convolution fusion | flops 2122186752 | bytes 8454144 | tf_op jit(solution)/shard_map/dot_general | solution.py:75
  204.7 1.2 copy-done.2
  205.9 0.1 dynamic-slice_bitcast_fusion.6
  206.0 0.5 collective-permute-start.10
  206.5 0.7 gather_fusion.3
  207.2 0.7 gather_fusion.2
  207.9 2.3 collective-permute-start.9
  210.2 4.5 %collective-permute-start.7 = (f32[96,512]{1,0:T(8,128)S(1)}, f32[96,512]{1,0:T(8,128)}, u32[]{:S(2)}, u32[]{:S(2)}) collective-permute-start(f32[96,512]{1,0:T(8,128)S(1)} %get-tuple-element.31), channel_id=1, source_target_pairs={{0,160},{32,192},{64,224},{96,0},{128,32},{160,64},{192,96},{224,1... | collective-permute-start | bytes 589832 | tf_op jit(solution)/shard_map/ppermute | solution.py:52
  214.7 4.6 %collective-permute-done.11 = f32[96,512]{1,0:T(8,128)S(1)} collective-permute-done((f32[96,512]{1,0:T(8,128)S(1)}, f32[96,512]{1,0:T(8,128)S(1)}, u32[]{:S(2)}, u32[]{:S(2)}) %collective-permute-start.11) | collective-permute-done | bytes 196640 | tf_op jit(solution)/shard_map/ppermute | solution.py:52
  219.3 2.9 %collective-permute-start.6 = (f32[96,512]{1,0:T(8,128)S(1)}, f32[96,512]{1,0:T(8,128)}, u32[]{:S(2)}, u32[]{:S(2)}) collective-permute-start(f32[96,512]{1,0:T(8,128)S(1)} %get-tuple-element.32), channel_id=1, source_target_pairs={{0,96},{32,128},{64,160},{96,192},{128,224},{160,0},{192,32},{224,... | collective-permute-start | bytes 589832 | tf_op jit(solution)/shard_map/ppermute | solution.py:52
  222.2 1.4 collective-permute-start.5
  223.7 4.6 %copy.52 = f32[8,1,8,64,131]{4,3,2,0,1:T(8,128)S(1)} copy(f32[8,1,8,64,131]{4,2,0,1,3:T(8,128)} %all-to-all-done) | data formatting | bytes 4292608 | tf_op jit(solution)/shard_map/all_to_all | solution.py:37
  228.3 2.6 copy.47
  230.9 4.2 %gather_fusion.4 = f32[32,8,8,131]{3,2,1,0:T(8,128)} fusion(f32[64,8,8,131]{3,2,1,0:T(8,128)} %bitcast.68, s32[1024]{0:T(1024)S(1)} %pad_clamp_fusion), kind=kCustom, calls=%fused_computation.4 | custom fusion | bytes 2146432 | tf_op jit(solution)/shard_map/gather | solution.py:39
  235.1 3.9 %all-to-all-start.1 = ((f32[32,1,8,8,131]{4,3,2,1,0:T(8,128)}), f32[32,1,8,8,131]{4,3,2,1,0:T(8,128)S(1)}, u32[]{:S(2)}, u32[]{:S(2)}) async-start(f32[32,1,8,8,131]{4,3,2,1,0:T(8,128)} %bitcast.71), calls=%async_computation.2 | async-start | bytes 4194304 | tf_op jit(solution)/shard_map/all_to_all | solution.py:40
  239.1 1.6 fusion.19
  240.7 0.7 fusion.29
  241.3 1.8 collective-permute-start.12
  243.1 22.7 %all-to-all-done.1 = f32[32,1,8,8,131]{4,3,2,1,0:T(8,128)S(1)} async-done(((f32[32,1,8,8,131]{4,3,2,1,0:T(8,128)}), f32[32,1,8,8,131]{4,3,2,1,0:T(8,128)S(1)}, u32[]{:S(2)}, u32[]{:S(2)}) %all-to-all-start.1) | async-done | bytes 1073184 | tf_op jit(solution)/shard_map/all_to_all | solution.py:40
  265.9 0.1 slice.28
  265.9 0.1 slice.29
  266.0 1.1 copy.49
  267.1 1.6 copy.50
  268.7 1.6 fusion.13
  (50 shorter events, 0.3 us)
Async XLA Ops:
  7.2 143.9 %copy-start = (f32[24,1,8,64,3]{3,2,4,1,0:T(8,128)S(1)}, f32[24,1,8,64,3]{3,2,4,1,0:T(8,128)}, u32[]{:S(2)}) copy-start(f32[24,1,8,64,3]{3,2,4,1,0:T(8,128)} %param.11) | copy-start | bytes 442372
  7.2 5.1 %copy-start.5 = (bf16[192,256]{1,0:T(8,128)(2,1)S(1)}, bf16[192,256]{1,0:T(8,128)(2,1)}, u32[]{:S(2)}) copy-start(bf16[192,256]{1,0:T(8,128)(2,1)} %param.7) | copy-start | bytes 294916
  7.2 137.5 %reduce-scatter.2.cloned.1.call-start = ((), (), s32[]{:S(2)}) async-start(), calls=%async_computation.3 | async-start | bytes 9289728 | tf_op jit(solution)/shard_map/reduce_scatter | solution.py:69
  9.2 34.4 %collective-permute-start.2 = (bf16[256,1344]{0,1:T(8,128)(2,1)S(1)}, bf16[256,1344]{0,1:T(8,128)(2,1)}, u32[]{:S(2)}, u32[]{:S(2)}) collective-permute-start(bf16[256,1344]{0,1:T(8,128)(2,1)S(1)} %get-tuple-element.36), channel_id=1, source_target_pairs={{0,17},{17,0},{1,16},{16,1},{2,19},{19,2},{3,18},{18,3},{4,21},{21... | collective-permute-start | bytes 2064392 | tf_op jit(solution)/shard_map/ppermute | solution.py:18
  12.0 31.6 %collective-permute-start.1 = (bf16[256,1344]{0,1:T(8,128)(2,1)S(1)}, bf16[256,1344]{0,1:T(8,128)(2,1)}, u32[]{:S(2)}, u32[]{:S(2)}) collective-permute-start(bf16[256,1344]{0,1:T(8,128)(2,1)S(1)} %get-tuple-element.35), channel_id=1, source_target_pairs={{0,16},{16,0},{1,17},{17,1},{2,18},{18,2},{3,19},{19,3},{4,20},{20... | collective-permute-start | bytes 2064392 | tf_op jit(solution)/shard_map/ppermute | solution.py:18
  12.3 17.7 %collective-permute-start = (bf16[96,256]{1,0:T(8,128)(2,1)S(1)}, bf16[96,256]{1,0:T(8,128)(2,1)S(1)}, u32[]{:S(2)}, u32[]{:S(2)}) collective-permute-start(bf16[96,256]{1,0:T(8,128)(2,1)S(1)} %get-tuple-element.40), channel_id=1, source_target_pairs={{0,16},{16,0},{1,17},{17,1},{2,18},{18,2},{3,19},{19,3},{4,20},{20... | collective-permute-start | bytes 147464 | tf_op jit(solution)/shard_map/ppermute | solution.py:63
  50.6 96.2 %copy-start.3 = (bf16[2688,256]{1,0:T(8,128)(2,1)S(1)}, bf16[2688,256]{1,0:T(8,128)(2,1)}, u32[]{:S(2)}) copy-start(bf16[2688,256]{1,0:T(8,128)(2,1)} %param.9) | copy-start | bytes 4128772
  50.6 100.1 %copy-start.10 = (s32[32]{0:T(128)S(1)}, s32[32]{0:T(128)}, u32[]{:S(2)}) copy-start(s32[32]{0:T(128)} %param.12) | copy-start | bytes 388
  50.6 149.1 %all-gather.2.cloned.1.call-start = ((), (), s32[]{:S(2)}) async-start(), calls=%async_computation.4 | async-start | bytes 4644864 | tf_op jit(solution)/shard_map/all_gather | solution.py:72
  147.8 21.2 %collective-permute-start.4 = (bf16[1344,256]{1,0:T(8,128)(2,1)}, bf16[1344,256]{1,0:T(8,128)(2,1)}, u32[]{:S(2)}, u32[]{:S(2)}) collective-permute-start(bf16[1344,256]{1,0:T(8,128)(2,1)} %get-tuple-element.34), channel_id=1, source_target_pairs={{0,17},{17,0},{1,16},{16,1},{2,19},{19,2},{3,18},{18,3},{4,21},{21... | collective-permute-start | bytes 2064392 | tf_op jit(solution)/shard_map/ppermute | solution.py:18
  150.5 18.5 %collective-permute-start.3 = (bf16[1344,256]{1,0:T(8,128)(2,1)S(1)}, bf16[1344,256]{1,0:T(8,128)(2,1)}, u32[]{:S(2)}, u32[]{:S(2)}) collective-permute-start(bf16[1344,256]{1,0:T(8,128)(2,1)S(1)} %get-tuple-element.33), channel_id=1, source_target_pairs={{0,16},{16,0},{1,17},{17,1},{2,18},{18,2},{3,19},{19,3},{4,20},{20... | collective-permute-start | bytes 2064392 | tf_op jit(solution)/shard_map/ppermute | solution.py:18
  163.7 5.1 %copy-start.11 = (s32[32]{0:T(128)S(1)}, s32[32]{0:T(128)}, u32[]{:S(2)}) copy-start(s32[32]{0:T(128)} %param.13) | copy-start | bytes 388
  163.7 36.1 %copy-start.4 = (bf16[2688,256]{1,0:T(8,128)(2,1)S(1)}, bf16[2688,256]{1,0:T(8,128)(2,1)}, u32[]{:S(2)}) copy-start(bf16[2688,256]{1,0:T(8,128)(2,1)} %param.9) | copy-start | bytes 4128772
  163.7 60.0 %all-to-all-start = ((f32[8,1,8,64,131]{4,2,0,1,3:T(8,128)}), f32[8,1,8,64,131]{4,2,0,1,3:T(8,128)}, u32[]{:S(2)}, u32[]{:S(2)}) async-start(f32[8,1,8,64,131]{4,2,0,1,3:T(8,128)} %copy.45), calls=%async_computation.1 | async-start | bytes 8388608 | tf_op jit(solution)/shard_map/all_to_all | solution.py:37
  204.7 1.2 copy-start.2
  206.0 13.3 %collective-permute-start.11 = (f32[96,512]{1,0:T(8,128)S(1)}, f32[96,512]{1,0:T(8,128)S(1)}, u32[]{:S(2)}, u32[]{:S(2)}) collective-permute-start(f32[96,512]{1,0:T(8,128)S(1)} %get-tuple-element.27), channel_id=1, source_target_pairs={{0,224},{32,0},{64,32},{96,64},{128,96},{160,128},{192,160},{224,1... | collective-permute-start | bytes 589832 | tf_op jit(solution)/shard_map/ppermute | solution.py:52
  206.0 16.2 %collective-permute-start.10 = (f32[96,512]{1,0:T(8,128)S(1)}, f32[96,512]{1,0:T(8,128)S(1)}, u32[]{:S(2)}, u32[]{:S(2)}) collective-permute-start(f32[96,512]{1,0:T(8,128)S(1)} %get-tuple-element.28), channel_id=1, source_target_pairs={{0,32},{32,64},{64,96},{96,128},{128,160},{160,192},{192,224},{224... | collective-permute-start | bytes 589832 | tf_op jit(solution)/shard_map/ppermute | solution.py:52
  207.9 31.1 %collective-permute-start.9 = (f32[96,512]{1,0:T(8,128)S(1)}, f32[96,512]{1,0:T(8,128)}, u32[]{:S(2)}, u32[]{:S(2)}) collective-permute-start(f32[96,512]{1,0:T(8,128)S(1)} %get-tuple-element.29), channel_id=1, source_target_pairs={{0,192},{32,224},{64,0},{96,32},{128,64},{160,96},{192,128},{224,1... | collective-permute-start | bytes 589832 | tf_op jit(solution)/shard_map/ppermute | solution.py:52
  210.2 28.8 %collective-permute-start.8 = (f32[96,512]{1,0:T(8,128)S(1)}, f32[96,512]{1,0:T(8,128)}, u32[]{:S(2)}, u32[]{:S(2)}) collective-permute-start(f32[96,512]{1,0:T(8,128)S(1)} %get-tuple-element.30), channel_id=1, source_target_pairs={{0,64},{32,96},{64,128},{96,160},{128,192},{160,224},{192,0},{224,... | collective-permute-start | bytes 589832 | tf_op jit(solution)/shard_map/ppermute | solution.py:52
  210.2 28.8 %collective-permute-start.7 = (f32[96,512]{1,0:T(8,128)S(1)}, f32[96,512]{1,0:T(8,128)}, u32[]{:S(2)}, u32[]{:S(2)}) collective-permute-start(f32[96,512]{1,0:T(8,128)S(1)} %get-tuple-element.31), channel_id=1, source_target_pairs={{0,160},{32,192},{64,224},{96,0},{128,32},{160,64},{192,96},{224,1... | collective-permute-start | bytes 589832 | tf_op jit(solution)/shard_map/ppermute | solution.py:52
  219.3 9.0 %copy-start.7 = (f32[96,512]{1,0:T(8,128)}, f32[96,512]{1,0:T(8,128)S(1)}, u32[]{:S(2)}) copy-start(f32[96,512]{1,0:T(8,128)S(1)} %collective-permute-done.11) | copy-start | bytes 589828
  219.3 19.8 %collective-permute-start.6 = (f32[96,512]{1,0:T(8,128)S(1)}, f32[96,512]{1,0:T(8,128)}, u32[]{:S(2)}, u32[]{:S(2)}) collective-permute-start(f32[96,512]{1,0:T(8,128)S(1)} %get-tuple-element.32), channel_id=1, source_target_pairs={{0,96},{32,128},{64,160},{96,192},{128,224},{160,0},{192,32},{224,... | collective-permute-start | bytes 589832 | tf_op jit(solution)/shard_map/ppermute | solution.py:52
  222.2 6.1 %copy-start.9 = (f32[96,512]{1,0:T(8,128)}, f32[96,512]{1,0:T(8,128)S(1)}, u32[]{:S(2)}) copy-start(f32[96,512]{1,0:T(8,128)S(1)} %collective-permute-done.10) | copy-start | bytes 589828
  222.2 16.9 %collective-permute-start.5 = (f32[96,512]{1,0:T(8,128)S(1)}, f32[96,512]{1,0:T(8,128)}, u32[]{:S(2)}, u32[]{:S(2)}) collective-permute-start(f32[96,512]{1,0:T(8,128)S(1)} %get-tuple-element.26), channel_id=1, source_target_pairs={{0,128},{32,160},{64,192},{96,224},{128,0},{160,32},{192,64},{224,... | collective-permute-start | bytes 589832 | tf_op jit(solution)/shard_map/ppermute | solution.py:52
  235.1 4.0 %copy-start.8 = (f32[96,512]{1,0:T(8,128)S(1)}, f32[96,512]{1,0:T(8,128)}, u32[]{:S(2)}) copy-start(f32[96,512]{1,0:T(8,128)} %copy-done.7) | copy-start | bytes 589828
  235.1 30.7 %all-to-all-start.1 = ((f32[32,1,8,8,131]{4,3,2,1,0:T(8,128)}), f32[32,1,8,8,131]{4,3,2,1,0:T(8,128)S(1)}, u32[]{:S(2)}, u32[]{:S(2)}) async-start(f32[32,1,8,8,131]{4,3,2,1,0:T(8,128)} %bitcast.71), calls=%async_computation.2 | async-start | bytes 4194304 | tf_op jit(solution)/shard_map/all_to_all | solution.py:40
  241.3 27.3 %collective-permute-start.12 = (f32[96,256]{1,0:T(8,128)}, f32[96,256]{1,0:T(8,128)}, u32[]{:S(2)}, u32[]{:S(2)}) collective-permute-start(f32[96,256]{1,0:T(8,128)} %get-tuple-element.38), channel_id=1, source_target_pairs={{0,16},{16,0},{1,17},{17,1},{2,18},{18,2},{3,19},{19,3},{4,20},{20... | collective-permute-start | bytes 294920 | tf_op jit(solution)/shard_map/ppermute | solution.py:78
  265.8 4.5 %copy-start.1 = (f32[24,1,8,64,3]{3,2,4,1,0:T(8,128)S(1)}, f32[24,1,8,64,3]{3,2,4,1,0:T(8,128)}, u32[]{:S(2)}) copy-start(f32[24,1,8,64,3]{3,2,4,1,0:T(8,128)} %param.11) | copy-start | bytes 442372
  266.0 2.7 copy-start.6
Sparse Core Ops, SparseCore 0:
  50.7 93.9 reduce-scatter.1
  146.9 52.7 all-gather.1

commit v9 on v8

--- a/solution.py
+++ b/solution.py
@@ -46,11 +46,11 @@
     n = lax.axis_size("row")
     r = lax.axis_index("row")
     blocks = x.reshape(n, x.shape[0] // n, *x.shape[1:])
-    total = lax.dynamic_index_in_dim(blocks, r, 0, keepdims=False)
+    pieces = [lax.dynamic_index_in_dim(blocks, r, 0, keepdims=False)]
     for s in sorted(range(1, n), key=lambda s: -min(s, n - s)):
         part = lax.dynamic_index_in_dim(blocks, (r + s) % n, 0, keepdims=False)
-        total = total + lax.ppermute(part, "row", [(j, (j + s) % n) for j in range(n)])
-    return total
+        pieces.append(lax.ppermute(part, "row", [(j, (j + s) % n) for j in range(n)]))
+    return pieces
 
 
 def ffn(tokens, up_weight, down_weight):
@@ -73,9 +73,9 @@
     w2p = fetch_partner(down_weight, 0)
     w2 = jnp.concatenate([down_weight, w2p], axis=1)
     products = jnp.dot(hg, w2, preferred_element_type=jnp.float32)
-    summed = scatter_row(products)
-    own = summed[:, :width]
-    other = lax.ppermute(summed[:, width:], "cx", SWAP)
+    pieces = scatter_row(products)
+    other = lax.ppermute(sum(p[:, width:] for p in pieces), "cx", SWAP)
+    own = sum(p[:, :width] for p in pieces)
     full = jnp.where(i == 0, jnp.concatenate([own, other], 0), jnp.concatenate([other, own], 0))
     return (tokens.astype(jnp.float32) + full).astype(jnp.bfloat16)
 

time: 279 us -> 275 us (0.986)
    all_gather x1, waiting for transfers between devices: 30.8 us -> 14.8 us  [ffn(): hg = lax.all_gather(hidden, 'cz', axis=0, tiled=True)]
    ppermute x2, waiting for transfers between devices: 0.01 us -> 14.3 us  [fetch_partner(): lax.ppermute(far, ('cx', 'req'), CROSS)]
    unnamed x27 -> x19, local copies, waits for them, and re-layouts: 5.72 us -> 4.51 us
  transfers between devices with their start and end apart: 17 -> 17, of which waited for: 5 -> 7; matrix products, arithmetic and copies ran while one was open for 13% -> 13% of each run, Pallas kernels for 0% -> 0%
where the time goes in v9:
time: 275 us; the launch traced here: 273 us
  waiting for transfers between devices  166 us (60%)
  starting transfers between devices  29.8 us (11%)
  local copies, waits for them, and re-layouts  29 us (11%)
  between operations  14.3 us (5%)
  blocking collectives  13.6 us (5%)
  matrix products  11.9 us (4%)
  other arithmetic  8.33 us (3%)
    reduce_scatter x1, waiting for transfers between devices, ffn(): preact = lax.psum_scatter(partial, 'cz', scatter_dimension=0, tiled=True)  94.1 us
    all_to_all x1, waiting for transfers between devices, handover(): both = lax.all_to_all(rows, 'req', split_axis=0, concat_axis=1, tiled=True)  23.4 us
    ppermute x1, waiting for transfers between devices, ffn(): recv = lax.ppermute(theirs, 'cx', SWAP)  15.8 us
    all_gather x1, waiting for transfers between devices, ffn(): hg = lax.all_gather(hidden, 'cz', axis=0, tiled=True)  14.8 us
    ppermute x2, waiting for transfers between devices, fetch_partner(): lax.ppermute(far, ('cx', 'req'), CROSS)  14.3 us
    all_gather x1, blocking collectives, ffn(): xg = lax.all_gather(xa, 'row', axis=0, tiled=True)  13.6 us
    ppermute x7, starting transfers between devices, scatter_row(): lax.ppermute(part, 'row', [(j, (j + s) % n) for j in range(n)])  11.4 us
    all_to_all x2, local copies, waits for them, and re-layouts, handover(): lax.all_to_all(picked, 'row', split_axis=3, concat_axis=0, tiled=True)  7.18 us
  transfers between devices with their start and end apart: 17, of which 7 were waited for; matrix products, arithmetic and copies ran while one was open for 13% of the time, Pallas kernels for 0%

profile of v9, /device:TPU:8, one launch (start us, length us, event | category | flops | bytes accessed | tf_op | source)
XLA Modules:
  0.0 273.2 jit_solution(11837035669664196324)
XLA Ops:
  7.2 1.8 copy.43
  9.1 0.1 fusion.22
  9.2 2.8 %collective-permute-start.2 = (bf16[256,1344]{0,1:T(8,128)(2,1)S(1)}, bf16[256,1344]{0,1:T(8,128)(2,1)}, u32[]{:S(2)}, u32[]{:S(2)}) collective-permute-start(bf16[256,1344]{0,1:T(8,128)(2,1)S(1)} %get-tuple-element.39), channel_id=1, source_target_pairs={{0,17},{17,0},{1,16},{16,1},{2,19},{19,2},{3,18},{18,3},{4,21},{21... | collective-permute-start | bytes 2064392 | tf_op jit(solution)/shard_map/ppermute | solution.py:18
  12.0 0.2 collective-permute-start.1
  12.3 1.9 collective-permute-start
  14.2 15.8 %collective-permute-done = bf16[96,256]{1,0:T(8,128)(2,1)S(1)} collective-permute-done((bf16[96,256]{1,0:T(8,128)(2,1)S(1)}, bf16[96,256]{1,0:T(8,128)(2,1)S(1)}, u32[]{:S(2)}, u32[]{:S(2)}) %collective-permute-start) | collective-permute-done | bytes 49184 | tf_op jit(solution)/shard_map/ppermute | solution.py:63
  30.0 13.6 %all_gather.6 = bf16[768,512]{1,0:T(8,128)(2,1)S(1)} all-gather(bf16[96,512]{1,0:T(8,128)(2,1)S(1)} %pad_maximum_fusion.1), channel_id=1, replica_groups=mesh['row'=8,'cx'=2,'cz'=8,'req'=2] {'row'}, dimensions={0}, use_global_device_ids=true | all-gather | bytes 884736 | tf_op jit(solution)/shard_map/all_gather | solution.py:65
  43.6 6.9 %fusion = f32[768,2688]{1,0:T(8,128)} fusion(bf16[768,512]{1,0:T(8,128)(2,1)S(1)} %all_gather.6, bf16[256,1344]{0,1:T(8,128)(2,1)} %collective-permute-done.2, bf16[256,1344]{0,1:T(8,128)(2,1)} %collective-permute-done.1, bf16[256,2688]{0,1:T(8,128)(2,1)S(1)} %copy.43), kind=kOutput, calls=%fused_computation.7 | convolution fusion | flops 2122186752 | bytes 11796480 | tf_op jit(solution)/shard_map/dot_general | solution.py:68
  50.6 0.0 all-gather.2.cloned.1.call-start
  50.6 94.1 %reduce-scatter.2.cloned.1.call-done = f32[96,2688]{1,0:T(8,128)} async-done(((f32[768,2688]{1,0:T(8,128)}), f32[96,2688]{1,0:T(8,128)}) %reduce-scatter.2.cloned.1.call-update) | async-done | bytes 1032208 | tf_op jit(solution)/shard_map/reduce_scatter | solution.py:69
  144.7 2.1 multiply_convert_fusion
  146.8 0.2 select_reduce_fusion.1
  147.0 0.1 select_reduce_fusion.2
  147.2 0.6 gather_fusion.1
  147.7 0.7 copy.44
  148.5 4.8 %gather_fusion = f32[8,8,64,128]{3,2,1,0:T(8,128)} fusion(f32[24,8,64,128]{3,2,1,0:T(8,128)} %bitcast.63, s32[1024]{0:T(1024)S(1)} %pad_clamp_fusion.2), kind=kCustom, calls=%fused_computation | custom fusion | bytes 4194336 | tf_op jit(solution)/shard_map/gather | solution.py:36
  153.3 2.0 pad_maximum_fusion
  155.3 4.4 %copy.45 = f32[8,1,8,64,131]{4,2,0,1,3:T(8,128)} copy(f32[8,1,8,64,131]{4,3,2,0,1:T(8,128)S(1)} %pad_maximum_fusion) | data formatting | bytes 4292608 | tf_op jit(solution)/shard_map/concatenate | solution.py:36
  159.8 5.1 %all-to-all-start = ((f32[8,1,8,64,131]{4,2,0,1,3:T(8,128)}), f32[8,1,8,64,131]{4,2,0,1,3:T(8,128)}, u32[]{:S(2)}, u32[]{:S(2)}) async-start(f32[8,1,8,64,131]{4,2,0,1,3:T(8,128)} %copy.45), calls=%async_computation.1 | async-start | bytes 8388608 | tf_op jit(solution)/shard_map/all_to_all | solution.py:37
  164.9 0.1 fusion.21
  164.9 2.8 %collective-permute-start.4 = (bf16[1344,256]{1,0:T(8,128)(2,1)S(1)}, bf16[1344,256]{1,0:T(8,128)(2,1)}, u32[]{:S(2)}, u32[]{:S(2)}) collective-permute-start(bf16[1344,256]{1,0:T(8,128)(2,1)S(1)} %get-tuple-element.37), channel_id=1, source_target_pairs={{0,17},{17,0},{1,16},{16,1},{2,19},{19,2},{3,18},{18,3},{4,21},{21... | collective-permute-start | bytes 2064392 | tf_op jit(solution)/shard_map/ppermute | solution.py:18
  167.7 0.2 collective-permute-start.3
  168.0 0.1 select_reduce_fusion
  168.1 0.7 gather_fusion.3
  168.8 0.7 gather_fusion.2
  169.6 14.3 %collective-permute-done.4 = bf16[1344,256]{1,0:T(8,128)(2,1)} collective-permute-done((bf16[1344,256]{1,0:T(8,128)(2,1)S(1)}, bf16[1344,256]{1,0:T(8,128)(2,1)}, u32[]{:S(2)}, u32[]{:S(2)}) %collective-permute-start.4) | collective-permute-done | bytes 688160 | tf_op jit(solution)/shard_map/ppermute | solution.py:18
  183.8 1.2 collective-permute-done.3
  185.0 14.8 %all-gather.2.cloned.1.call-done = bf16[768,2688]{1,0:T(8,128)(2,1)} async-done(((bf16[96,2688]{1,0:T(8,128)(2,1)}), bf16[768,2688]{1,0:T(8,128)(2,1)}) %all-gather.2.cloned.1.call-update) | async-done | bytes 4128784 | tf_op jit(solution)/shard_map/all_gather | solution.py:72
  199.9 4.9 %fusion.6 = f32[768,512]{1,0:T(8,128)S(1)} fusion(bf16[768,2688]{1,0:T(8,128)(2,1)} %all-gather.2.cloned.1.call-done, bf16[1344,256]{1,0:T(8,128)(2,1)} %collective-permute-done.4, bf16[1344,256]{1,0:T(8,128)(2,1)} %collective-permute-done.3, bf16[2688,256]{1,0:T(8,128)(2,1)S(1)} %copy-done.2), kind=kOutput, calls=%fused_computation.13 | convolution fusion | flops 2122186752 | bytes 8454144 | tf_op jit(solution)/shard_map/dot_general | solution.py:75
  204.8 0.8 dynamic-slice_bitcast_fusion.7
  205.7 0.5 collective-permute-start.10
  206.2 2.0 collective-permute-start.9
  208.2 4.5 %collective-permute-start.7 = (f32[96,512]{1,0:T(8,128)S(1)}, f32[96,512]{1,0:T(8,128)}, u32[]{:S(2)}, u32[]{:S(2)}) collective-permute-start(f32[96,512]{1,0:T(8,128)S(1)} %get-tuple-element.33), channel_id=1, source_target_pairs={{0,160},{32,192},{64,224},{96,0},{128,32},{160,64},{192,96},{224,1... | collective-permute-start | bytes 589832 | tf_op jit(solution)/shard_map/ppermute | solution.py:52
  212.7 2.7 collective-permute-done.11
  215.3 2.9 %collective-permute-start.6 = (f32[96,512]{1,0:T(8,128)S(1)}, f32[96,512]{1,0:T(8,128)}, u32[]{:S(2)}, u32[]{:S(2)}) collective-permute-start(f32[96,512]{1,0:T(8,128)S(1)} %get-tuple-element.34), channel_id=1, source_target_pairs={{0,96},{32,128},{64,160},{96,192},{128,224},{160,0},{192,32},{224,... | collective-permute-start | bytes 589832 | tf_op jit(solution)/shard_map/ppermute | solution.py:52
  218.3 1.4 collective-permute-start.5
  219.7 4.6 %copy.52 = f32[8,1,8,64,131]{4,3,2,0,1:T(8,128)S(1)} copy(f32[8,1,8,64,131]{4,2,0,1,3:T(8,128)} %all-to-all-done) | data formatting | bytes 4292608 | tf_op jit(solution)/shard_map/all_to_all | solution.py:37
  224.4 2.6 copy.47
  226.9 4.2 %gather_fusion.4 = f32[32,8,8,131]{3,2,1,0:T(8,128)} fusion(f32[64,8,8,131]{3,2,1,0:T(8,128)} %bitcast.56, s32[1024]{0:T(1024)S(1)} %pad_clamp_fusion), kind=kCustom, calls=%fused_computation.4 | custom fusion | bytes 2146432 | tf_op jit(solution)/shard_map/gather | solution.py:39
  231.1 4.3 %all-to-all-start.1 = ((f32[32,1,8,8,131]{4,3,2,1,0:T(8,128)}), f32[32,1,8,8,131]{4,3,2,1,0:T(8,128)S(1)}, u32[]{:S(2)}, u32[]{:S(2)}) async-start(f32[32,1,8,8,131]{4,3,2,1,0:T(8,128)} %bitcast.59), calls=%async_computation.2 | async-start | bytes 4194304 | tf_op jit(solution)/shard_map/all_to_all | solution.py:40
  235.4 2.1 slice_add_fusion.7
  237.5 1.0 collective-permute-start.12
  238.5 23.4 %all-to-all-done.1 = f32[32,1,8,8,131]{4,3,2,1,0:T(8,128)S(1)} async-done(((f32[32,1,8,8,131]{4,3,2,1,0:T(8,128)}), f32[32,1,8,8,131]{4,3,2,1,0:T(8,128)S(1)}, u32[]{:S(2)}, u32[]{:S(2)}) %all-to-all-start.1) | async-done | bytes 1073184 | tf_op jit(solution)/shard_map/all_to_all | solution.py:40
  261.9 0.1 slice.98
  262.0 0.1 slice.99
  262.1 1.1 copy.49
  263.2 1.5 copy.50
  264.8 1.6 fusion.13
  (41 shorter events, 0.2 us)
Async XLA Ops:
  7.2 140.0 %copy-start = (f32[24,1,8,64,3]{3,2,4,1,0:T(8,128)S(1)}, f32[24,1,8,64,3]{3,2,4,1,0:T(8,128)}, u32[]{:S(2)}) copy-start(f32[24,1,8,64,3]{3,2,4,1,0:T(8,128)} %param.11) | copy-start | bytes 442372
  7.2 5.1 %copy-start.3 = (bf16[192,256]{1,0:T(8,128)(2,1)S(1)}, bf16[192,256]{1,0:T(8,128)(2,1)}, u32[]{:S(2)}) copy-start(bf16[192,256]{1,0:T(8,128)(2,1)} %param.7) | copy-start | bytes 294916
  7.2 137.5 %reduce-scatter.2.cloned.1.call-start = ((), (), s32[]{:S(2)}) async-start(), calls=%async_computation.3 | async-start | bytes 9289728 | tf_op jit(solution)/shard_map/reduce_scatter | solution.py:69
  9.2 34.4 %collective-permute-start.2 = (bf16[256,1344]{0,1:T(8,128)(2,1)S(1)}, bf16[256,1344]{0,1:T(8,128)(2,1)}, u32[]{:S(2)}, u32[]{:S(2)}) collective-permute-start(bf16[256,1344]{0,1:T(8,128)(2,1)S(1)} %get-tuple-element.39), channel_id=1, source_target_pairs={{0,17},{17,0},{1,16},{16,1},{2,19},{19,2},{3,18},{18,3},{4,21},{21... | collective-permute-start | bytes 2064392 | tf_op jit(solution)/shard_map/ppermute | solution.py:18
  12.0 31.6 %collective-permute-start.1 = (bf16[256,1344]{0,1:T(8,128)(2,1)S(1)}, bf16[256,1344]{0,1:T(8,128)(2,1)}, u32[]{:S(2)}, u32[]{:S(2)}) collective-permute-start(bf16[256,1344]{0,1:T(8,128)(2,1)S(1)} %get-tuple-element.38), channel_id=1, source_target_pairs={{0,16},{16,0},{1,17},{17,1},{2,18},{18,2},{3,19},{19,3},{4,20},{20... | collective-permute-start | bytes 2064392 | tf_op jit(solution)/shard_map/ppermute | solution.py:18
  12.3 17.7 %collective-permute-start = (bf16[96,256]{1,0:T(8,128)(2,1)S(1)}, bf16[96,256]{1,0:T(8,128)(2,1)S(1)}, u32[]{:S(2)}, u32[]{:S(2)}) collective-permute-start(bf16[96,256]{1,0:T(8,128)(2,1)S(1)} %get-tuple-element.41), channel_id=1, source_target_pairs={{0,16},{16,0},{1,17},{17,1},{2,18},{18,2},{3,19},{19,3},{4,20},{20... | collective-permute-start | bytes 147464 | tf_op jit(solution)/shard_map/ppermute | solution.py:63
  50.6 96.2 %copy-start.6 = (s32[32]{0:T(128)S(1)}, s32[32]{0:T(128)}, u32[]{:S(2)}) copy-start(s32[32]{0:T(128)} %param.12) | copy-start | bytes 388
  50.6 149.3 %all-gather.2.cloned.1.call-start = ((), (), s32[]{:S(2)}) async-start(), calls=%async_computation.4 | async-start | bytes 4644864 | tf_op jit(solution)/shard_map/all_gather | solution.py:72
  159.8 5.1 %copy-start.2 = (bf16[2688,256]{1,0:T(8,128)(2,1)S(1)}, bf16[2688,256]{1,0:T(8,128)(2,1)}, u32[]{:S(2)}) copy-start(bf16[2688,256]{1,0:T(8,128)(2,1)} %param.9) | copy-start | bytes 4128772
  159.8 60.0 %all-to-all-start = ((f32[8,1,8,64,131]{4,2,0,1,3:T(8,128)}), f32[8,1,8,64,131]{4,2,0,1,3:T(8,128)}, u32[]{:S(2)}, u32[]{:S(2)}) async-start(f32[8,1,8,64,131]{4,2,0,1,3:T(8,128)} %copy.45), calls=%async_computation.1 | async-start | bytes 8388608 | tf_op jit(solution)/shard_map/all_to_all | solution.py:37
  164.9 3.1 %copy-start.7 = (s32[32]{0:T(128)S(1)}, s32[32]{0:T(128)}, u32[]{:S(2)}) copy-start(s32[32]{0:T(128)} %param.13) | copy-start | bytes 388
  164.9 18.9 %collective-permute-start.4 = (bf16[1344,256]{1,0:T(8,128)(2,1)S(1)}, bf16[1344,256]{1,0:T(8,128)(2,1)}, u32[]{:S(2)}, u32[]{:S(2)}) collective-permute-start(bf16[1344,256]{1,0:T(8,128)(2,1)S(1)} %get-tuple-element.37), channel_id=1, source_target_pairs={{0,17},{17,0},{1,16},{16,1},{2,19},{19,2},{3,18},{18,3},{4,21},{21... | collective-permute-start | bytes 2064392 | tf_op jit(solution)/shard_map/ppermute | solution.py:18
  167.7 17.3 %collective-permute-start.3 = (bf16[1344,256]{1,0:T(8,128)(2,1)S(1)}, bf16[1344,256]{1,0:T(8,128)(2,1)}, u32[]{:S(2)}, u32[]{:S(2)}) collective-permute-start(bf16[1344,256]{1,0:T(8,128)(2,1)S(1)} %get-tuple-element.36), channel_id=1, source_target_pairs={{0,16},{16,0},{1,17},{17,1},{2,18},{18,2},{3,19},{19,3},{4,20},{20... | collective-permute-start | bytes 2064392 | tf_op jit(solution)/shard_map/ppermute | solution.py:18
  205.6 9.7 %collective-permute-start.11 = (f32[96,512]{1,0:T(8,128)S(1)}, f32[96,512]{1,0:T(8,128)S(1)}, u32[]{:S(2)}, u32[]{:S(2)}) collective-permute-start(f32[96,512]{1,0:T(8,128)S(1)} %get-tuple-element.29), channel_id=1, source_target_pairs={{0,224},{32,0},{64,32},{96,64},{128,96},{160,128},{192,160},{224,1... | collective-permute-start | bytes 589832 | tf_op jit(solution)/shard_map/ppermute | solution.py:52
  205.7 12.6 %collective-permute-start.10 = (f32[96,512]{1,0:T(8,128)S(1)}, f32[96,512]{1,0:T(8,128)S(1)}, u32[]{:S(2)}, u32[]{:S(2)}) collective-permute-start(f32[96,512]{1,0:T(8,128)S(1)} %get-tuple-element.30), channel_id=1, source_target_pairs={{0,32},{32,64},{64,96},{96,128},{128,160},{160,192},{192,224},{224... | collective-permute-start | bytes 589832 | tf_op jit(solution)/shard_map/ppermute | solution.py:52
  206.2 29.2 %collective-permute-start.9 = (f32[96,512]{1,0:T(8,128)}, f32[96,512]{1,0:T(8,128)}, u32[]{:S(2)}, u32[]{:S(2)}) collective-permute-start(f32[96,512]{1,0:T(8,128)} %get-tuple-element.31), channel_id=1, source_target_pairs={{0,192},{32,224},{64,0},{96,32},{128,64},{160,96},{192,128},{224,1... | collective-permute-start | bytes 589832 | tf_op jit(solution)/shard_map/ppermute | solution.py:52
  208.2 27.2 %collective-permute-start.8 = (f32[96,512]{1,0:T(8,128)S(1)}, f32[96,512]{1,0:T(8,128)}, u32[]{:S(2)}, u32[]{:S(2)}) collective-permute-start(f32[96,512]{1,0:T(8,128)S(1)} %get-tuple-element.32), channel_id=1, source_target_pairs={{0,64},{32,96},{64,128},{96,160},{128,192},{160,224},{192,0},{224,... | collective-permute-start | bytes 589832 | tf_op jit(solution)/shard_map/ppermute | solution.py:52
  208.2 27.2 %collective-permute-start.7 = (f32[96,512]{1,0:T(8,128)S(1)}, f32[96,512]{1,0:T(8,128)}, u32[]{:S(2)}, u32[]{:S(2)}) collective-permute-start(f32[96,512]{1,0:T(8,128)S(1)} %get-tuple-element.33), channel_id=1, source_target_pairs={{0,160},{32,192},{64,224},{96,0},{128,32},{160,64},{192,96},{224,1... | collective-permute-start | bytes 589832 | tf_op jit(solution)/shard_map/ppermute | solution.py:52
  215.3 20.1 %collective-permute-start.6 = (f32[96,512]{1,0:T(8,128)S(1)}, f32[96,512]{1,0:T(8,128)}, u32[]{:S(2)}, u32[]{:S(2)}) collective-permute-start(f32[96,512]{1,0:T(8,128)S(1)} %get-tuple-element.34), channel_id=1, source_target_pairs={{0,96},{32,128},{64,160},{96,192},{128,224},{160,0},{192,32},{224,... | collective-permute-start | bytes 589832 | tf_op jit(solution)/shard_map/ppermute | solution.py:52
  218.3 1.4 copy-start.5
  218.3 17.1 %collective-permute-start.5 = (f32[96,512]{1,0:T(8,128)S(1)}, f32[96,512]{1,0:T(8,128)}, u32[]{:S(2)}, u32[]{:S(2)}) collective-permute-start(f32[96,512]{1,0:T(8,128)S(1)} %get-tuple-element.35), channel_id=1, source_target_pairs={{0,128},{32,160},{64,192},{96,224},{128,0},{160,32},{192,64},{224,... | collective-permute-start | bytes 589832 | tf_op jit(solution)/shard_map/ppermute | solution.py:52
  231.1 30.8 %all-to-all-start.1 = ((f32[32,1,8,8,131]{4,3,2,1,0:T(8,128)}), f32[32,1,8,8,131]{4,3,2,1,0:T(8,128)S(1)}, u32[]{:S(2)}, u32[]{:S(2)}) async-start(f32[32,1,8,8,131]{4,3,2,1,0:T(8,128)} %bitcast.59), calls=%async_computation.2 | async-start | bytes 4194304 | tf_op jit(solution)/shard_map/all_to_all | solution.py:40
  237.5 27.3 %collective-permute-start.12 = (f32[96,256]{1,0:T(8,128)}, f32[96,256]{1,0:T(8,128)}, u32[]{:S(2)}, u32[]{:S(2)}) collective-permute-start(f32[96,256]{1,0:T(8,128)} %get-tuple-element.27), channel_id=1, source_target_pairs={{0,16},{16,0},{1,17},{17,1},{2,18},{18,2},{3,19},{19,3},{4,20},{20... | collective-permute-start | bytes 294920 | tf_op jit(solution)/shard_map/ppermute | solution.py:77
  261.9 4.5 %copy-start.1 = (f32[24,1,8,64,3]{3,2,4,1,0:T(8,128)S(1)}, f32[24,1,8,64,3]{3,2,4,1,0:T(8,128)}, u32[]{:S(2)}) copy-start(f32[24,1,8,64,3]{3,2,4,1,0:T(8,128)} %param.11) | copy-start | bytes 442372
  262.1 2.7 copy-start.4
Sparse Core Ops, SparseCore 0:
  50.7 93.9 reduce-scatter.1
  147.1 52.7 all-gather.1
